TPU v7x, 32 devices: a whole 2x2x4 slice. The times are simulated.
32 devices in a mesh: fsdp: 8 (over y, x, core), dp: 4 (over z).
Axes of the slice: x: 2, y: 2, z: 4, core: 2. Of those that a mesh axis runs over, the one named last changes fastest.
Arguments:
- tokens: bfloat16 [2, 32, 128, 2560], P(None, ('fsdp', 'dp')), may hold values from -24 to 24
- lengths: int32 [2, 32], P(None, ('fsdp', 'dp')), may hold values from 64 to 128, as said below
- attn_gain: bfloat16 [2560], P(('fsdp', 'dp')), may hold values from 0.099609375 to 1.8984375
- query_down: bfloat16 [2560, 768], P(('fsdp', 'dp')), may hold values from -0.125 to 0.125
- query_gain: bfloat16 [768], P(('fsdp', 'dp')), may hold values from 0.099609375 to 1.8984375
- query_up: bfloat16 [768, 3840], P(('fsdp', 'dp')), may hold values from -0.21875 to 0.21875
- latent_down: bfloat16 [2560, 288], P(('fsdp', 'dp')), may hold values from -0.125 to 0.125
- latent_gain: bfloat16 [256], P(('fsdp', 'dp')), may hold values from 0.099609375 to 1.8984375
- latent_up: bfloat16 [256, 5120], P(('fsdp', 'dp')), may hold values from -0.375 to 0.375
- output_weight: bfloat16 [2560, 2560], P(('fsdp', 'dp')), may hold values from -2 to 2
- feed_gain: bfloat16 [2560], P(('fsdp', 'dp')), may hold values from 0.099609375 to 1.8984375
- gate_weight: bfloat16 [2560, 6400], P(('fsdp', 'dp')), may hold values from -0.125 to 0.125
- up_weight: bfloat16 [2560, 6400], P(('fsdp', 'dp')), may hold values from -0.125 to 0.125
- down_weight: bfloat16 [6400, 2560], P(('fsdp', 'dp')), may hold values from -0.75 to 0.75
- cotangent: bfloat16 [2, 32, 128, 2560], P(None, ('fsdp', 'dp')), may hold values from -6 to 6
Outputs:
- output: bfloat16 [2, 32, 128, 2560], P(None, ('fsdp', 'dp'))
- input_grad: float32 [2, 32, 128, 2560], P(None, ('fsdp', 'dp'))
- attn_gain_grad: float32 [2560], P(('fsdp', 'dp'))
- query_down_grad: float32 [2560, 768], P(('fsdp', 'dp'))
- query_gain_grad: float32 [768], P(('fsdp', 'dp'))
- query_up_grad: float32 [768, 3840], P(('fsdp', 'dp'))
- latent_down_grad: float32 [2560, 288], P(('fsdp', 'dp'))
- latent_gain_grad: float32 [256], P(('fsdp', 'dp'))
- latent_up_grad: float32 [256, 5120], P(('fsdp', 'dp'))
- output_weight_grad: float32 [2560, 2560], P(('fsdp', 'dp'))
- feed_gain_grad: float32 [2560], P(('fsdp', 'dp'))
- gate_weight_grad: float32 [2560, 6400], P(('fsdp', 'dp'))
- up_weight_grad: float32 [2560, 6400], P(('fsdp', 'dp'))
- down_weight_grad: float32 [6400, 2560], P(('fsdp', 'dp'))
Inputs may be any that keep to these rules, and one draw needn't show every extreme that they name: `lengths`: each sequence fills at least half of its slot of 128 token slots, and some sequence fills its whole slot.
All inputs are finite; a program needn't handle non-finite values.
Results may differ from a plain program's by a relative error of at most 0.018.
Values may be sent and summed in bfloat16 or wider, within the bound.
No kernel may reach another device: no remote copies, remote signals or barrier semaphores. Data moves between devices by JAX's collectives and lax.ppermute only.
A program may use at most 960 MiB of HBM per device.

v0:
```python
import math

import jax
import jax.numpy as jnp
from jax import lax
from jax.sharding import PartitionSpec as P

HEADS = 40
NOPE = 64
ROPE = 32
VDIM = 64
KVRANK = 256


epsilon = 1e-05
depth_scale = 1.4 / math.sqrt(62.0)
masked_score = -1e30


def matmul(left, right):
    return jnp.dot(left, right, preferred_element_type=jnp.float32)


def rows_product(left, right):
    return lax.dot_general(
        left, right, (((0,), (0,)), ((), ())), preferred_element_type=jnp.float32
    )


def back_product(left, right):
    return lax.dot_general(
        left, right, (((1,), (1,)), ((), ())), preferred_element_type=jnp.float32
    )


def normalize(values):
    inverse = lax.rsqrt(jnp.mean(values * values, axis=-1, keepdims=True) + epsilon)
    return (values * inverse, inverse)


def norm_back(grad, normed, inverse, gain):
    scaled = grad * gain.astype(jnp.float32)
    gain_grad = jnp.sum(grad * normed, axis=0)
    inner = jnp.mean(scaled * normed, axis=-1, keepdims=True)
    return (gain_grad, inverse * (scaled - normed * inner))


def rotate(values, cosines, sines):
    half = values.shape[-1] // 2
    first = values[..., :half]
    second = values[..., half:]
    return jnp.concatenate(
        [first * cosines - second * sines, second * cosines + first * sines], axis=-1
    )


def rotate_back(grad, cosines, sines):
    half = grad.shape[-1] // 2
    first = grad[..., :half]
    second = grad[..., half:]
    return jnp.concatenate(
        [first * cosines + second * sines, second * cosines - first * sines], axis=-1
    )


def packed_terms(terms, devices, count):
    pieces = []
    for left, right in terms:
        if right is None:
            share = left.shape[0] // devices
            pieces.append(left.reshape(count, share))
        else:
            share = left.shape[1] // devices
            product = rows_product(left, right)
            pieces.append(product.reshape(count, share * right.shape[1]))
    return jnp.concatenate(pieces, axis=1)


def unpack_row(packed, terms, devices):
    results = []
    offset = 0
    for left, right in terms:
        if right is None:
            share = left.shape[0] // devices
            results.append(packed[0, offset : offset + share])
            offset = offset + share
        else:
            share = left.shape[1] // devices
            width = share * right.shape[1]
            results.append(packed[0, offset : offset + width].reshape(share, right.shape[1]))
            offset = offset + width
    return results


def local(
    tokens,
    lengths,
    attn_gain,
    query_down,
    query_gain,
    query_up,
    latent_down,
    latent_gain,
    latent_up,
    output_weight,
    feed_gain,
    gate_weight,
    up_weight,
    down_weight,
    cotangent,
):
    micro, _, slot, width = tokens.shape
    rows = micro * slot
    devices = lax.axis_size(("fsdp", "dp"))
    attn_shards = (
        attn_gain,
        query_down,
        query_gain,
        query_up,
        latent_down,
        latent_gain,
        latent_up,
        output_weight,
    )
    feed_shards = (feed_gain, gate_weight, up_weight, down_weight)
    attn_full = (
        lax.all_gather(attn_shards[0], ("fsdp", "dp"), axis=0, tiled=True),
        lax.all_gather(attn_shards[1], ("fsdp", "dp"), axis=0, tiled=True),
        lax.all_gather(attn_shards[2], ("fsdp", "dp"), axis=0, tiled=True),
        lax.all_gather(attn_shards[3], ("fsdp", "dp"), axis=0, tiled=True),
        lax.all_gather(attn_shards[4], ("fsdp", "dp"), axis=0, tiled=True),
        lax.all_gather(attn_shards[5], ("fsdp", "dp"), axis=0, tiled=True),
        lax.all_gather(attn_shards[6], ("fsdp", "dp"), axis=0, tiled=True),
        lax.all_gather(attn_shards[7], ("fsdp", "dp"), axis=0, tiled=True),
    )
    feed_full = (
        lax.all_gather(feed_shards[0], ("fsdp", "dp"), axis=0, tiled=True),
        lax.all_gather(feed_shards[1], ("fsdp", "dp"), axis=0, tiled=True),
        lax.all_gather(feed_shards[2], ("fsdp", "dp"), axis=0, tiled=True),
        lax.all_gather(feed_shards[3], ("fsdp", "dp"), axis=0, tiled=True),
    )
    gain_one, down_query, gain_query, up_query, down_latent, gain_latent, up_latent, weight_out = (
        attn_full
    )
    gain_two, weight_gate, weight_up, weight_down = feed_full
    half = ROPE // 2
    freqs = 10000.0 ** (-(2.0 * jnp.arange(half, dtype=jnp.float32)) / ROPE)
    angles = jnp.arange(slot, dtype=jnp.float32)[:, None] * freqs[None, :]
    cosines = jnp.cos(angles)[:, None, :]
    sines = jnp.sin(angles)[:, None, :]
    positions = lax.broadcasted_iota(jnp.int32, (micro, slot), 1)
    valid_rows = (positions < lengths).astype(jnp.float32).reshape(rows, 1)
    query_pos = lax.broadcasted_iota(jnp.int32, (micro, 1, slot, slot), 2)
    key_pos = lax.broadcasted_iota(jnp.int32, (micro, 1, slot, slot), 3)
    allowed = (key_pos <= query_pos) & (key_pos < lengths[:, :, None, None])
    scale = 1.0 / math.sqrt(NOPE + ROPE)
    inputs = tokens.reshape(rows, width).astype(jnp.float32)
    normed_one, inverse_one = normalize(inputs)
    h_one = (normed_one * gain_one.astype(jnp.float32)).astype(jnp.bfloat16)
    latent_query = matmul(h_one, down_query)
    normed_query, inverse_query = normalize(latent_query)
    query_low = (normed_query * gain_query.astype(jnp.float32)).astype(jnp.bfloat16)
    query_raw = matmul(query_low, up_query).reshape(micro, slot, HEADS, NOPE + ROPE)
    queries = jnp.concatenate(
        [query_raw[..., :NOPE], rotate(query_raw[..., NOPE:], cosines, sines)], axis=-1
    ).astype(jnp.bfloat16)
    latent_all = matmul(h_one, down_latent)
    normed_latent, inverse_latent = normalize(latent_all[:, :KVRANK])
    latent_low = (normed_latent * gain_latent.astype(jnp.float32)).astype(jnp.bfloat16)
    kv_raw = matmul(latent_low, up_latent).reshape(micro, slot, HEADS, NOPE + VDIM)
    key_rope = rotate(latent_all[:, KVRANK:].reshape(micro, slot, 1, ROPE), cosines, sines)
    keys = jnp.concatenate(
        [kv_raw[..., :NOPE], jnp.broadcast_to(key_rope, (micro, slot, HEADS, ROPE))], axis=-1
    ).astype(jnp.bfloat16)
    values = kv_raw[..., NOPE:].astype(jnp.bfloat16)
    raw = jnp.einsum("mqhd,mkhd->mhqk", queries, keys, preferred_element_type=jnp.float32)
    scores = jnp.where(allowed, raw * scale, masked_score)
    top = jnp.max(scores, axis=-1, keepdims=True)
    expo = jnp.exp(scores - top)
    total = jnp.sum(expo, axis=-1, keepdims=True)
    probs = expo / total
    log_total = top + jnp.log(total)
    attended = jnp.einsum(
        "mhqk,mkhd->mqhd", probs.astype(jnp.bfloat16), values, preferred_element_type=jnp.float32
    )
    attended = attended.reshape(rows, HEADS * VDIM).astype(jnp.bfloat16)
    middle = inputs + depth_scale * matmul(attended, weight_out)
    normed_two, inverse_two = normalize(middle)
    h_two = (normed_two * gain_two.astype(jnp.float32)).astype(jnp.bfloat16)
    gate = matmul(h_two, weight_gate)
    upward = matmul(h_two, weight_up)
    sigma = jax.nn.sigmoid(gate)
    hidden = (gate * sigma * upward).astype(jnp.bfloat16)
    result = (middle + depth_scale * matmul(hidden, weight_down)) * valid_rows
    output = result.astype(jnp.bfloat16).reshape(tokens.shape)
    feed_back = (
        lax.all_gather(feed_shards[0], ("fsdp", "dp"), axis=0, tiled=True),
        lax.all_gather(feed_shards[1], ("fsdp", "dp"), axis=0, tiled=True),
        lax.all_gather(feed_shards[2], ("fsdp", "dp"), axis=0, tiled=True),
        lax.all_gather(feed_shards[3], ("fsdp", "dp"), axis=0, tiled=True),
    )
    attn_back = (
        lax.all_gather(attn_shards[0], ("fsdp", "dp"), axis=0, tiled=True),
        lax.all_gather(attn_shards[1], ("fsdp", "dp"), axis=0, tiled=True),
        lax.all_gather(attn_shards[2], ("fsdp", "dp"), axis=0, tiled=True),
        lax.all_gather(attn_shards[3], ("fsdp", "dp"), axis=0, tiled=True),
        lax.all_gather(attn_shards[4], ("fsdp", "dp"), axis=0, tiled=True),
        lax.all_gather(attn_shards[5], ("fsdp", "dp"), axis=0, tiled=True),
        lax.all_gather(attn_shards[6], ("fsdp", "dp"), axis=0, tiled=True),
        lax.all_gather(attn_shards[7], ("fsdp", "dp"), axis=0, tiled=True),
    )
    grad_out = cotangent.reshape(rows, width).astype(jnp.float32) * valid_rows
    grad_feed = (depth_scale * grad_out).astype(jnp.bfloat16)
    grad_hidden = back_product(grad_feed, feed_back[3])
    grad_gate = (grad_hidden * upward * sigma * (1.0 + gate * (1.0 - sigma))).astype(jnp.bfloat16)
    grad_up = (grad_hidden * gate * sigma).astype(jnp.bfloat16)
    grad_h_two = back_product(grad_gate, feed_back[1]) + back_product(grad_up, feed_back[2])
    gain_two_term, grad_middle_norm = norm_back(grad_h_two, normed_two, inverse_two, feed_back[0])
    feed_terms = [(gain_two_term, None), (h_two, grad_gate), (h_two, grad_up), (hidden, grad_feed)]
    feed_packed = lax.psum_scatter(
        packed_terms(feed_terms, devices, lax.axis_size(("fsdp", "dp")) * 1),
        ("fsdp", "dp"),
        scatter_dimension=0,
        tiled=True,
    )
    feed_sums = unpack_row(feed_packed, feed_terms, devices)
    grad_middle = grad_out + grad_middle_norm
    grad_attn = (depth_scale * grad_middle).astype(jnp.bfloat16)
    grad_heads = (
        back_product(grad_attn, attn_back[7]).astype(jnp.bfloat16).reshape(micro, slot, HEADS, VDIM)
    )
    probs_again = jnp.exp(scores - log_total)
    grad_values = jnp.einsum(
        "mhqk,mqhd->mkhd",
        probs_again.astype(jnp.bfloat16),
        grad_heads,
        preferred_element_type=jnp.float32,
    )
    grad_probs = jnp.einsum(
        "mqhd,mkhd->mhqk", grad_heads, values, preferred_element_type=jnp.float32
    )
    inner = jnp.sum(probs_again * grad_probs, axis=-1, keepdims=True)
    grad_scores = (probs_again * (grad_probs - inner)).astype(jnp.bfloat16)
    grad_queries = scale * jnp.einsum(
        "mhqk,mkhd->mqhd", grad_scores, keys, preferred_element_type=jnp.float32
    )
    grad_keys = scale * jnp.einsum(
        "mhqk,mqhd->mkhd", grad_scores, queries, preferred_element_type=jnp.float32
    )
    grad_query_raw = jnp.concatenate(
        [grad_queries[..., :NOPE], rotate_back(grad_queries[..., NOPE:], cosines, sines)], axis=-1
    )
    grad_query_raw = grad_query_raw.reshape(rows, HEADS * (NOPE + ROPE)).astype(jnp.bfloat16)
    grad_query_low = back_product(grad_query_raw, attn_back[3])
    grad_kv = (
        jnp.concatenate([grad_keys[..., :NOPE], grad_values], axis=-1)
        .reshape(rows, HEADS * (NOPE + VDIM))
        .astype(jnp.bfloat16)
    )
    grad_latent_low = back_product(grad_kv, attn_back[6])
    latent_gain_term, grad_latent = norm_back(
        grad_latent_low, normed_latent, inverse_latent, attn_back[5]
    )
    grad_key_rope = rotate_back(
        jnp.sum(grad_keys[..., NOPE:], axis=2, keepdims=True), cosines, sines
    ).reshape(rows, ROPE)
    grad_latent_all = jnp.concatenate([grad_latent, grad_key_rope], axis=-1).astype(jnp.bfloat16)
    query_gain_term, grad_latent_query = norm_back(
        grad_query_low, normed_query, inverse_query, attn_back[2]
    )
    grad_latent_query = grad_latent_query.astype(jnp.bfloat16)
    grad_h_one = back_product(grad_latent_all, attn_back[4]) + back_product(
        grad_latent_query, attn_back[1]
    )
    gain_one_term, grad_input_norm = norm_back(grad_h_one, normed_one, inverse_one, attn_back[0])
    input_grad = (grad_middle + grad_input_norm).reshape(tokens.shape)
    attn_terms = [
        (gain_one_term, None),
        (h_one, grad_latent_query),
        (query_gain_term, None),
        (query_low, grad_query_raw),
        (h_one, grad_latent_all),
        (latent_gain_term, None),
        (latent_low, grad_kv),
        (attended, grad_attn),
    ]
    attn_packed = lax.psum_scatter(
        packed_terms(attn_terms, devices, lax.axis_size(("fsdp", "dp")) * 1),
        ("fsdp", "dp"),
        scatter_dimension=0,
        tiled=True,
    )
    attn_sums = unpack_row(attn_packed, attn_terms, devices)
    return (
        output,
        input_grad,
        attn_sums[0],
        attn_sums[1],
        attn_sums[2],
        attn_sums[3],
        attn_sums[4],
        attn_sums[5],
        attn_sums[6],
        attn_sums[7],
        feed_sums[0],
        feed_sums[1],
        feed_sums[2],
        feed_sums[3],
    )


def solution(mesh):
    placed = (
        P(None, ("fsdp", "dp"), None, None),
        P(None, ("fsdp", "dp")),
        P(("fsdp", "dp")),
        P(("fsdp", "dp"), None),
        P(("fsdp", "dp")),
        P(("fsdp", "dp"), None),
        P(("fsdp", "dp"), None),
        P(("fsdp", "dp")),
        P(("fsdp", "dp"), None),
        P(("fsdp", "dp"), None),
        P(("fsdp", "dp")),
        P(("fsdp", "dp"), None),
        P(("fsdp", "dp"), None),
        P(("fsdp", "dp"), None),
        P(None, ("fsdp", "dp"), None, None),
    )
    return jax.shard_map(
        local,
        mesh=mesh,
        in_specs=placed,
        out_specs=(
            P(None, ("fsdp", "dp"), None, None),
            P(None, ("fsdp", "dp"), None, None),
            P(("fsdp", "dp")),
            P(("fsdp", "dp"), None),
            P(("fsdp", "dp")),
            P(("fsdp", "dp"), None),
            P(("fsdp", "dp"), None),
            P(("fsdp", "dp")),
            P(("fsdp", "dp"), None),
            P(("fsdp", "dp"), None),
            P(("fsdp", "dp")),
            P(("fsdp", "dp"), None),
            P(("fsdp", "dp"), None),
            P(("fsdp", "dp"), None),
        ),
        check_vma=False,
    )
```

profile of v0, /device:TPU:0, one launch (start us, length us, event | category | flops | bytes accessed | tf_op | source)
XLA Modules:
  0.0 4849.1 jit_solution(3591033641761901371)
XLA Ops:
  13.8 42.3 all-reduce.6
  58.6 11.0 all-gather.9.cloned.1.call-done
  72.2 56.9 %all-gather.11.cloned.1.call-done = bf16[256,5120]{1,0:T(8,128)(2,1)} async-done(((bf16[8,5120]{1,0:T(8,128)(2,1)}), bf16[256,5120]{1,0:T(8,128)(2,1)}) %all-gather.11.cloned.1.call-update) | async-done | bytes 2621456 | tf_op jit(solution)/shard_map/all_gather | solution.py:133
  145.4 46.3 all-gather.13.cloned.1.call-done
  195.1 65.8 %all-gather.15.cloned.1.call-done = bf16[768,3840]{1,0:T(8,128)(2,1)} async-done(((bf16[24,3840]{1,0:T(8,128)(2,1)}), bf16[768,3840]{1,0:T(8,128)(2,1)}) %all-gather.15.cloned.1.call-update) | async-done | bytes 5898256 | tf_op jit(solution)/shard_map/all_gather | solution.py:130
  285.5 74.4 %all-gather.17.cloned.1.call-done = bf16[2560,2560]{1,0:T(8,128)(2,1)} async-done(((bf16[80,2560]{1,0:T(8,128)(2,1)}), bf16[2560,2560]{1,0:T(8,128)(2,1)}) %all-gather.17.cloned.1.call-update) | async-done | bytes 13107216 | tf_op jit(solution)/shard_map/all_gather | solution.py:134
  368.7 182.9 %all-gather.19.cloned.1.call-done = bf16[2560,6400]{1,0:T(8,128)(2,1)} async-done(((bf16[80,6400]{1,0:T(8,128)(2,1)}), bf16[2560,6400]{1,0:T(8,128)(2,1)}) %all-gather.19.cloned.1.call-update) | async-done | bytes 32768016 | tf_op jit(solution)/shard_map/all_gather | solution.py:138
  551.6 18.2 fusion.58
  569.8 173.2 %all-gather.21.cloned.1.call-done = bf16[2560,6400]{1,0:T(8,128)(2,1)} async-done(((bf16[80,6400]{1,0:T(8,128)(2,1)}), bf16[2560,6400]{1,0:T(8,128)(2,1)}) %all-gather.21.cloned.1.call-update) | async-done | bytes 32768016 | tf_op jit(solution)/shard_map/all_gather | solution.py:139
  743.0 18.3 fusion.59
  761.4 173.1 %all-gather.23.cloned.1.call-done = bf16[6400,2560]{1,0:T(8,128)(2,1)} async-done(((bf16[200,2560]{1,0:T(8,128)(2,1)}), bf16[6400,2560]{1,0:T(8,128)(2,1)}) %all-gather.23.cloned.1.call-update) | async-done | bytes 32768016 | tf_op jit(solution)/shard_map/all_gather | solution.py:140
  934.5 21.0 multiply_convert_fusion
  955.5 17.0 fusion.60
  972.5 18.4 multiply_reduce_fusion.1
  1025.0 11.0 fusion.34
  1098.0 27.1 reshape.254
  1126.5 23.3 dynamic-update-slice.9
  1151.3 34.3 dynamic-update-slice.11
  1196.0 17.6 dynamic-update-slice.14
  1213.6 72.7 %dynamic-update-slice.15 = f32[32,422512]{1,0:T(8,128)} dynamic-update-slice(f32[32,422512]{1,0:T(8,128)} %dynamic-update-slice.14, f32[32,204800]{1,0:T(8,128)} %reshape.254, s32[]{} %constant.88, s32[]{} %constant.97) | dynamic-update-slice | bytes 52428804 | tf_op jit(solution)/shard_map/concatenate | solution.py:76
  1287.7 26.1 fusion.63
  1313.8 59.1 %reshape.256 = f32[32,512000]{1,0:T(8,128)} reshape(f32[2560,6400]{1,0:T(8,128)} %fusion.63) | data formatting | bytes 131072000 | tf_op jit(solution)/shard_map/reshape | solution.py:75
  1372.9 26.7 fusion.64
  1399.5 59.2 %reshape.257 = f32[32,512000]{1,0:T(8,128)} reshape(f32[2560,6400]{1,0:T(8,128)} %fusion.64) | data formatting | bytes 131072000 | tf_op jit(solution)/shard_map/reshape | solution.py:75
  1458.8 27.2 fusion.65
  1486.0 59.4 %reshape.258 = f32[32,512000]{1,0:T(8,128)} reshape(f32[6400,2560]{1,0:T(8,128)} %fusion.65) | data formatting | bytes 131072000 | tf_op jit(solution)/shard_map/reshape | solution.py:75
  1546.8 177.6 %dynamic-update-slice.5 = f32[32,1536080]{1,0:T(8,128)} dynamic-update-slice(f32[32,1536080]{1,0:T(8,128)} %dynamic-update-slice.4, f32[32,512000]{1,0:T(8,128)} %reshape.256, s32[]{} %constant.88, s32[]{} %constant.89) | dynamic-update-slice | bytes 131072000
  1724.4 178.1 %dynamic-update-slice.6 = f32[32,1536080]{1,0:T(8,128)} dynamic-update-slice(f32[32,1536080]{1,0:T(8,128)} %dynamic-update-slice.5, f32[32,512000]{1,0:T(8,128)} %reshape.257, s32[]{} %constant.88, s32[]{} %constant.90) | dynamic-update-slice | bytes 131072000
  1902.5 177.8 %dynamic-update-slice.7 = f32[32,1536080]{1,0:T(8,128)} dynamic-update-slice(f32[32,1536080]{1,0:T(8,128)} %dynamic-update-slice.6, f32[32,512000]{1,0:T(8,128)} %reshape.258, s32[]{} %constant.88, s32[]{} %constant.91) | dynamic-update-slice | bytes 131072000 | tf_op jit(solution)/shard_map/concatenate | solution.py:76
  2086.7 17.6 fusion.5
  2131.2 2673.4 %all-reduce.12.cloned.1.call-done = f32[32,1536080]{1,0:T(8,128)} async-done(((f32[32,1536080]{1,0:T(8,128)}), f32[32,1536080]{1,0:T(8,128)}) %all-reduce.12.cloned.1.call-update) | async-done | bytes 196618256
  4804.6 28.9 dynamic-slice_reduce_fusion
  (267 shorter events, 217.5 us)
Async XLA Ops:
  7.2 6.1 copy-start.57
  7.2 6.4 copy-start.58
  7.2 48.9 %copy-start.3 = (bf16[2,1,128,2560]{3,2,1,0:T(8,128)(2,1)S(1)}, bf16[2,1,128,2560]{3,2,1,0:T(8,128)(2,1)}, u32[]{:S(2)}) copy-start(bf16[2,1,128,2560]{3,2,1,0:T(8,128)(2,1)} %param.15) | copy-start | bytes 3932164
  7.2 62.4 %all-gather.9.cloned.1.call-start = ((), (), s32[]{:S(2)}) async-start(), calls=%async_computation | async-start | bytes 2027520 | tf_op jit(solution)/shard_map/all_gather | solution.py:131
  8.0 121.1 %all-gather.11.cloned.1.call-start = ((), (), s32[]{:S(2)}) async-start(), calls=%async_computation.1 | async-start | bytes 2703360 | tf_op jit(solution)/shard_map/all_gather | solution.py:133
  8.7 47.8 copy-start.54
  8.7 48.1 copy-start.21
  8.7 183.0 %all-gather.13.cloned.1.call-start = ((), (), s32[]{:S(2)}) async-start(), calls=%async_computation.2 | async-start | bytes 4055040 | tf_op jit(solution)/shard_map/all_gather | solution.py:128
  9.5 251.4 %all-gather.15.cloned.1.call-start = ((), (), s32[]{:S(2)}) async-start(), calls=%async_computation.3 | async-start | bytes 6082560 | tf_op jit(solution)/shard_map/all_gather | solution.py:130
  10.0 349.9 %all-gather.17.cloned.1.call-start = ((), (), s32[]{:S(2)}) async-start(), calls=%async_computation.4 | async-start | bytes 13516800 | tf_op jit(solution)/shard_map/all_gather | solution.py:134
  10.6 541.0 %all-gather.19.cloned.1.call-start = ((), (), s32[]{:S(2)}) async-start(), calls=%async_computation.5 | async-start | bytes 33792000 | tf_op jit(solution)/shard_map/all_gather | solution.py:138
  11.2 731.8 %all-gather.21.cloned.1.call-start = ((), (), s32[]{:S(2)}) async-start(), calls=%async_computation.6 | async-start | bytes 33792000 | tf_op jit(solution)/shard_map/all_gather | solution.py:139
  12.0 922.5 %all-gather.23.cloned.1.call-start = ((), (), s32[]{:S(2)}) async-start(), calls=%async_computation.7 | async-start | bytes 33792000 | tf_op jit(solution)/shard_map/all_gather | solution.py:140
  12.7 2091.6 %all-reduce.10.cloned.1.call-start = ((), (), s32[]{:S(2)}) async-start(), calls=%async_computation.8 | async-start | bytes 108167168
  56.1 73.0 %copy-start.42 = (f32[256]{0:T(256)}, f32[256]{0:T(256)S(1)}, u32[]{:S(2)}) copy-start(f32[256]{0:T(256)S(1)} %convert_element_type.112) | copy-start | bytes 3076
  56.1 204.8 %copy-start.36 = (f32[768]{0:T(1024)}, f32[768]{0:T(1024)S(1)}, u32[]{:S(2)}) copy-start(f32[768]{0:T(1024)S(1)} %convert_element_type.114) | copy-start | bytes 9220
  56.6 934.3 %copy-start.51 = (f32[256]{0:T(256)}, f32[256]{0:T(256)S(1)}, u32[]{:S(2)}) copy-start(f32[256]{0:T(256)S(1)} %fusion.44) | copy-start | bytes 3076
  58.6 133.1 %copy-start.1 = (bf16[256,2560]{1,0:T(8,128)(2,1)}, bf16[256,2560]{1,0:T(8,128)(2,1)S(1)}, u32[]{:S(2)}) copy-start(bf16[256,2560]{1,0:T(8,128)(2,1)S(1)} %multiply_convert_fusion.6) | copy-start | bytes 3932164
  72.0 59.8 %copy-start.18 = (f32[256,288]{0,1:T(8,128)}, f32[256,288]{0,1:T(8,128)S(1)}, u32[]{:S(2)}) copy-start(f32[256,288]{0,1:T(8,128)S(1)} %fusion.57) | copy-start | bytes 884740
  72.2 59.7 %copy-start.44 = (f32[256]{0:T(256)}, f32[256]{0:T(256)S(1)}, u32[]{:S(2)}) copy-start(f32[256]{0:T(256)S(1)} %add_rsqrt_fusion.2) | copy-start | bytes 3076
  195.1 72.8 %copy-start.16 = (f32[256,768]{1,0:T(8,128)}, f32[256,768]{1,0:T(8,128)S(1)}, u32[]{:S(2)}) copy-start(f32[256,768]{1,0:T(8,128)S(1)} %get-tuple-element.91) | copy-start | bytes 2359300
  195.1 72.8 %copy-start.46 = (f32[256]{0:T(256)}, f32[256]{0:T(256)S(1)}, u32[]{:S(2)}) copy-start(f32[256]{0:T(256)S(1)} %add_rsqrt_fusion.1) | copy-start | bytes 3076
  285.5 81.5 %copy-start.11 = (bf16[2,128,40,64]{1,0,3,2:T(2,128)(2,1)}, bf16[2,128,40,64]{1,0,3,2:T(2,128)(2,1)S(1)}, u32[]{:S(2)}) copy-start(bf16[2,128,40,64]{1,0,3,2:T(2,128)(2,1)S(1)} %copy.72) | copy-start | bytes 3932164
  368.7 374.3 %copy-start.13 = (bf16[256,2560]{1,0:T(8,128)(2,1)}, bf16[256,2560]{1,0:T(8,128)(2,1)S(1)}, u32[]{:S(2)}) copy-start(bf16[256,2560]{1,0:T(8,128)(2,1)S(1)} %multiply_convert_fusion.5) | copy-start | bytes 3932164
  569.8 364.7 %copy-start.26 = (bf16[256,2560]{1,0:T(8,128)(2,1)S(1)}, bf16[256,2560]{1,0:T(8,128)(2,1)}, u32[]{:S(2)}) copy-start(bf16[256,2560]{1,0:T(8,128)(2,1)} %fusion.14) | copy-start | bytes 3932164
  955.5 17.0 copy-start.9
  1006.3 8.7 slice-start
  1036.1 8.5 slice-start.2
  1038.3 6.2 slice-start.3
  1286.4 3518.2 %all-reduce.12.cloned.1.call-start = ((), (), s32[]{:S(2)}) async-start(), calls=%async_computation.9 | async-start | bytes 393248768
  1399.5 59.2 %copy-start.27 = (bf16[256,2560]{1,0:T(8,128)(2,1)S(1)}, bf16[256,2560]{1,0:T(8,128)(2,1)}, u32[]{:S(2)}) copy-start(bf16[256,2560]{1,0:T(8,128)(2,1)} %fusion.14) | copy-start | bytes 3932164
  1486.0 59.4 %copy-start.41 = (f32[32,80]{1,0:T(8,128)S(1)}, f32[32,80]{1,0:T(8,128)}, u32[]{:S(2)}) copy-start(f32[32,80]{1,0:T(8,128)} %reshape.255) | copy-start | bytes 30724
  (41 other events, 101.9 us)
Sparse Core Ops, SparseCore 0:
  10.8 58.7 all-gather.8
  72.5 56.5 all-gather.10
  131.9 59.7 all-gather.12
  194.4 66.5 all-gather.14
  263.6 96.3 all-gather.16
  362.6 188.9 all-gather.18
  554.4 188.5 all-gather.20
  745.9 188.5 all-gather.22
  1286.5 766.2 all-reduce.9
  2080.5 2724.0 all-reduce.11
where the time goes:
time: 4880 us; the launch traced here: 4850 us
  waiting for transfers between devices  3460 us (71%)
  local copies, waits for them, and re-layouts  1040 us (21%)
  matrix products  270 us (6%)
    unnamed x12, waiting for transfers between devices  2680 us
    unnamed x149, local copies, waits for them, and re-layouts  468 us
    concatenate x2, local copies, waits for them, and re-layouts, packed_terms(): return jnp.concatenate(pieces, axis=1)  250 us
    reshape x8, local copies, waits for them, and re-layouts, packed_terms(): pieces.append(product.reshape(count, share * right.shape[1]))  230 us
    all_gather x1, waiting for transfers between devices, local(): lax.all_gather(feed_shards[1], ('fsdp', 'dp'), axis=0, tiled=True)  183 us
    all_gather x1, waiting for transfers between devices, local(): lax.all_gather(feed_shards[2], ('fsdp', 'dp'), axis=0, tiled=True)  173 us
    all_gather x1, waiting for transfers between devices, local(): lax.all_gather(feed_shards[3], ('fsdp', 'dp'), axis=0, tiled=True)  173 us
    dot_general x8, matrix products, rows_product(): lax.dot_general(left, right, (((0,), (0,)), ((), ())), preferred_element_...  109 us
  transfers between devices with their start and end apart: 10, of which 9 were waited for; matrix products, arithmetic and copies ran while one was open for 19% of the time, Pallas kernels for 0%

commit v1 on v0

--- a/solution.py
+++ b/solution.py
@@ -63,33 +63,8 @@
     )
 
 
-def packed_terms(terms, devices, count):
-    pieces = []
-    for left, right in terms:
-        if right is None:
-            share = left.shape[0] // devices
-            pieces.append(left.reshape(count, share))
-        else:
-            share = left.shape[1] // devices
-            product = rows_product(left, right)
-            pieces.append(product.reshape(count, share * right.shape[1]))
-    return jnp.concatenate(pieces, axis=1)
-
-
-def unpack_row(packed, terms, devices):
-    results = []
-    offset = 0
-    for left, right in terms:
-        if right is None:
-            share = left.shape[0] // devices
-            results.append(packed[0, offset : offset + share])
-            offset = offset + share
-        else:
-            share = left.shape[1] // devices
-            width = share * right.shape[1]
-            results.append(packed[0, offset : offset + width].reshape(share, right.shape[1]))
-            offset = offset + width
-    return results
+def scatter_rows(term):
+    return lax.psum_scatter(term, ("fsdp", "dp"), scatter_dimension=0, tiled=True)
 
 
 def local(
@@ -216,14 +191,12 @@
     grad_up = (grad_hidden * gate * sigma).astype(jnp.bfloat16)
     grad_h_two = back_product(grad_gate, feed_back[1]) + back_product(grad_up, feed_back[2])
     gain_two_term, grad_middle_norm = norm_back(grad_h_two, normed_two, inverse_two, feed_back[0])
-    feed_terms = [(gain_two_term, None), (h_two, grad_gate), (h_two, grad_up), (hidden, grad_feed)]
-    feed_packed = lax.psum_scatter(
-        packed_terms(feed_terms, devices, lax.axis_size(("fsdp", "dp")) * 1),
-        ("fsdp", "dp"),
-        scatter_dimension=0,
-        tiled=True,
-    )
-    feed_sums = unpack_row(feed_packed, feed_terms, devices)
+    feed_sums = [
+        scatter_rows(gain_two_term),
+        scatter_rows(rows_product(h_two, grad_gate)),
+        scatter_rows(rows_product(h_two, grad_up)),
+        scatter_rows(rows_product(hidden, grad_feed)),
+    ]
     grad_middle = grad_out + grad_middle_norm
     grad_attn = (depth_scale * grad_middle).astype(jnp.bfloat16)
     grad_heads = (
@@ -274,23 +247,16 @@
     )
     gain_one_term, grad_input_norm = norm_back(grad_h_one, normed_one, inverse_one, attn_back[0])
     input_grad = (grad_middle + grad_input_norm).reshape(tokens.shape)
-    attn_terms = [
-        (gain_one_term, None),
-        (h_one, grad_latent_query),
-        (query_gain_term, None),
-        (query_low, grad_query_raw),
-        (h_one, grad_latent_all),
-        (latent_gain_term, None),
-        (latent_low, grad_kv),
-        (attended, grad_attn),
+    attn_sums = [
+        scatter_rows(gain_one_term),
+        scatter_rows(rows_product(h_one, grad_latent_query)),
+        scatter_rows(query_gain_term),
+        scatter_rows(rows_product(query_low, grad_query_raw)),
+        scatter_rows(rows_product(h_one, grad_latent_all)),
+        scatter_rows(latent_gain_term),
+        scatter_rows(rows_product(latent_low, grad_kv)),
+        scatter_rows(rows_product(attended, grad_attn)),
     ]
-    attn_packed = lax.psum_scatter(
-        packed_terms(attn_terms, devices, lax.axis_size(("fsdp", "dp")) * 1),
-        ("fsdp", "dp"),
-        scatter_dimension=0,
-        tiled=True,
-    )
-    attn_sums = unpack_row(attn_packed, attn_terms, devices)
     return (
         output,
         input_grad,

time: 4880 us -> 6290 us (1.29)
  waiting for transfers between devices: 3460 us -> 5840 us
  local copies, waits for them, and re-layouts: 1040 us -> 54.9 us
    reduce_scatter x0 -> x7, waiting for transfers between devices: none -> 3670 us  [scatter_rows(): lax.psum_scatter(term, ('fsdp', 'dp'), scatter_dimension=0, tiled=True)]
    unnamed x12 -> x17, waiting for transfers between devices: 2680 us -> 1390 us
    unnamed x149 -> x153, local copies, waits for them, and re-layouts: 468 us -> 26.4 us
    concatenate x2 -> x0, local copies, waits for them, and re-layouts: 250 us -> none  [packed_terms(): return jnp.concatenate(pieces, axis=1)]
    reshape x12 -> x0, local copies, waits for them, and re-layouts: 231 us -> none  [the longest x8 230 us: packed_terms(): pieces.append(product.reshape(count, share * right.shape[1]))]
  transfers between devices with their start and end apart: 10 -> 16, of which waited for: 9 -> 15; matrix products, arithmetic and copies ran while one was open for 19% -> 4% of each run, Pallas kernels for 0% -> 0%
where the time goes in v1:
time: 6290 us; the launch traced here: 6280 us
  waiting for transfers between devices  5840 us (93%)
  matrix products  273 us (4%)
  blocking collectives  83.3 us (1%)
    reduce_scatter x7, waiting for transfers between devices, scatter_rows(): lax.psum_scatter(term, ('fsdp', 'dp'), scatter_dimension=0, tiled=True)  3670 us
    unnamed x17, waiting for transfers between devices  1390 us
    all_gather x1, waiting for transfers between devices, local(): lax.all_gather(feed_shards[2], ('fsdp', 'dp'), axis=0, tiled=True)  183 us
    all_gather x1, waiting for transfers between devices, local(): lax.all_gather(feed_shards[1], ('fsdp', 'dp'), axis=0, tiled=True)  173 us
    all_gather x1, waiting for transfers between devices, local(): lax.all_gather(feed_shards[3], ('fsdp', 'dp'), axis=0, tiled=True)  173 us
  transfers between devices with their start and end apart: 16, of which 15 were waited for; matrix products, arithmetic and copies ran while one was open for 4% of the time, Pallas kernels for 0%

profile of v1, /device:TPU:0, one launch (start us, length us, event | category | flops | bytes accessed | tf_op | source)
XLA Modules:
  0.0 6283.9 jit_solution(18246836513395783366)
XLA Ops:
  13.8 42.3 all-reduce.10
  58.6 11.0 all-gather.9.cloned.1.call-done
  72.2 57.0 all-gather.11.cloned.1.call-done
  145.5 46.3 all-gather.13.cloned.1.call-done
  195.2 65.8 %all-gather.15.cloned.1.call-done = bf16[768,3840]{1,0:T(8,128)(2,1)} async-done(((bf16[24,3840]{1,0:T(8,128)(2,1)}), bf16[768,3840]{1,0:T(8,128)(2,1)}) %all-gather.15.cloned.1.call-update) | async-done | bytes 5898256 | tf_op jit(solution)/shard_map/all_gather | solution.py:105
  261.0 7.0 fusion.52
  268.0 5.9 reshape.205
  285.5 74.5 %all-gather.17.cloned.1.call-done = bf16[2560,2560]{1,0:T(8,128)(2,1)} async-done(((bf16[80,2560]{1,0:T(8,128)(2,1)}), bf16[2560,2560]{1,0:T(8,128)(2,1)}) %all-gather.17.cloned.1.call-update) | async-done | bytes 13107216 | tf_op jit(solution)/shard_map/all_gather | solution.py:109
  360.0 7.0 multiply_reduce_fusion.5
  368.9 182.8 %all-gather.21.cloned.1.call-done = bf16[2560,6400]{1,0:T(8,128)(2,1)} async-done(((bf16[80,6400]{1,0:T(8,128)(2,1)}), bf16[2560,6400]{1,0:T(8,128)(2,1)}) %all-gather.21.cloned.1.call-update) | async-done | bytes 32768016 | tf_op jit(solution)/shard_map/all_gather | solution.py:114
  551.7 18.2 fusion.59
  569.8 173.3 %all-gather.19.cloned.1.call-done = bf16[2560,6400]{1,0:T(8,128)(2,1)} async-done(((bf16[80,6400]{1,0:T(8,128)(2,1)}), bf16[2560,6400]{1,0:T(8,128)(2,1)}) %all-gather.19.cloned.1.call-update) | async-done | bytes 32768016 | tf_op jit(solution)/shard_map/all_gather | solution.py:113
  743.1 18.5 fusion.58
  761.6 173.0 %all-gather.23.cloned.1.call-done = bf16[6400,2560]{1,0:T(8,128)(2,1)} async-done(((bf16[200,2560]{1,0:T(8,128)(2,1)}), bf16[6400,2560]{1,0:T(8,128)(2,1)}) %all-gather.23.cloned.1.call-update) | async-done | bytes 32768016 | tf_op jit(solution)/shard_map/all_gather | solution.py:115
  934.5 21.0 multiply_convert_fusion
  955.5 17.0 fusion.60
  972.5 18.9 multiply_reduce_fusion.1
  995.9 8.3 convolution_convert_fusion.1
  1053.2 6.1 fusion.19
  1061.0 12.2 fusion.34
  1074.6 25.0 fusion.64
  1099.7 24.8 fusion.63
  1125.9 25.4 fusion.65
  1158.8 41.0 all-reduce.9
  1207.1 16.6 fusion.5
  1223.7 68.6 %reduce-scatter.18.cloned.1.call-done = f32[8,5120]{1,0:T(8,128)} async-done(((f32[256,5120]{1,0:T(8,128)}), f32[8,5120]{1,0:T(8,128)}) %reduce-scatter.18.cloned.1.call-update) | async-done | bytes 163856 | tf_op jit(solution)/shard_map/reduce_scatter | solution.py:67
  1292.3 128.5 %reduce-scatter.12.cloned.1.call-done = f32[80,768]{1,0:T(8,128)} async-done(((f32[2560,768]{1,0:T(8,128)}), f32[80,768]{1,0:T(8,128)}) %reduce-scatter.12.cloned.1.call-update) | async-done | bytes 245776 | tf_op jit(solution)/shard_map/reduce_scatter | solution.py:67
  1420.9 154.0 %reduce-scatter.14.cloned.1.call-done = f32[24,3840]{1,0:T(8,128)} async-done(((f32[768,3840]{1,0:T(8,128)}), f32[24,3840]{1,0:T(8,128)}) %reduce-scatter.14.cloned.1.call-update) | async-done | bytes 368656 | tf_op jit(solution)/shard_map/reduce_scatter | solution.py:67
  1574.9 561.8 %reduce-scatter.20.cloned.1.call-done = f32[80,2560]{1,0:T(8,128)} async-done(((f32[2560,2560]{1,0:T(8,128)}), f32[80,2560]{1,0:T(8,128)}) %reduce-scatter.20.cloned.1.call-update) | async-done | bytes 819216 | tf_op jit(solution)/shard_map/reduce_scatter | solution.py:67
  2136.7 1379.4 %reduce-scatter.24.cloned.1.call-done = f32[80,6400]{1,0:T(8,128)} async-done(((f32[2560,6400]{1,0:T(8,128)}), f32[80,6400]{1,0:T(8,128)}) %reduce-scatter.24.cloned.1.call-update) | async-done | bytes 2048016 | tf_op jit(solution)/shard_map/reduce_scatter | solution.py:67
  3516.1 1380.5 %reduce-scatter.22.cloned.1.call-done = f32[80,6400]{1,0:T(8,128)} async-done(((f32[2560,6400]{1,0:T(8,128)}), f32[80,6400]{1,0:T(8,128)}) %reduce-scatter.22.cloned.1.call-update) | async-done | bytes 2048016 | tf_op jit(solution)/shard_map/reduce_scatter | solution.py:67
  4896.6 1380.5 %reduce-scatter.26.cloned.1.call-done = f32[200,2560]{1,0:T(8,128)} async-done(((f32[6400,2560]{1,0:T(8,128)}), f32[200,2560]{1,0:T(8,128)}) %reduce-scatter.26.cloned.1.call-update) | async-done | bytes 2048016
  (256 shorter events, 116.2 us)
Async XLA Ops:
  7.2 48.9 copy-start.3
  7.2 62.4 all-gather.9.cloned.1.call-start
  8.0 121.2 %all-gather.11.cloned.1.call-start = ((), (), s32[]{:S(2)}) async-start(), calls=%async_computation.9 | async-start | bytes 2703360 | tf_op jit(solution)/shard_map/all_gather | solution.py:108
  8.7 47.7 copy-start.59
  8.7 48.1 copy-start.22
  8.7 183.0 %all-gather.13.cloned.1.call-start = ((), (), s32[]{:S(2)}) async-start(), calls=%async_computation.10 | async-start | bytes 4055040 | tf_op jit(solution)/shard_map/all_gather | solution.py:103
  9.5 251.5 %all-gather.15.cloned.1.call-start = ((), (), s32[]{:S(2)}) async-start(), calls=%async_computation.11 | async-start | bytes 6082560 | tf_op jit(solution)/shard_map/all_gather | solution.py:105
  10.0 350.0 %all-gather.17.cloned.1.call-start = ((), (), s32[]{:S(2)}) async-start(), calls=%async_computation.12 | async-start | bytes 13516800 | tf_op jit(solution)/shard_map/all_gather | solution.py:109
  10.6 541.0 %all-gather.21.cloned.1.call-start = ((), (), s32[]{:S(2)}) async-start(), calls=%async_computation.14 | async-start | bytes 33792000 | tf_op jit(solution)/shard_map/all_gather | solution.py:114
  11.2 731.9 %all-gather.19.cloned.1.call-start = ((), (), s32[]{:S(2)}) async-start(), calls=%async_computation.13 | async-start | bytes 33792000 | tf_op jit(solution)/shard_map/all_gather | solution.py:113
  12.0 922.6 %all-gather.23.cloned.1.call-start = ((), (), s32[]{:S(2)}) async-start(), calls=%async_computation.15 | async-start | bytes 33792000 | tf_op jit(solution)/shard_map/all_gather | solution.py:115
  12.7 1211.0 %reduce-scatter.16.cloned.1.call-start = ((), (), s32[]{:S(2)}) async-start(), calls=%async_computation.18 | async-start | bytes 4055040 | tf_op jit(solution)/shard_map/reduce_scatter | solution.py:67
  56.0 73.2 %copy-start.46 = (f32[256]{0:T(256)}, f32[256]{0:T(256)S(1)}, u32[]{:S(2)}) copy-start(f32[256]{0:T(256)S(1)} %convert_element_type.112) | copy-start | bytes 3076
  56.0 204.9 %copy-start.40 = (f32[768]{0:T(1024)}, f32[768]{0:T(1024)S(1)}, u32[]{:S(2)}) copy-start(f32[768]{0:T(1024)S(1)} %convert_element_type.114) | copy-start | bytes 9220
  56.5 934.9 %copy-start.55 = (f32[256]{0:T(256)}, f32[256]{0:T(256)S(1)}, u32[]{:S(2)}) copy-start(f32[256]{0:T(256)S(1)} %fusion.44) | copy-start | bytes 3076
  56.7 222.4 %copy-start.36 = (f32[128,16]{0,1:T(8,128)}, f32[128,16]{0,1:T(8,128)S(1)}, u32[]{:S(2)}) copy-start(f32[128,16]{0,1:T(8,128)S(1)} %get-tuple-element.89) | copy-start | bytes 24580
  56.7 222.4 %copy-start.38 = (f32[128,16]{0,1:T(8,128)}, f32[128,16]{0,1:T(8,128)S(1)}, u32[]{:S(2)}) copy-start(f32[128,16]{0,1:T(8,128)S(1)} %get-tuple-element.90) | copy-start | bytes 24580
  58.6 133.2 %copy-start.1 = (bf16[256,2560]{1,0:T(8,128)(2,1)}, bf16[256,2560]{1,0:T(8,128)(2,1)S(1)}, u32[]{:S(2)}) copy-start(bf16[256,2560]{1,0:T(8,128)(2,1)S(1)} %multiply_convert_fusion.6) | copy-start | bytes 3932164
  72.0 59.9 copy-start.18
  72.2 59.7 copy-start.48
  195.2 72.8 %copy-start.15 = (f32[256,768]{1,0:T(8,128)}, f32[256,768]{1,0:T(8,128)S(1)}, u32[]{:S(2)}) copy-start(f32[256,768]{1,0:T(8,128)S(1)} %get-tuple-element.92) | copy-start | bytes 2359300
  195.2 72.8 %copy-start.50 = (f32[256]{0:T(256)}, f32[256]{0:T(256)S(1)}, u32[]{:S(2)}) copy-start(f32[256]{0:T(256)S(1)} %add_rsqrt_fusion.1) | copy-start | bytes 3076
  285.4 81.6 %copy-start.11 = (bf16[2,128,40,64]{1,0,3,2:T(2,128)(2,1)}, bf16[2,128,40,64]{1,0,3,2:T(2,128)(2,1)S(1)}, u32[]{:S(2)}) copy-start(bf16[2,128,40,64]{1,0,3,2:T(2,128)(2,1)S(1)} %copy.71) | copy-start | bytes 3932164
  368.9 374.2 %copy-start.12 = (bf16[256,2560]{1,0:T(8,128)(2,1)}, bf16[256,2560]{1,0:T(8,128)(2,1)S(1)}, u32[]{:S(2)}) copy-start(bf16[256,2560]{1,0:T(8,128)(2,1)S(1)} %multiply_convert_fusion.5) | copy-start | bytes 3932164
  569.8 364.7 %copy-start.27 = (bf16[256,2560]{1,0:T(8,128)(2,1)S(1)}, bf16[256,2560]{1,0:T(8,128)(2,1)}, u32[]{:S(2)}) copy-start(bf16[256,2560]{1,0:T(8,128)(2,1)} %fusion.14) | copy-start | bytes 3932164
  1032.2 260.1 %reduce-scatter.18.cloned.1.call-start = ((), (), s32[]{:S(2)}) async-start(), calls=%async_computation.19 | async-start | bytes 5406720 | tf_op jit(solution)/shard_map/reduce_scatter | solution.py:67
  1037.2 383.7 %reduce-scatter.12.cloned.1.call-start = ((), (), s32[]{:S(2)}) async-start(), calls=%async_computation.16 | async-start | bytes 8110080 | tf_op jit(solution)/shard_map/reduce_scatter | solution.py:67
  1052.0 522.8 %reduce-scatter.14.cloned.1.call-start = ((), (), s32[]{:S(2)}) async-start(), calls=%async_computation.17 | async-start | bytes 12165120 | tf_op jit(solution)/shard_map/reduce_scatter | solution.py:67
  1059.3 1077.4 %reduce-scatter.20.cloned.1.call-start = ((), (), s32[]{:S(2)}) async-start(), calls=%async_computation.20 | async-start | bytes 27033600 | tf_op jit(solution)/shard_map/reduce_scatter | solution.py:67
  1073.3 2442.8 %reduce-scatter.24.cloned.1.call-start = ((), (), s32[]{:S(2)}) async-start(), calls=%async_computation.22 | async-start | bytes 67584000 | tf_op jit(solution)/shard_map/reduce_scatter | solution.py:67
  1099.7 3796.9 %reduce-scatter.22.cloned.1.call-start = ((), (), s32[]{:S(2)}) async-start(), calls=%async_computation.21 | async-start | bytes 67584000 | tf_op jit(solution)/shard_map/reduce_scatter | solution.py:67
  1124.6 5152.5 %reduce-scatter.26.cloned.1.call-start = ((), (), s32[]{:S(2)}) async-start(), calls=%async_computation.23 | async-start | bytes 67584000
  (52 other events, 180.0 us)
Sparse Core Ops, SparseCore 0:
  10.8 58.7 all-gather.8
  72.5 56.6 all-gather.10
  132.0 59.7 all-gather.12
  194.4 66.5 all-gather.14
  263.7 96.3 all-gather.16
  362.7 188.9 all-gather.20
  554.5 188.5 all-gather.18
  745.9 188.5 all-gather.22
  1032.3 102.6 reduce-scatter.15
  1137.8 154.5 reduce-scatter.17
  1298.6 122.2 reduce-scatter.11
  1427.4 147.4 reduce-scatter.13
  1577.7 558.9 reduce-scatter.19
  2139.5 1376.5 reduce-scatter.23
  3518.9 1377.6 reduce-scatter.21
  4899.4 1377.6 reduce-scatter.25

commit v2 on v1

--- a/solution.py
+++ b/solution.py
@@ -63,8 +63,23 @@
     )
 
 
+AXES = ("fsdp", "dp")
+
+
 def scatter_rows(term):
-    return lax.psum_scatter(term, ("fsdp", "dp"), scatter_dimension=0, tiled=True)
+    return lax.psum_scatter(term, AXES, scatter_dimension=0, tiled=True)
+
+
+def gather_tokens(values):
+    return lax.all_gather(values, AXES, axis=0, tiled=True)
+
+
+def column_share(values):
+    return lax.all_to_all(values, AXES, 1, 0, tiled=True)
+
+
+def rows_from_columns(grad):
+    return lax.all_to_all(grad, AXES, 0, 1, tiled=True)
 
 
 def local(
@@ -86,7 +101,6 @@
 ):
     micro, _, slot, width = tokens.shape
     rows = micro * slot
-    devices = lax.axis_size(("fsdp", "dp"))
     attn_shards = (
         attn_gain,
         query_down,
@@ -191,11 +205,12 @@
     grad_up = (grad_hidden * gate * sigma).astype(jnp.bfloat16)
     grad_h_two = back_product(grad_gate, feed_back[1]) + back_product(grad_up, feed_back[2])
     gain_two_term, grad_middle_norm = norm_back(grad_h_two, normed_two, inverse_two, feed_back[0])
+    h_two_all = gather_tokens(h_two)
     feed_sums = [
         scatter_rows(gain_two_term),
-        scatter_rows(rows_product(h_two, grad_gate)),
-        scatter_rows(rows_product(h_two, grad_up)),
-        scatter_rows(rows_product(hidden, grad_feed)),
+        rows_from_columns(rows_product(h_two_all, column_share(grad_gate))),
+        rows_from_columns(rows_product(h_two_all, column_share(grad_up))),
+        rows_product(column_share(hidden), gather_tokens(grad_feed)),
     ]
     grad_middle = grad_out + grad_middle_norm
     grad_attn = (depth_scale * grad_middle).astype(jnp.bfloat16)
@@ -247,15 +262,16 @@
     )
     gain_one_term, grad_input_norm = norm_back(grad_h_one, normed_one, inverse_one, attn_back[0])
     input_grad = (grad_middle + grad_input_norm).reshape(tokens.shape)
+    h_one_cols = column_share(h_one)
     attn_sums = [
         scatter_rows(gain_one_term),
-        scatter_rows(rows_product(h_one, grad_latent_query)),
+        rows_product(h_one_cols, gather_tokens(grad_latent_query)),
         scatter_rows(query_gain_term),
-        scatter_rows(rows_product(query_low, grad_query_raw)),
-        scatter_rows(rows_product(h_one, grad_latent_all)),
+        rows_from_columns(rows_product(gather_tokens(query_low), column_share(grad_query_raw))),
+        rows_product(h_one_cols, gather_tokens(grad_latent_all)),
         scatter_rows(latent_gain_term),
-        scatter_rows(rows_product(latent_low, grad_kv)),
-        scatter_rows(rows_product(attended, grad_attn)),
+        rows_from_columns(rows_product(gather_tokens(latent_low), column_share(grad_kv))),
+        rows_product(column_share(attended), gather_tokens(grad_attn)),
     ]
     return (
         output,

time: 6290 us -> 2350 us (0.37)
  waiting for transfers between devices: 5840 us -> 1560 us
  local copies, waits for them, and re-layouts: 54.9 us -> 211 us
  blocking collectives: 83.3 us -> 182 us
  starting transfers between devices: 0.63 us -> 75.2 us
    reduce_scatter x7 -> x0, waiting for transfers between devices: 3670 us -> none  [scatter_rows(): lax.psum_scatter(term, ('fsdp', 'dp'), scatter_dimension=0, tiled=True)]
    unnamed x17 -> x15, waiting for transfers between devices: 1390 us -> 6.34 us
    all_to_all x0 -> x11, waiting for transfers between devices: none -> 472 us  [the longest x7 413 us: column_share(): return lax.all_to_all(values, AXES, 1, 0, tiled=True)]
    all_gather x0 -> x7, waiting for transfers between devices: none -> 303 us  [gather_tokens(): return lax.all_gather(values, AXES, axis=0, tiled=True)]
    unnamed x2, blocking collectives: 83.3 us -> 182 us
    all_to_all x0 -> x11, starting transfers between devices: none -> 74 us  [the longest x7 53.5 us: column_share(): return lax.all_to_all(values, AXES, 1, 0, tiled=True)]
    dot_general x0 -> x2, local copies, waits for them, and re-layouts: none -> 66.1 us  [rows_product(): lax.dot_general(left, right, (((0,), (0,)), ((), ())), preferred_element_...]
  transfers between devices with their start and end apart: 16 -> 26, of which waited for: 15 -> 19; matrix products, arithmetic and copies ran while one was open for 4% -> 21% of each run, Pallas kernels for 0% -> 0%
where the time goes in v2:
time: 2350 us; the launch traced here: 2340 us
  waiting for transfers between devices  1560 us (66%)
  matrix products  274 us (12%)
  local copies, waits for them, and re-layouts  211 us (9%)
  blocking collectives  182 us (8%)
  starting transfers between devices  75.2 us (3%)
  other arithmetic  27.7 us (1%)
    all_to_all x7, waiting for transfers between devices, column_share(): return lax.all_to_all(values, AXES, 1, 0, tiled=True)  413 us
    all_gather x7, waiting for transfers between devices, gather_tokens(): return lax.all_gather(values, AXES, axis=0, tiled=True)  303 us
    unnamed x2, blocking collectives  182 us
    all_gather x1, waiting for transfers between devices, local(): lax.all_gather(feed_shards[1], ('fsdp', 'dp'), axis=0, tiled=True)  177 us
    all_gather x1, waiting for transfers between devices, local(): lax.all_gather(feed_shards[3], ('fsdp', 'dp'), axis=0, tiled=True)  174 us
    all_gather x1, waiting for transfers between devices, local(): lax.all_gather(feed_shards[2], ('fsdp', 'dp'), axis=0, tiled=True)  173 us
    dot_general x8, matrix products, rows_product(): lax.dot_general(left, right, (((0,), (0,)), ((), ())), preferred_element_...  104 us
    dot_general x8, matrix products, matmul(): return jnp.dot(left, right, preferred_element_type=jnp.float32)  79.2 us
  transfers between devices with their start and end apart: 26, of which 19 were waited for; matrix products, arithmetic and copies ran while one was open for 21% of the time, Pallas kernels for 0%

profile of v2, /device:TPU:0, one launch (start us, length us, event | category | flops | bytes accessed | tf_op | source)
XLA Modules:
  0.0 2342.2 jit_solution(2989831390764208140)
XLA Ops:
  13.8 42.4 %all-reduce.9 = (bf16[2560]{0:T(1024)(128)(2,1)S(1)}, bf16[256]{0:T(256)(128)(2,1)S(1)}, bf16[768]{0:T(1024)(128)(2,1)S(1)}, bf16[2560]{0:T(1024)(128)(2,1)S(1)}) all-reduce(bf16[2560]{0:T(1024)(128)(2,1)S(1)} %dynamic-update-slice, bf16[256]{0:T(256)(128)(2,1)S(1)} %dynamic-update-slice.1, ...), channel_id=1, replica_groups=mesh['fsdp'=8,'dp'=4] {'fsdp','dp'}, use_global_device_ids=true, to_apply=%add | all-reduce | flops 6144 | bytes 24576
  57.6 17.0 all-gather.20.cloned.1.call-done
  79.9 52.5 %all-gather.16.cloned.1.call-done = bf16[2560,288]{1,0:T(8,128)(2,1)} async-done(((bf16[80,288]{1,0:T(8,128)(2,1)}), bf16[2560,288]{1,0:T(8,128)(2,1)}) %all-gather.16.cloned.1.call-update) | async-done | bytes 1474576 | tf_op jit(solution)/shard_map/all_gather | solution.py:120
  138.6 53.3 %all-gather.18.cloned.1.call-done = bf16[256,5120]{1,0:T(8,128)(2,1)} async-done(((bf16[8,5120]{1,0:T(8,128)(2,1)}), bf16[256,5120]{1,0:T(8,128)(2,1)}) %all-gather.18.cloned.1.call-update) | async-done | bytes 2621456 | tf_op jit(solution)/shard_map/all_gather | solution.py:122
  205.8 55.2 %all-gather.22.cloned.1.call-done = bf16[768,3840]{1,0:T(8,128)(2,1)} async-done(((bf16[24,3840]{1,0:T(8,128)(2,1)}), bf16[768,3840]{1,0:T(8,128)(2,1)}) %all-gather.22.cloned.1.call-update) | async-done | bytes 5898256 | tf_op jit(solution)/shard_map/all_gather | solution.py:119
  286.5 73.5 %all-gather.24.cloned.1.call-done = bf16[2560,2560]{1,0:T(8,128)(2,1)} async-done(((bf16[80,2560]{1,0:T(8,128)(2,1)}), bf16[2560,2560]{1,0:T(8,128)(2,1)}) %all-gather.24.cloned.1.call-update) | async-done | bytes 13107216 | tf_op jit(solution)/shard_map/all_gather | solution.py:123
  374.3 177.4 %all-gather.26.cloned.1.call-done = bf16[2560,6400]{1,0:T(8,128)(2,1)} async-done(((bf16[80,6400]{1,0:T(8,128)(2,1)}), bf16[2560,6400]{1,0:T(8,128)(2,1)}) %all-gather.26.cloned.1.call-update) | async-done | bytes 32768016 | tf_op jit(solution)/shard_map/all_gather | solution.py:127
  551.7 18.2 fusion.44
  569.9 173.3 %all-gather.28.cloned.1.call-done = bf16[2560,6400]{1,0:T(8,128)(2,1)} async-done(((bf16[80,6400]{1,0:T(8,128)(2,1)}), bf16[2560,6400]{1,0:T(8,128)(2,1)}) %all-gather.28.cloned.1.call-update) | async-done | bytes 32768016 | tf_op jit(solution)/shard_map/all_gather | solution.py:128
  743.2 17.7 fusion.45
  760.9 173.8 %all-gather.30.cloned.1.call-done = bf16[6400,2560]{1,0:T(8,128)(2,1)} async-done(((bf16[200,2560]{1,0:T(8,128)(2,1)}), bf16[6400,2560]{1,0:T(8,128)(2,1)}) %all-gather.30.cloned.1.call-update) | async-done | bytes 32768016 | tf_op jit(solution)/shard_map/all_gather | solution.py:129
  934.6 21.6 multiply_convert_fusion
  956.2 16.9 fusion.46
  973.1 19.0 multiply_reduce_fusion.1
  1060.0 40.8 %all-to-all-done = bf16[256,32,80]{0,2,1:T(8,128)(2,1)} async-done(((bf16[256,32,80]{0,2,1:T(8,128)(2,1)}), bf16[256,32,80]{0,2,1:T(8,128)(2,1)}, u32[]{:S(2)}, u32[]{:S(2)}) %all-to-all-start) | async-done | bytes 1310752 | tf_op jit(solution)/shard_map/all_to_all | solution.py:78
  1108.0 31.3 %all-to-all-done.5 = bf16[256,32,80]{0,2,1:T(8,128)(2,1)} async-done(((bf16[256,32,80]{0,2,1:T(8,128)(2,1)}), bf16[256,32,80]{0,2,1:T(8,128)(2,1)}, u32[]{:S(2)}, u32[]{:S(2)}) %all-to-all-start.5) | async-done | bytes 1310752 | tf_op jit(solution)/shard_map/all_to_all | solution.py:78
  1158.4 58.4 %all-to-all-done.1 = bf16[256,32,120]{0,2,1:T(8,128)(2,1)S(1)} async-done(((bf16[256,32,120]{0,2,1:T(8,128)(2,1)}), bf16[256,32,120]{0,2,1:T(8,128)(2,1)S(1)}, u32[]{:S(2)}, u32[]{:S(2)}) %all-to-all-start.1) | async-done | bytes 1966112 | tf_op jit(solution)/shard_map/all_to_all | solution.py:78
  1228.4 15.7 copy.108
  1255.8 65.9 %all-to-all-done.3 = bf16[256,32,160]{0,2,1:T(8,128)(2,1)} async-done(((bf16[256,32,160]{0,2,1:T(8,128)(2,1)}), bf16[256,32,160]{0,2,1:T(8,128)(2,1)}, u32[]{:S(2)}, u32[]{:S(2)}) %all-to-all-start.3) | async-done | bytes 2621472 | tf_op jit(solution)/shard_map/all_to_all | solution.py:78
  1378.6 133.6 %all-to-all-done.6 = bf16[256,32,200]{0,2,1:T(8,128)(2,1)} async-done(((bf16[256,32,200]{0,2,1:T(8,128)(2,1)}), bf16[256,32,200]{0,2,1:T(8,128)(2,1)}, u32[]{:S(2)}, u32[]{:S(2)}) %all-to-all-start.6) | async-done | bytes 3276832 | tf_op jit(solution)/shard_map/all_to_all | solution.py:78
  1525.0 83.1 %all-to-all-done.8 = bf16[256,32,200]{0,2,1:T(8,128)(2,1)} async-done(((bf16[256,32,200]{0,2,1:T(8,128)(2,1)}), bf16[256,32,200]{0,2,1:T(8,128)(2,1)}, u32[]{:S(2)}, u32[]{:S(2)}) %all-to-all-start.8) | async-done | bytes 3276832 | tf_op jit(solution)/shard_map/all_to_all | solution.py:78
  1608.1 12.1 all-to-all-start.10
  1629.1 139.5 %all-reduce.8 = (f32[2560]{0:T(1024)S(1)}, f32[768]{0:T(1024)S(1)}, f32[256]{0:T(256)S(1)}, f32[2560]{0:T(1024)S(1)}) all-reduce(f32[2560]{0:T(1024)S(1)} %get-tuple-element.58, f32[768]{0:T(1024)S(1)} %copy-done.44, f32[256]{0:T(256)S(1)} %copy-done.45, f32[2560]{0:T(1024)S(1)} %copy-done.35), channel_id=2, replica_groups=mesh['fsdp'=8,'dp'=4] {'fsdp','dp'}, use_global_device_ids=true, to_apply=%region_13.14.clone | all-reduce | flops 6144 | bytes 49152
  1781.6 50.4 %copy.117 = bf16[2560,8192]{1,0:T(8,128)(2,1)} copy(bf16[2560,8192]{0,1:T(8,128)(2,1)} %bitcast.173) | data formatting | bytes 83886080 | tf_op jit(solution)/shard_map/dot_general | solution.py:25
  1831.9 20.9 fusion.52
  1859.2 18.4 fusion.7
  1888.2 20.8 fusion.53
  1909.0 45.2 %all-to-all-done.7 = f32[32,80,200]{2,1,0:T(8,128)} async-done(((f32[32,80,200]{2,1,0:T(8,128)}), f32[32,80,200]{2,1,0:T(8,128)}, u32[]{:S(2)}, u32[]{:S(2)}) %all-to-all-start.7) | async-done | bytes 2048032 | tf_op jit(solution)/shard_map/all_to_all | solution.py:82
  1975.7 19.7 fusion.54
  1995.3 86.5 %all-gather.32.cloned.1.call-done = bf16[8192,768]{1,0:T(8,128)(2,1)} async-done(((bf16[256,768]{1,0:T(8,128)(2,1)}), bf16[8192,768]{1,0:T(8,128)(2,1)}) %all-gather.32.cloned.1.call-update) | async-done | bytes 12582928 | tf_op jit(solution)/shard_map/all_gather | solution.py:74
  2101.3 216.2 %all-gather.40.cloned.1.call-done = bf16[8192,2560]{1,0:T(8,128)(2,1)} async-done(((bf16[256,2560]{1,0:T(8,128)(2,1)}), bf16[8192,2560]{1,0:T(8,128)(2,1)}) %all-gather.40.cloned.1.call-update) | async-done | bytes 41943056 | tf_op jit(solution)/shard_map/all_gather | solution.py:74
  2317.6 17.9 fusion.51
  (285 shorter events, 338.9 us)
Async XLA Ops:
  7.2 67.4 %all-gather.20.cloned.1.call-start = ((), (), s32[]{:S(2)}) async-start(), calls=%async_computation.13 | async-start | bytes 4055040 | tf_op jit(solution)/shard_map/all_gather | solution.py:117
  8.0 124.4 %all-gather.16.cloned.1.call-start = ((), (), s32[]{:S(2)}) async-start(), calls=%async_computation.11 | async-start | bytes 2027520 | tf_op jit(solution)/shard_map/all_gather | solution.py:120
  8.7 183.1 %all-gather.18.cloned.1.call-start = ((), (), s32[]{:S(2)}) async-start(), calls=%async_computation.12 | async-start | bytes 2703360 | tf_op jit(solution)/shard_map/all_gather | solution.py:122
  9.4 251.6 %all-gather.22.cloned.1.call-start = ((), (), s32[]{:S(2)}) async-start(), calls=%async_computation.14 | async-start | bytes 6082560 | tf_op jit(solution)/shard_map/all_gather | solution.py:119
  10.0 350.0 %all-gather.24.cloned.1.call-start = ((), (), s32[]{:S(2)}) async-start(), calls=%async_computation.15 | async-start | bytes 13516800 | tf_op jit(solution)/shard_map/all_gather | solution.py:123
  10.6 541.1 %all-gather.26.cloned.1.call-start = ((), (), s32[]{:S(2)}) async-start(), calls=%async_computation.16 | async-start | bytes 33792000 | tf_op jit(solution)/shard_map/all_gather | solution.py:127
  11.2 732.0 %all-gather.28.cloned.1.call-start = ((), (), s32[]{:S(2)}) async-start(), calls=%async_computation.17 | async-start | bytes 33792000 | tf_op jit(solution)/shard_map/all_gather | solution.py:128
  11.9 922.7 %all-gather.30.cloned.1.call-start = ((), (), s32[]{:S(2)}) async-start(), calls=%async_computation.18 | async-start | bytes 33792000 | tf_op jit(solution)/shard_map/all_gather | solution.py:129
  12.7 1215.7 %all-gather.34.cloned.1.call-start = ((), (), s32[]{:S(2)}) async-start(), calls=%async_computation.20 | async-start | bytes 12976128 | tf_op jit(solution)/shard_map/all_gather | solution.py:74
  79.8 1257.0 %all-gather.38.cloned.1.call-start = ((), (), s32[]{:S(2)}) async-start(), calls=%async_computation.22 | async-start | bytes 4325376 | tf_op jit(solution)/shard_map/all_gather | solution.py:74
  79.9 58.4 %copy-start.42 = (f32[256]{0:T(256)}, f32[256]{0:T(256)S(1)}, u32[]{:S(2)}) copy-start(f32[256]{0:T(256)S(1)} %convert_element_type.138) | copy-start | bytes 3076
  134.7 59.7 %copy-start.15 = (f32[256,288]{0,1:T(8,128)}, f32[256,288]{0,1:T(8,128)S(1)}, u32[]{:S(2)}) copy-start(f32[256,288]{0,1:T(8,128)S(1)} %fusion.42) | copy-start | bytes 884740
  136.2 55.6 %copy-start.23 = (bf16[256,256]{0,1:T(8,128)(2,1)S(1)}, bf16[256,256]{0,1:T(8,128)(2,1)}, u32[]{:S(2)}) copy-start(bf16[256,256]{0,1:T(8,128)(2,1)} %multiply_convert_fusion.11) | copy-start | bytes 393220
  136.2 1645.4 %all-gather.42.cloned.1.call-start = ((), (), s32[]{:S(2)}) async-start(), calls=%async_computation.24 | async-start | bytes 43253760 | tf_op jit(solution)/shard_map/all_gather | solution.py:74
  202.4 58.7 %copy-start.18 = (bf16[256,768]{1,0:T(8,128)(2,1)S(1)}, bf16[256,768]{1,0:T(8,128)(2,1)}, u32[]{:S(2)}) copy-start(bf16[256,768]{1,0:T(8,128)(2,1)} %multiply_convert_fusion.9) | copy-start | bytes 1179652
  369.7 622.5 %copy-start.3 = (f32[256,2560]{1,0:T(8,128)}, f32[256,2560]{1,0:T(8,128)S(1)}, u32[]{:S(2)}) copy-start(f32[256,2560]{1,0:T(8,128)S(1)} %get-tuple-element.98) | copy-start | bytes 7864324
  371.3 1599.6 %all-gather.36.cloned.1.call-start = ((), (), s32[]{:S(2)}) async-start(), calls=%async_computation.21 | async-start | bytes 4866048 | tf_op jit(solution)/shard_map/all_gather | solution.py:74
  371.4 620.7 %copy-start.40 = (f32[256]{0:T(256)}, f32[256]{0:T(256)S(1)}, u32[]{:S(2)}) copy-start(f32[256]{0:T(256)S(1)} %fusion.33) | copy-start | bytes 3076
  1032.9 942.8 %all-gather.44.cloned.1.call-start = ((), (), s32[]{:S(2)}) async-start(), calls=%async_computation.25 | async-start | bytes 43253760 | tf_op jit(solution)/shard_map/all_gather | solution.py:74
  1033.6 1048.2 %all-gather.32.cloned.1.call-start = ((), (), s32[]{:S(2)}) async-start(), calls=%async_computation.19 | async-start | bytes 12976128 | tf_op jit(solution)/shard_map/all_gather | solution.py:74
  1042.8 1274.8 %all-gather.40.cloned.1.call-start = ((), (), s32[]{:S(2)}) async-start(), calls=%async_computation.23 | async-start | bytes 43253760 | tf_op jit(solution)/shard_map/all_gather | solution.py:74
  1054.5 46.3 %all-to-all-start = ((bf16[256,32,80]{0,2,1:T(8,128)(2,1)}), bf16[256,32,80]{0,2,1:T(8,128)(2,1)}, u32[]{:S(2)}, u32[]{:S(2)}) async-start(bf16[256,32,80]{0,2,1:T(8,128)(2,1)} %multiply_convert_fusion.4), calls=%async_computation | async-start | bytes 2621440 | tf_op jit(solution)/shard_map/all_to_all | solution.py:78
  1100.8 38.5 %all-to-all-start.5 = ((bf16[256,32,80]{0,2,1:T(8,128)(2,1)}), bf16[256,32,80]{0,2,1:T(8,128)(2,1)}, u32[]{:S(2)}, u32[]{:S(2)}) async-start(bf16[256,32,80]{0,2,1:T(8,128)(2,1)} %convert_element_type.171), calls=%async_computation.5 | async-start | bytes 2621440 | tf_op jit(solution)/shard_map/all_to_all | solution.py:78
  1139.3 77.5 %all-to-all-start.1 = ((bf16[256,32,120]{0,2,1:T(8,128)(2,1)}), bf16[256,32,120]{0,2,1:T(8,128)(2,1)S(1)}, u32[]{:S(2)}, u32[]{:S(2)}) async-start(bf16[256,32,120]{0,2,1:T(8,128)(2,1)} %convert_element_type.169), calls=%async_computation.1 | async-start | bytes 3932160 | tf_op jit(solution)/shard_map/all_to_all | solution.py:78
  1216.8 105.0 %all-to-all-start.3 = ((bf16[256,32,160]{0,2,1:T(8,128)(2,1)}), bf16[256,32,160]{0,2,1:T(8,128)(2,1)}, u32[]{:S(2)}, u32[]{:S(2)}) async-start(bf16[256,32,160]{0,2,1:T(8,128)(2,1)} %convert_element_type.170), calls=%async_computation.3 | async-start | bytes 5242880 | tf_op jit(solution)/shard_map/all_to_all | solution.py:78
  1321.7 25.5 %all-to-all-start.2 = ((f32[32,24,120]{2,1,0:T(8,128)}), f32[32,24,120]{2,1,0:T(8,128)S(1)}, u32[]{:S(2)}, u32[]{:S(2)}) async-start(f32[32,24,120]{2,1,0:T(8,128)} %fusion.49), calls=%async_computation.2 | async-start | bytes 786432 | tf_op jit(solution)/shard_map/all_to_all | solution.py:82
  1347.3 18.4 all-to-all-start.4
  1366.4 145.8 %all-to-all-start.6 = ((bf16[256,32,200]{0,2,1:T(8,128)(2,1)}), bf16[256,32,200]{0,2,1:T(8,128)(2,1)}, u32[]{:S(2)}, u32[]{:S(2)}) async-start(bf16[256,32,200]{0,2,1:T(8,128)(2,1)} %bitcast.181), calls=%async_computation.6 | async-start | bytes 6553600 | tf_op jit(solution)/shard_map/all_to_all | solution.py:78
  1512.1 96.0 %all-to-all-start.8 = ((bf16[256,32,200]{0,2,1:T(8,128)(2,1)}), bf16[256,32,200]{0,2,1:T(8,128)(2,1)}, u32[]{:S(2)}, u32[]{:S(2)}) async-start(bf16[256,32,200]{0,2,1:T(8,128)(2,1)} %bitcast.182), calls=%async_computation.8 | async-start | bytes 6553600 | tf_op jit(solution)/shard_map/all_to_all | solution.py:78
  1608.1 244.8 %all-to-all-start.10 = ((bf16[256,32,200]{0,2,1:T(8,128)(2,1)}), bf16[256,32,200]{0,2,1:T(8,128)(2,1)}, u32[]{:S(2)}, u32[]{:S(2)}) async-start(bf16[256,32,200]{0,2,1:T(8,128)(2,1)} %bitcast.180), calls=%async_computation.10 | async-start | bytes 6553600 | tf_op jit(solution)/shard_map/all_to_all | solution.py:78
  1852.9 101.4 %all-to-all-start.7 = ((f32[32,80,200]{2,1,0:T(8,128)}), f32[32,80,200]{2,1,0:T(8,128)}, u32[]{:S(2)}, u32[]{:S(2)}) async-start(f32[32,80,200]{2,1,0:T(8,128)} %fusion.52), calls=%async_computation.7 | async-start | bytes 5242880 | tf_op jit(solution)/shard_map/all_to_all | solution.py:82
  1954.2 141.1 %all-to-all-start.9 = ((f32[32,80,200]{2,1,0:T(8,128)}), f32[32,80,200]{2,1,0:T(8,128)}, u32[]{:S(2)}, u32[]{:S(2)}) async-start(f32[32,80,200]{2,1,0:T(8,128)} %fusion.53), calls=%async_computation.9 | async-start | bytes 5242880 | tf_op jit(solution)/shard_map/all_to_all | solution.py:82
  (49 other events, 269.9 us)
Sparse Core Ops, SparseCore 0:
  10.8 63.7 all-gather.19
  77.4 54.9 all-gather.15
  135.2 56.5 all-gather.17
  194.5 66.5 all-gather.21
  263.7 96.3 all-gather.23
  362.8 188.9 all-gather.25
  554.6 188.5 all-gather.27
  746.0 188.5 all-gather.29
  937.5 93.3 all-gather.33
  1034.2 90.8 all-gather.37
  1128.6 396.8 all-gather.41
  1528.7 93.9 all-gather.35
  1625.6 327.0 all-gather.43
  1955.9 125.8 all-gather.31
  2084.5 233.0 all-gather.39

commit v3 on v1

--- a/solution.py
+++ b/solution.py
@@ -15,6 +15,8 @@
 epsilon = 1e-05
 depth_scale = 1.4 / math.sqrt(62.0)
 masked_score = -1e30
+AXES = ("fsdp", "dp")
+LANES = 128
 
 
 def matmul(left, right):
@@ -63,8 +65,48 @@
     )
 
 
-def scatter_rows(term):
-    return lax.psum_scatter(term, ("fsdp", "dp"), scatter_dimension=0, tiled=True)
+def padded(size):
+    return -(-size // LANES) * LANES
+
+
+def gather_packed(shards):
+    flat = []
+    for shard in shards:
+        piece = shard.reshape(-1)
+        flat.append(jnp.pad(piece, (0, padded(piece.size) - piece.size)))
+    gathered = lax.all_gather(jnp.concatenate(flat), AXES, axis=0, tiled=False)
+    devices = gathered.shape[0]
+    results = []
+    offset = 0
+    for shard in shards:
+        piece = gathered[:, offset : offset + shard.size]
+        results.append(piece.reshape((devices * shard.shape[0],) + shard.shape[1:]))
+        offset = offset + padded(shard.size)
+    return results
+
+
+def gather_tokens(values):
+    return lax.all_gather(values, AXES, axis=0, tiled=True)
+
+
+def column_shares(stacked, devices):
+    tokens, count, width = stacked.shape
+    blocks = stacked.reshape(tokens, count, devices, width // devices)
+    moved = lax.all_to_all(blocks, AXES, 2, 0, tiled=True)
+    return moved.reshape(devices * tokens, count, width // devices)
+
+
+def rows_from_columns(grad, devices):
+    rows, count, share = grad.shape
+    moved = lax.all_to_all(grad, AXES, 0, 2, tiled=True)
+    return moved.reshape(rows // devices, count, devices, share).reshape(
+        rows // devices, count, devices * share
+    )
+
+
+def split_exact(values):
+    high = lax.reduce_precision(values, exponent_bits=8, mantissa_bits=7)
+    return (high.astype(jnp.bfloat16), (values - high).astype(jnp.bfloat16))
 
 
 def local(
@@ -86,38 +128,35 @@
 ):
     micro, _, slot, width = tokens.shape
     rows = micro * slot
-    devices = lax.axis_size(("fsdp", "dp"))
+    devices = lax.axis_size(AXES)
+    me = lax.axis_index(AXES)
+    ffn = gate_weight.shape[1]
     attn_shards = (
-        attn_gain,
         query_down,
-        query_gain,
         query_up,
         latent_down,
-        latent_gain,
         latent_up,
         output_weight,
-    )
-    feed_shards = (feed_gain, gate_weight, up_weight, down_weight)
-    attn_full = (
-        lax.all_gather(attn_shards[0], ("fsdp", "dp"), axis=0, tiled=True),
-        lax.all_gather(attn_shards[1], ("fsdp", "dp"), axis=0, tiled=True),
-        lax.all_gather(attn_shards[2], ("fsdp", "dp"), axis=0, tiled=True),
-        lax.all_gather(attn_shards[3], ("fsdp", "dp"), axis=0, tiled=True),
-        lax.all_gather(attn_shards[4], ("fsdp", "dp"), axis=0, tiled=True),
-        lax.all_gather(attn_shards[5], ("fsdp", "dp"), axis=0, tiled=True),
-        lax.all_gather(attn_shards[6], ("fsdp", "dp"), axis=0, tiled=True),
-        lax.all_gather(attn_shards[7], ("fsdp", "dp"), axis=0, tiled=True),
-    )
-    feed_full = (
-        lax.all_gather(feed_shards[0], ("fsdp", "dp"), axis=0, tiled=True),
-        lax.all_gather(feed_shards[1], ("fsdp", "dp"), axis=0, tiled=True),
-        lax.all_gather(feed_shards[2], ("fsdp", "dp"), axis=0, tiled=True),
-        lax.all_gather(feed_shards[3], ("fsdp", "dp"), axis=0, tiled=True),
-    )
-    gain_one, down_query, gain_query, up_query, down_latent, gain_latent, up_latent, weight_out = (
-        attn_full
-    )
-    gain_two, weight_gate, weight_up, weight_down = feed_full
+        attn_gain,
+        query_gain,
+        latent_gain,
+        feed_gain,
+    )
+    (
+        down_query,
+        up_query,
+        down_latent,
+        up_latent,
+        weight_out,
+        gain_one,
+        gain_query,
+        gain_latent,
+        gain_two,
+    ) = gather_packed(attn_shards)
+    weight_gate_up = lax.all_gather(
+        jnp.concatenate([gate_weight, up_weight], axis=1), AXES, axis=0, tiled=True
+    )
+    weight_down = lax.all_gather(down_weight, AXES, axis=0, tiled=True)
     half = ROPE // 2
     freqs = 10000.0 ** (-(2.0 * jnp.arange(half, dtype=jnp.float32)) / ROPE)
     angles = jnp.arange(slot, dtype=jnp.float32)[:, None] * freqs[None, :]
@@ -159,48 +198,61 @@
         "mhqk,mkhd->mqhd", probs.astype(jnp.bfloat16), values, preferred_element_type=jnp.float32
     )
     attended = attended.reshape(rows, HEADS * VDIM).astype(jnp.bfloat16)
+    q_rank = query_low.shape[1]
+    kv_rank = latent_low.shape[1]
+    latents_all = gather_tokens(jnp.concatenate([query_low, latent_low, attended], axis=1))
+    query_low_all = latents_all[:, :q_rank]
+    latent_low_all = latents_all[:, q_rank : q_rank + kv_rank]
+    attended_all = latents_all[:, q_rank + kv_rank :]
+    h_one_cols = column_shares(h_one[:, None, :], devices)[:, 0]
     middle = inputs + depth_scale * matmul(attended, weight_out)
     normed_two, inverse_two = normalize(middle)
     h_two = (normed_two * gain_two.astype(jnp.float32)).astype(jnp.bfloat16)
-    gate = matmul(h_two, weight_gate)
-    upward = matmul(h_two, weight_up)
+    gate_up = matmul(h_two, weight_gate_up)
+    gate = gate_up[:, :ffn]
+    upward = gate_up[:, ffn:]
     sigma = jax.nn.sigmoid(gate)
     hidden = (gate * sigma * upward).astype(jnp.bfloat16)
     result = (middle + depth_scale * matmul(hidden, weight_down)) * valid_rows
     output = result.astype(jnp.bfloat16).reshape(tokens.shape)
-    feed_back = (
-        lax.all_gather(feed_shards[0], ("fsdp", "dp"), axis=0, tiled=True),
-        lax.all_gather(feed_shards[1], ("fsdp", "dp"), axis=0, tiled=True),
-        lax.all_gather(feed_shards[2], ("fsdp", "dp"), axis=0, tiled=True),
-        lax.all_gather(feed_shards[3], ("fsdp", "dp"), axis=0, tiled=True),
-    )
-    attn_back = (
-        lax.all_gather(attn_shards[0], ("fsdp", "dp"), axis=0, tiled=True),
-        lax.all_gather(attn_shards[1], ("fsdp", "dp"), axis=0, tiled=True),
-        lax.all_gather(attn_shards[2], ("fsdp", "dp"), axis=0, tiled=True),
-        lax.all_gather(attn_shards[3], ("fsdp", "dp"), axis=0, tiled=True),
-        lax.all_gather(attn_shards[4], ("fsdp", "dp"), axis=0, tiled=True),
-        lax.all_gather(attn_shards[5], ("fsdp", "dp"), axis=0, tiled=True),
-        lax.all_gather(attn_shards[6], ("fsdp", "dp"), axis=0, tiled=True),
-        lax.all_gather(attn_shards[7], ("fsdp", "dp"), axis=0, tiled=True),
-    )
     grad_out = cotangent.reshape(rows, width).astype(jnp.float32) * valid_rows
     grad_feed = (depth_scale * grad_out).astype(jnp.bfloat16)
-    grad_hidden = back_product(grad_feed, feed_back[3])
+    feed_all = lax.all_gather(jnp.stack([h_two, grad_feed]), AXES, axis=1, tiled=True)
+    h_two_all = feed_all[0]
+    grad_feed_all = feed_all[1]
+    grad_hidden = back_product(grad_feed, weight_down)
     grad_gate = (grad_hidden * upward * sigma * (1.0 + gate * (1.0 - sigma))).astype(jnp.bfloat16)
     grad_up = (grad_hidden * gate * sigma).astype(jnp.bfloat16)
-    grad_h_two = back_product(grad_gate, feed_back[1]) + back_product(grad_up, feed_back[2])
-    gain_two_term, grad_middle_norm = norm_back(grad_h_two, normed_two, inverse_two, feed_back[0])
-    feed_sums = [
-        scatter_rows(gain_two_term),
-        scatter_rows(rows_product(h_two, grad_gate)),
-        scatter_rows(rows_product(h_two, grad_up)),
-        scatter_rows(rows_product(hidden, grad_feed)),
-    ]
+    grad_h_two = back_product(jnp.concatenate([grad_gate, grad_up], axis=1), weight_gate_up)
+    gain_two_term, grad_middle_norm = norm_back(grad_h_two, normed_two, inverse_two, gain_two)
     grad_middle = grad_out + grad_middle_norm
     grad_attn = (depth_scale * grad_middle).astype(jnp.bfloat16)
+    ff_share = ffn // devices
+    attn_share = width // devices
+    feed_cols = column_shares(
+        jnp.concatenate(
+            [
+                jnp.stack([hidden, grad_gate, grad_up], axis=1)
+                .reshape(rows, 3, devices, ff_share)
+                .transpose(0, 2, 1, 3)
+                .reshape(rows, devices, 3 * ff_share),
+                grad_attn.reshape(rows, devices, attn_share),
+            ],
+            axis=2,
+        ).reshape(rows, 1, devices * (3 * ff_share + attn_share)),
+        devices,
+    )[:, 0]
+    down_grad = rows_product(feed_cols[:, :ff_share], grad_feed_all)
+    gate_up_cols = rows_product(h_two_all, feed_cols[:, ff_share : 3 * ff_share])
+    out_cols = rows_product(attended_all, feed_cols[:, 3 * ff_share :])
+    wide_rows = rows_from_columns(
+        jnp.concatenate([gate_up_cols, out_cols], axis=1)[:, None, :], devices
+    ).reshape(width // devices, devices, 2 * ff_share + attn_share)
+    gate_grad = wide_rows[:, :, :ff_share].reshape(width // devices, ffn)
+    up_grad = wide_rows[:, :, ff_share : 2 * ff_share].reshape(width // devices, ffn)
+    output_weight_grad = wide_rows[:, :, 2 * ff_share :].reshape(width // devices, width)
     grad_heads = (
-        back_product(grad_attn, attn_back[7]).astype(jnp.bfloat16).reshape(micro, slot, HEADS, VDIM)
+        back_product(grad_attn, weight_out).astype(jnp.bfloat16).reshape(micro, slot, HEADS, VDIM)
     )
     probs_again = jnp.exp(scores - log_total)
     grad_values = jnp.einsum(
@@ -224,54 +276,116 @@
         [grad_queries[..., :NOPE], rotate_back(grad_queries[..., NOPE:], cosines, sines)], axis=-1
     )
     grad_query_raw = grad_query_raw.reshape(rows, HEADS * (NOPE + ROPE)).astype(jnp.bfloat16)
-    grad_query_low = back_product(grad_query_raw, attn_back[3])
+    grad_query_low = back_product(grad_query_raw, up_query)
     grad_kv = (
         jnp.concatenate([grad_keys[..., :NOPE], grad_values], axis=-1)
         .reshape(rows, HEADS * (NOPE + VDIM))
         .astype(jnp.bfloat16)
     )
-    grad_latent_low = back_product(grad_kv, attn_back[6])
+    grad_latent_low = back_product(grad_kv, up_latent)
     latent_gain_term, grad_latent = norm_back(
-        grad_latent_low, normed_latent, inverse_latent, attn_back[5]
+        grad_latent_low, normed_latent, inverse_latent, gain_latent
     )
     grad_key_rope = rotate_back(
         jnp.sum(grad_keys[..., NOPE:], axis=2, keepdims=True), cosines, sines
     ).reshape(rows, ROPE)
     grad_latent_all = jnp.concatenate([grad_latent, grad_key_rope], axis=-1).astype(jnp.bfloat16)
     query_gain_term, grad_latent_query = norm_back(
-        grad_query_low, normed_query, inverse_query, attn_back[2]
+        grad_query_low, normed_query, inverse_query, gain_query
     )
     grad_latent_query = grad_latent_query.astype(jnp.bfloat16)
-    grad_h_one = back_product(grad_latent_all, attn_back[4]) + back_product(
-        grad_latent_query, attn_back[1]
-    )
-    gain_one_term, grad_input_norm = norm_back(grad_h_one, normed_one, inverse_one, attn_back[0])
+    query_width = up_query.shape[1]
+    kv_width = up_latent.shape[1]
+    up_cols = column_shares(
+        jnp.concatenate(
+            [
+                grad_query_raw.reshape(rows, devices, query_width // devices),
+                grad_kv.reshape(rows, devices, kv_width // devices),
+            ],
+            axis=2,
+        ).reshape(rows, 1, query_width + kv_width),
+        devices,
+    )[:, 0]
+    query_cols = query_width // devices
+    query_up_cols = rows_product(query_low_all, up_cols[:, :query_cols])
+    latent_up_cols = rows_product(latent_low_all, up_cols[:, query_cols:])
+    grad_h_one = back_product(grad_latent_all, down_latent) + back_product(
+        grad_latent_query, down_query
+    )
+    gain_one_term, grad_input_norm = norm_back(grad_h_one, normed_one, inverse_one, gain_one)
     input_grad = (grad_middle + grad_input_norm).reshape(tokens.shape)
-    attn_sums = [
-        scatter_rows(gain_one_term),
-        scatter_rows(rows_product(h_one, grad_latent_query)),
-        scatter_rows(query_gain_term),
-        scatter_rows(rows_product(query_low, grad_query_raw)),
-        scatter_rows(rows_product(h_one, grad_latent_all)),
-        scatter_rows(latent_gain_term),
-        scatter_rows(rows_product(latent_low, grad_kv)),
-        scatter_rows(rows_product(attended, grad_attn)),
-    ]
+    gain_terms = jnp.concatenate([gain_one_term, query_gain_term, latent_gain_term, gain_two_term])
+    high, low = split_exact(gain_terms)
+    down_grads = jnp.concatenate([grad_latent_all, grad_latent_query], axis=1)
+    grad_width = down_grads.shape[1]
+    gain_rows = -(-(2 * gain_terms.size) // grad_width)
+    gain_block = jnp.pad(
+        jnp.concatenate([high, low]), (0, gain_rows * grad_width - 2 * gain_terms.size)
+    ).reshape(gain_rows, grad_width)
+    last_all = lax.all_gather(
+        jnp.concatenate([down_grads, gain_block], axis=0), AXES, axis=0, tiled=False
+    )
+    down_grads_all = last_all[:, :rows].reshape(devices * rows, grad_width)
+    gain_parts = last_all[:, rows:].reshape(devices, gain_rows * grad_width)[:, : 2 * gain_terms.size]
+    gain_sums = jnp.sum(
+        gain_parts[:, : gain_terms.size].astype(jnp.float32)
+        + gain_parts[:, gain_terms.size :].astype(jnp.float32),
+        axis=0,
+    )
+    latent_width = grad_latent_all.shape[1]
+    latent_down_grad = rows_product(h_one_cols, down_grads_all[:, :latent_width])
+    query_down_grad = rows_product(h_one_cols, down_grads_all[:, latent_width:])
+    up_rows = rows_from_columns(
+        jnp.concatenate(
+            [
+                query_up_cols.reshape(devices, -1),
+                latent_up_cols.reshape(devices, -1),
+            ],
+            axis=1,
+        ).reshape(devices, 1, -1),
+        devices,
+    )
+    q_rows = up_query.shape[0] // devices
+    kv_rows = up_latent.shape[0] // devices
+    kv_cols = kv_width // devices
+    up_rows = up_rows.reshape(devices, -1)
+    query_up_grad = (
+        up_rows[:, : q_rows * query_cols]
+        .reshape(devices, q_rows, query_cols)
+        .transpose(1, 0, 2)
+        .reshape(q_rows, query_width)
+    )
+    latent_up_grad = (
+        up_rows[:, q_rows * query_cols :]
+        .reshape(devices, kv_rows, kv_cols)
+        .transpose(1, 0, 2)
+        .reshape(kv_rows, kv_width)
+    )
+
+    def own(vector, offset, size):
+        share = size // devices
+        return lax.dynamic_slice(vector, (offset + me * share,), (share,))
+
+    d_model = gain_one_term.size
+    attn_gain_grad = own(gain_sums, 0, d_model)
+    query_gain_grad = own(gain_sums, d_model, q_rank)
+    latent_gain_grad = own(gain_sums, d_model + q_rank, kv_rank)
+    feed_gain_grad = own(gain_sums, d_model + q_rank + kv_rank, d_model)
     return (
         output,
         input_grad,
-        attn_sums[0],
-        attn_sums[1],
-        attn_sums[2],
-        attn_sums[3],
-        attn_sums[4],
-        attn_sums[5],
-        attn_sums[6],
-        attn_sums[7],
-        feed_sums[0],
-        feed_sums[1],
-        feed_sums[2],
-        feed_sums[3],
+        attn_gain_grad,
+        query_down_grad,
+        query_gain_grad,
+        query_up_grad,
+        latent_down_grad,
+        latent_gain_grad,
+        latent_up_grad,
+        output_weight_grad,
+        feed_gain_grad,
+        gate_grad,
+        up_grad,
+        down_grad,
     )
 
 

time: 6290 us -> 2170 us (0.34)
  waiting for transfers between devices: 5840 us -> 1540 us
  local copies, waits for them, and re-layouts: 54.9 us -> 264 us
  blocking collectives: 83.3 us -> 0 us
    reduce_scatter x7 -> x0, waiting for transfers between devices: 3670 us -> none  [scatter_rows(): lax.psum_scatter(term, ('fsdp', 'dp'), scatter_dimension=0, tiled=True)]
    unnamed x17 -> x6, waiting for transfers between devices: 1390 us -> 0.76 us
    all_gather x8 -> x6, waiting for transfers between devices: 784 us -> 1200 us  [the longest x1 411 us: local(): lax.all_gather(jnp.stack([h_two, grad_feed]), AXES, axis=1, tiled=True)]
    all_to_all x0 -> x5, waiting for transfers between devices: none -> 340 us  [the longest x3 340 us: column_shares(): moved = lax.all_to_all(blocks, AXES, 2, 0, tiled=True)]
    unnamed x2 -> x0, blocking collectives: 83.3 us -> none
  transfers between devices with their start and end apart: 16 -> 11, of which waited for: 15 -> 8; matrix products, arithmetic and copies ran while one was open for 4% -> 24% of each run, Pallas kernels for 0% -> 0%
where the time goes in v3:
time: 2170 us; the launch traced here: 2160 us
  waiting for transfers between devices  1540 us (71%)
  local copies, waits for them, and re-layouts  264 us (12%)
  matrix products  239 us (11%)
  other arithmetic  59.4 us (3%)
  starting transfers between devices  37.7 us (2%)
    all_gather x1, waiting for transfers between devices, local(): lax.all_gather(jnp.stack([h_two, grad_feed]), AXES, axis=1, tiled=True)  411 us
    all_to_all x3, waiting for transfers between devices, column_shares(): moved = lax.all_to_all(blocks, AXES, 2, 0, tiled=True)  340 us
    all_gather x1, waiting for transfers between devices, local(): lax.all_gather(jnp.concatenate([gate_weight, up_weight], axis=1), AXES, a...  204 us
    all_gather x1, waiting for transfers between devices, gather_packed(): gathered = lax.all_gather(jnp.concatenate(flat), AXES, axis=0, tiled=False)  161 us
    all_gather x1, waiting for transfers between devices, local(): weight_down = lax.all_gather(down_weight, AXES, axis=0, tiled=True)  160 us
    all_gather x1, waiting for transfers between devices, local(): lax.all_gather(jnp.concatenate([down_grads, gain_block], axis=0), AXES, a...  154 us
    all_gather x1, waiting for transfers between devices, gather_tokens(): return lax.all_gather(values, AXES, axis=0, tiled=True)  113 us
    dot_general x7, matrix products, rows_product(): lax.dot_general(left, right, (((0,), (0,)), ((), ())), preferred_element_...  82.9 us
  transfers between devices with their start and end apart: 11, of which 8 were waited for; matrix products, arithmetic and copies ran while one was open for 24% of the time, Pallas kernels for 0%

profile of v3, /device:TPU:0, one launch (start us, length us, event | category | flops | bytes accessed | tf_op | source)
XLA Modules:
  0.0 2159.4 jit_solution(6513888739489658642)
XLA Ops:
  27.7 160.9 %all-gather.18.cloned.1.call-done = bf16[13533184]{0:T(1024)(128)(2,1)} async-done(((bf16[422912]{0:T(1024)(128)(2,1)}), bf16[13533184]{0:T(1024)(128)(2,1)}) %all-gather.18.cloned.1.call-update) | async-done | bytes 27066384 | tf_op jit(solution)/shard_map/all_gather | solution.py:77
  188.5 35.5 %reshape.481 = bf16[32,422912]{1,0:T(8,128)(2,1)} reshape(bf16[13533184]{0:T(1024)(128)(2,1)} %all-gather.18.cloned.1.call-done) | data formatting | bytes 54132736 | tf_op jit(solution)/shard_map/all_gather | solution.py:77
  260.4 7.0 reshape.449
  267.4 8.5 copy.162
  301.6 10.7 slice.220
  312.3 12.5 reshape.451
  324.9 9.6 multiply_reduce_fusion.5
  334.5 203.7 %all-gather.10.cloned.1.call-done = bf16[2560,12800]{1,0:T(8,128)(2,1)} async-done(((bf16[80,12800]{1,0:T(8,128)(2,1)}), bf16[2560,12800]{1,0:T(8,128)(2,1)}) %all-gather.10.cloned.1.call-update) | async-done | bytes 65536016 | tf_op jit(solution)/shard_map/all_gather | solution.py:156
  538.3 31.1 %fusion.67 = f32[256,12800]{1,0:T(8,128)} fusion(bf16[2560,12800]{1,0:T(8,128)(2,1)} %all-gather.10.cloned.1.call-done, f32[256,2560]{1,0:T(8,128)S(1)} %get-tuple-element.125, f32[2560]{0:T(1024)S(1)} %reshape.476, f32[256]{0:T(256)S(1)} %add_rsqrt_fusion), kind=kOutput, calls=%fused_computation.163 | convolution fusion | flops 16779182080 | bytes 81275904 | tf_op jit(solution)/shard_map/dot_general | solution.py:23
  569.4 160.3 %all-gather.12.cloned.1.call-done = bf16[6400,2560]{1,0:T(8,128)(2,1)} async-done(((bf16[200,2560]{1,0:T(8,128)(2,1)}), bf16[6400,2560]{1,0:T(8,128)(2,1)}) %all-gather.12.cloned.1.call-update) | async-done | bytes 32768016 | tf_op jit(solution)/shard_map/all_gather | solution.py:159
  729.7 21.6 multiply_convert_fusion.1
  751.3 28.7 %fusion.9 = f32[256,2560]{1,0:T(8,128)} fusion(bf16[2560,12800]{1,0:T(8,128)(2,1)} %all-gather.10.cloned.1.call-done, bf16[256,6400]{1,0:T(8,128)(2,1)} %get-tuple-element.97, bf16[256,6400]{1,0:T(8,128)(2,1)} %get-tuple-element.96), kind=kOutput, calls=%fused_computation.13 | convolution fusion | flops 16790323200 | bytes 74711040 | tf_op jit(solution)/shard_map/dot_general | solution.py:33
  790.8 8.5 convolution_convert_fusion
  874.1 8.0 maximum_bitcast_fusion.1
  882.1 8.4 copy.195
  897.3 6.7 maximum_bitcast_fusion
  904.0 64.4 %all-to-all-done.1 = bf16[256,1,32,280]{0,3,1,2:T(8,128)(2,1)} async-done(((bf16[256,1,32,280]{0,3,1,2:T(8,128)(2,1)}), bf16[256,1,32,280]{0,3,1,2:T(8,128)(2,1)}, u32[]{:S(2)}, u32[]{:S(2)}) %all-to-all-start.1) | async-done | bytes 4587552 | tf_op jit(solution)/shard_map/all_to_all | solution.py:95
  968.3 8.6 all-to-all-start.3
  997.8 275.3 %all-to-all-done.3 = bf16[256,1,32,680]{0,3,1,2:T(8,128)(2,1)} async-done(((bf16[256,1,32,680]{0,3,1,2:T(8,128)(2,1)}), bf16[256,1,32,680]{0,3,1,2:T(8,128)(2,1)}, u32[]{:S(2)}, u32[]{:S(2)}) %all-to-all-start.3) | async-done | bytes 11141152 | tf_op jit(solution)/shard_map/all_to_all | solution.py:95
  1273.1 13.7 all-to-all-start
  1286.8 10.4 copy.227
  1297.3 112.8 %all-gather.14.cloned.1.call-done = bf16[8192,3584]{0,1:T(8,128)(2,1)} async-done(((bf16[256,3584]{0,1:T(8,128)(2,1)}), bf16[8192,3584]{0,1:T(8,128)(2,1)}) %all-gather.14.cloned.1.call-update) | async-done | bytes 58720272 | tf_op jit(solution)/shard_map/all_gather | solution.py:89
  1414.6 7.0 fusion.4
  1423.2 22.3 %fusion.1 = f32[2560,80]{0,1:T(8,128)} fusion(bf16[8192,3584]{0,1:T(8,128)(2,1)} %all-gather.14.cloned.1.call-done, bf16[8192,680]{0,1:T(8,128)(2,1)} %bitcast.215), kind=kOutput, calls=%fused_computation.2 | convolution fusion | flops 3355443200 | bytes 44072960 | tf_op jit(solution)/shard_map/dot_general | solution.py:27
  1445.5 7.8 all-to-all-start.2
  1453.3 411.5 %all-gather.16.cloned.1.call-done = bf16[2,8192,2560]{2,1,0:T(8,128)(2,1)} async-done(((bf16[2,256,2560]{2,1,0:T(8,128)(2,1)}), bf16[2,8192,2560]{2,1,0:T(8,128)(2,1)}) %all-gather.16.cloned.1.call-update) | async-done | bytes 83886096 | tf_op jit(solution)/shard_map/all_gather | solution.py:220
  1864.8 23.4 %fusion.3 = f32[2560,400]{0,1:T(8,128)S(1)} fusion(bf16[2,8192,2560]{2,1,0:T(8,128)(2,1)} %all-gather.16.cloned.1.call-done, bf16[8192,680]{0,1:T(8,128)(2,1)} %bitcast.216), kind=kOutput, calls=%fused_computation.5 | convolution fusion | flops 16777216000 | bytes 52592640 | tf_op jit(solution)/shard_map/dot_general | solution.py:27
  1890.7 11.8 copy.199
  1912.7 16.6 fusion.22
  1929.3 153.6 %all-gather.20.cloned.1.call-done = bf16[32,268,1056]{2,1,0:T(8,128)(2,1)} async-done(((bf16[1,268,1056]{2,1,0:T(8,128)(2,1)}), bf16[32,268,1056]{2,1,0:T(8,128)(2,1)}) %all-gather.20.cloned.1.call-update) | async-done | bytes 18112528 | tf_op jit(solution)/shard_map/all_gather | solution.py:325
  2086.4 10.7 slice.234
  2106.9 19.4 fusion
  (307 shorter events, 252.6 us)
Async XLA Ops:
  7.2 181.3 %all-gather.18.cloned.1.call-start = ((), (), s32[]{:S(2)}) async-start(), calls=%async_computation.9 | async-start | bytes 27912192 | tf_op jit(solution)/shard_map/all_gather | solution.py:77
  22.6 515.7 %all-gather.10.cloned.1.call-start = ((), (), s32[]{:S(2)}) async-start(), calls=%async_computation.5 | async-start | bytes 67584000 | tf_op jit(solution)/shard_map/all_gather | solution.py:156
  25.7 704.0 %all-gather.12.cloned.1.call-start = ((), (), s32[]{:S(2)}) async-start(), calls=%async_computation.6 | async-start | bytes 33792000 | tf_op jit(solution)/shard_map/all_gather | solution.py:159
  26.4 1383.7 %all-gather.14.cloned.1.call-start = ((), (), s32[]{:S(2)}) async-start(), calls=%async_computation.7 | async-start | bytes 60555264 | tf_op jit(solution)/shard_map/all_gather | solution.py:89
  27.5 258.7 %copy-start.35 = (f32[128,16]{0,1:T(8,128)}, f32[128,16]{0,1:T(8,128)S(1)}, u32[]{:S(2)}) copy-start(f32[128,16]{0,1:T(8,128)S(1)} %get-tuple-element.118) | copy-start | bytes 24580
  27.5 258.7 %copy-start.37 = (f32[128,16]{0,1:T(8,128)}, f32[128,16]{0,1:T(8,128)S(1)}, u32[]{:S(2)}) copy-start(f32[128,16]{0,1:T(8,128)S(1)} %get-tuple-element.119) | copy-start | bytes 24580
  228.4 6.5 slice-start
  252.3 38.1 %copy-start.12 = (bf16[2,128,40,128]{1,3,2,0:T(8,128)(2,1)}, bf16[2,128,40,128]{1,3,2,0:T(8,128)(2,1)S(1)}, u32[]{:S(2)}) copy-start(bf16[2,128,40,128]{1,3,2,0:T(8,128)(2,1)S(1)} %convolution_convert_fusion.1) | copy-start | bytes 7864324
  260.4 19.2 copy-start.47
  279.7 6.2 copy-start.57
  296.2 1568.5 %all-gather.16.cloned.1.call-start = ((), (), s32[]{:S(2)}) async-start(), calls=%async_computation.8 | async-start | bytes 86507520 | tf_op jit(solution)/shard_map/all_gather | solution.py:220
  298.7 486.3 %copy-start.51 = (f32[256]{0:T(256)}, f32[256]{0:T(256)S(1)}, u32[]{:S(2)}) copy-start(f32[256]{0:T(256)S(1)} %fusion.59) | copy-start | bytes 3076
  334.5 450.5 %copy-start.5 = (f32[256,2560]{1,0:T(8,128)}, f32[256,2560]{1,0:T(8,128)S(1)}, u32[]{:S(2)}) copy-start(f32[256,2560]{1,0:T(8,128)S(1)} %get-tuple-element.125) | copy-start | bytes 7864324
  801.9 9.3 slice-start.2
  806.3 4.9 slice-start.3
  842.9 125.4 %all-to-all-start.1 = ((bf16[256,1,32,280]{0,3,1,2:T(8,128)(2,1)}), bf16[256,1,32,280]{0,3,1,2:T(8,128)(2,1)}, u32[]{:S(2)}, u32[]{:S(2)}) async-start(bf16[256,1,32,280]{0,3,1,2:T(8,128)(2,1)} %maximum_bitcast_fusion.3), calls=%async_computation.1 | async-start | bytes 9175040 | tf_op jit(solution)/shard_map/all_to_all | solution.py:95
  856.3 7.1 copy-start.54
  856.3 7.1 copy-start.56
  863.4 4.4 copy-start.44
  882.1 8.4 copy-start.14
  882.1 8.4 copy-start.26
  882.1 8.4 copy-start.48
  882.1 8.4 copy-start.58
  890.5 6.3 copy-start.4
  968.3 304.8 %all-to-all-start.3 = ((bf16[256,1,32,680]{0,3,1,2:T(8,128)(2,1)}), bf16[256,1,32,680]{0,3,1,2:T(8,128)(2,1)}, u32[]{:S(2)}, u32[]{:S(2)}) async-start(bf16[256,1,32,680]{0,3,1,2:T(8,128)(2,1)} %maximum_bitcast_fusion), calls=%async_computation.3 | async-start | bytes 22282240 | tf_op jit(solution)/shard_map/all_to_all | solution.py:95
  976.9 1106.0 %all-gather.20.cloned.1.call-start = ((), (), s32[]{:S(2)}) async-start(), calls=%async_computation.10 | async-start | bytes 20680704 | tf_op jit(solution)/shard_map/all_gather | solution.py:325
  1273.1 172.4 %all-to-all-start = ((bf16[256,1,32,80]{0,3,1,2:T(8,128)(2,1)}), bf16[256,1,32,80]{0,3,1,2:T(8,128)(2,1)S(1)}, u32[]{:S(2)}, u32[]{:S(2)}) async-start(bf16[256,1,32,80]{0,3,1,2:T(8,128)(2,1)} %fusion.43), calls=%async_computation | async-start | bytes 2621440 | tf_op jit(solution)/shard_map/all_to_all | solution.py:95
  1445.5 457.0 %all-to-all-start.2 = ((f32[32,1,4160]{2,1,0:T(1,128)}), f32[32,1,4160]{2,1,0:T(1,128)S(1)}, u32[]{:S(2)}, u32[]{:S(2)}) async-start(f32[32,1,4160]{2,1,0:T(1,128)} %copy.189), calls=%async_computation.2 | async-start | bytes 1081344 | tf_op jit(solution)/shard_map/all_to_all | solution.py:101
  1864.8 23.4 %copy-start.34 = (f32[2560,80]{0,1:T(8,128)S(1)}, f32[2560,80]{0,1:T(8,128)}, u32[]{:S(2)}) copy-start(f32[2560,80]{0,1:T(8,128)} %fusion.1) | copy-start | bytes 2457604
  1902.4 223.9 %all-to-all-start.4 = ((f32[2560,1,480]{2,1,0:T(1,128)}), f32[2560,1,480]{2,1,0:T(1,128)}, u32[]{:S(2)}, u32[]{:S(2)}) async-start(f32[2560,1,480]{2,1,0:T(1,128)} %copy.199), calls=%async_computation.4 | async-start | bytes 10485760 | tf_op jit(solution)/shard_map/all_to_all | solution.py:101
  1908.5 4.2 copy-start.52
  2086.4 11.3 copy-start.32
  (47 other events, 122.7 us)
Sparse Core Ops, SparseCore 0:
  22.7 165.7 all-gather.17
  191.9 346.2 all-gather.9
  541.1 188.5 all-gather.11
  731.0 679.0 all-gather.13
  1412.9 451.8 all-gather.15
  1868.0 214.8 all-gather.19

commit v4 on v3

--- a/solution.py
+++ b/solution.py
@@ -204,7 +204,6 @@
     query_low_all = latents_all[:, :q_rank]
     latent_low_all = latents_all[:, q_rank : q_rank + kv_rank]
     attended_all = latents_all[:, q_rank + kv_rank :]
-    h_one_cols = column_shares(h_one[:, None, :], devices)[:, 0]
     middle = inputs + depth_scale * matmul(attended, weight_out)
     normed_two, inverse_two = normalize(middle)
     h_two = (normed_two * gain_two.astype(jnp.float32)).astype(jnp.bfloat16)
@@ -229,22 +228,22 @@
     grad_attn = (depth_scale * grad_middle).astype(jnp.bfloat16)
     ff_share = ffn // devices
     attn_share = width // devices
-    feed_cols = column_shares(
-        jnp.concatenate(
-            [
-                jnp.stack([hidden, grad_gate, grad_up], axis=1)
-                .reshape(rows, 3, devices, ff_share)
-                .transpose(0, 2, 1, 3)
-                .reshape(rows, devices, 3 * ff_share),
-                grad_attn.reshape(rows, devices, attn_share),
-            ],
-            axis=2,
-        ).reshape(rows, 1, devices * (3 * ff_share + attn_share)),
-        devices,
-    )[:, 0]
-    down_grad = rows_product(feed_cols[:, :ff_share], grad_feed_all)
-    gate_up_cols = rows_product(h_two_all, feed_cols[:, ff_share : 3 * ff_share])
-    out_cols = rows_product(attended_all, feed_cols[:, 3 * ff_share :])
+    gate_c = matmul(h_two_all, lax.dynamic_slice_in_dim(weight_gate_up, me * ff_share, ff_share, 1))
+    up_c = matmul(
+        h_two_all, lax.dynamic_slice_in_dim(weight_gate_up, ffn + me * ff_share, ff_share, 1)
+    )
+    sigma_c = jax.nn.sigmoid(gate_c)
+    hidden_c = (gate_c * sigma_c * up_c).astype(jnp.bfloat16)
+    grad_hidden_c = back_product(grad_feed_all, down_weight)
+    grad_gate_c = (grad_hidden_c * up_c * sigma_c * (1.0 + gate_c * (1.0 - sigma_c))).astype(
+        jnp.bfloat16
+    )
+    grad_up_c = (grad_hidden_c * gate_c * sigma_c).astype(jnp.bfloat16)
+    down_grad = rows_product(hidden_c, grad_feed_all)
+    gate_up_cols = rows_product(h_two_all, jnp.concatenate([grad_gate_c, grad_up_c], axis=1))
+    inner_cols = column_shares(jnp.stack([h_one, grad_attn], axis=1), devices)
+    h_one_cols = inner_cols[:, 0]
+    out_cols = rows_product(attended_all, inner_cols[:, 1])
     wide_rows = rows_from_columns(
         jnp.concatenate([gate_up_cols, out_cols], axis=1)[:, None, :], devices
     ).reshape(width // devices, devices, 2 * ff_share + attn_share)

time: 2170 us -> 1930 us (0.89)
  waiting for transfers between devices: 1540 us -> 1250 us
  matrix products: 239 us -> 332 us
  local copies, waits for them, and re-layouts: 264 us -> 241 us
    all_to_all x3 -> x2, waiting for transfers between devices: 340 us -> 154 us  [column_shares(): moved = lax.all_to_all(blocks, AXES, 2, 0, tiled=True)]
    all_gather x1, waiting for transfers between devices: 154 us -> 0.01 us  [local(): lax.all_gather(jnp.concatenate([down_grads, gain_block], axis=0), AXES, a...]
    dot_general x7 -> x9, matrix products: 68.8 us -> 139 us  [matmul(): return jnp.dot(left, right, preferred_element_type=jnp.float32)]
    all_to_all x2, waiting for transfers between devices: 0.01 us -> 43.1 us  [rows_from_columns(): moved = lax.all_to_all(grad, AXES, 0, 2, tiled=True)]
    dot_general x7 -> x8, matrix products: 75.1 us -> 94.9 us  [back_product(): lax.dot_general(left, right, (((1,), (1,)), ((), ())), preferred_element_...]
  transfers between devices with their start and end apart: 11 -> 10, of which waited for: 8 -> 8; matrix products, arithmetic and copies ran while one was open for 24% -> 30% of each run, Pallas kernels for 0% -> 0%
where the time goes in v4:
time: 1930 us; the launch traced here: 1920 us
  waiting for transfers between devices  1250 us (65%)
  matrix products  332 us (17%)
  local copies, waits for them, and re-layouts  241 us (12%)
  other arithmetic  59.1 us (3%)
  starting transfers between devices  24.6 us (1%)
    all_gather x1, waiting for transfers between devices, local(): lax.all_gather(jnp.stack([h_two, grad_feed]), AXES, axis=1, tiled=True)  413 us
    all_gather x1, waiting for transfers between devices, local(): lax.all_gather(jnp.concatenate([gate_weight, up_weight], axis=1), AXES, a...  188 us
    all_gather x1, waiting for transfers between devices, local(): weight_down = lax.all_gather(down_weight, AXES, axis=0, tiled=True)  161 us
    all_gather x1, waiting for transfers between devices, gather_packed(): gathered = lax.all_gather(jnp.concatenate(flat), AXES, axis=0, tiled=False)  160 us
    all_to_all x2, waiting for transfers between devices, column_shares(): moved = lax.all_to_all(blocks, AXES, 2, 0, tiled=True)  154 us
    dot_general x9, matrix products, matmul(): return jnp.dot(left, right, preferred_element_type=jnp.float32)  139 us
    all_gather x1, waiting for transfers between devices, gather_tokens(): return lax.all_gather(values, AXES, axis=0, tiled=True)  127 us
    dot_general x8, matrix products, back_product(): lax.dot_general(left, right, (((1,), (1,)), ((), ())), preferred_element_...  94.9 us
  transfers between devices with their start and end apart: 10, of which 8 were waited for; matrix products, arithmetic and copies ran while one was open for 30% of the time, Pallas kernels for 0%

profile of v4, /device:TPU:0, one launch (start us, length us, event | category | flops | bytes accessed | tf_op | source)
XLA Modules:
  0.0 1919.1 jit_solution(14374721879641303215)
XLA Ops:
  28.3 160.2 %all-gather.18.cloned.1.call-done = bf16[13533184]{0:T(1024)(128)(2,1)} async-done(((bf16[422912]{0:T(1024)(128)(2,1)}), bf16[13533184]{0:T(1024)(128)(2,1)}) %all-gather.18.cloned.1.call-update) | async-done | bytes 27066384 | tf_op jit(solution)/shard_map/all_gather | solution.py:77
  188.5 35.7 %reshape.476 = bf16[32,422912]{1,0:T(8,128)(2,1)} reshape(bf16[13533184]{0:T(1024)(128)(2,1)} %all-gather.18.cloned.1.call-done) | data formatting | bytes 54132736 | tf_op jit(solution)/shard_map/all_gather | solution.py:77
  262.7 7.0 reshape.445
  269.7 8.5 copy.110
  283.1 15.8 fusion.82
  315.5 10.9 slice.216
  326.4 12.3 reshape.447
  338.8 11.0 multiply_reduce_fusion.5
  349.8 188.4 %all-gather.10.cloned.1.call-done = bf16[2560,12800]{1,0:T(8,128)(2,1)} async-done(((bf16[80,12800]{1,0:T(8,128)(2,1)}), bf16[2560,12800]{1,0:T(8,128)(2,1)}) %all-gather.10.cloned.1.call-update) | async-done | bytes 65536016 | tf_op jit(solution)/shard_map/all_gather | solution.py:156
  538.3 30.4 %fusion.76 = f32[256,12800]{1,0:T(8,128)} fusion(bf16[2560,12800]{1,0:T(8,128)(2,1)} %all-gather.10.cloned.1.call-done, f32[256,2560]{1,0:T(8,128)} %get-tuple-element.112, f32[2560]{0:T(1024)S(1)} %reshape.471, f32[256]{0:T(256)S(1)} %add_rsqrt_fusion), kind=kOutput, calls=%fused_computation.177 | convolution fusion | flops 16779182080 | bytes 81275904 | tf_op jit(solution)/shard_map/dot_general | solution.py:23
  568.7 161.0 %all-gather.12.cloned.1.call-done = bf16[6400,2560]{1,0:T(8,128)(2,1)} async-done(((bf16[200,2560]{1,0:T(8,128)(2,1)}), bf16[6400,2560]{1,0:T(8,128)(2,1)}) %all-gather.12.cloned.1.call-update) | async-done | bytes 32768016 | tf_op jit(solution)/shard_map/all_gather | solution.py:159
  729.7 20.9 %multiply_convert_fusion.4 = (bf16[256,6400]{1,0:T(8,128)(2,1)}, bf16[256,6400]{1,0:T(8,128)(2,1)}) fusion(f32[256,12800]{1,0:T(8,128)} %fusion.76, bf16[256,2560]{1,0:T(8,128)(2,1)} %multiply_convert_fusion.12, bf16[6400,2560]{1,0:T(8,128)(2,1)} %all-gather.12.cloned.1.call-done), kind=kOutput, calls=%fused_computation.25 | convolution fusion | flops 8409907200 | bytes 53739520 | tf_op jit(solution)/shard_map/dot_general | solution.py:33
  750.6 29.0 %fusion.11 = f32[256,2560]{1,0:T(8,128)} fusion(bf16[2560,12800]{1,0:T(8,128)(2,1)} %all-gather.10.cloned.1.call-done, bf16[256,6400]{1,0:T(8,128)(2,1)} %get-tuple-element.83, bf16[256,6400]{1,0:T(8,128)(2,1)} %get-tuple-element.82), kind=kOutput, calls=%fused_computation.13 | convolution fusion | flops 16790323200 | bytes 74711040 | tf_op jit(solution)/shard_map/dot_general | solution.py:33
  787.9 6.4 multiply_convert_fusion.10
  801.6 9.9 convolution_convert_fusion
  853.1 6.9 pad_maximum_fusion
  896.9 38.4 %all-to-all-done = bf16[256,2,32,80]{0,1,3,2:T(2,128)(2,1)} async-done(((bf16[256,2,32,80]{0,1,3,2:T(2,128)(2,1)}), bf16[256,2,32,80]{0,1,3,2:T(2,128)(2,1)}, u32[]{:S(2)}, u32[]{:S(2)}) %all-to-all-start) | async-done | bytes 2621472 | tf_op jit(solution)/shard_map/all_to_all | solution.py:95
  947.3 115.4 %all-to-all-done.1 = bf16[256,1,32,280]{0,3,1,2:T(8,128)(2,1)} async-done(((bf16[256,1,32,280]{0,3,1,2:T(8,128)(2,1)}), bf16[256,1,32,280]{0,3,1,2:T(8,128)(2,1)}, u32[]{:S(2)}, u32[]{:S(2)}) %all-to-all-start.1) | async-done | bytes 4587552 | tf_op jit(solution)/shard_map/all_to_all | solution.py:95
  1067.8 126.9 %all-gather.14.cloned.1.call-done = bf16[8192,3584]{0,1:T(8,128)(2,1)} async-done(((bf16[256,3584]{0,1:T(8,128)(2,1)}), bf16[8192,3584]{0,1:T(8,128)(2,1)}) %all-gather.14.cloned.1.call-update) | async-done | bytes 58720272 | tf_op jit(solution)/shard_map/all_gather | solution.py:89
  1199.1 7.0 fusion.7
  1207.7 9.5 all-to-all-start.2
  1217.3 19.0 fusion
  1236.2 412.7 %all-gather.16.cloned.1.call-done = bf16[2,8192,2560]{2,1,0:T(8,128)(2,1)} async-done(((bf16[2,256,2560]{2,1,0:T(8,128)(2,1)}), bf16[2,8192,2560]{2,1,0:T(8,128)(2,1)}) %all-gather.16.cloned.1.call-update) | async-done | bytes 83886096 | tf_op jit(solution)/shard_map/all_gather | solution.py:219
  1648.9 21.4 %fusion.3 = f32[8192,200]{0,1:T(8,128)} fusion(bf16[200,2560]{1,0:T(8,128)(2,1)} %param.28, bf16[2,8192,2560]{2,1,0:T(8,128)(2,1)} %all-gather.16.cloned.1.call-done), kind=kOutput, calls=%fused_computation.5 | convolution fusion | flops 8388608000 | bytes 49520640 | tf_op jit(solution)/shard_map/dot_general | solution.py:33
  1670.3 22.4 %fusion.6 = f32[8192,200]{0,1:T(8,128)} fusion(bf16[2,8192,2560]{2,1,0:T(8,128)(2,1)} %all-gather.16.cloned.1.call-done, bf16[2560,12800]{1,0:T(8,128)(2,1)} %all-gather.10.cloned.1.call-done, s32[]{:T(128)S(6)} %select_n.26), kind=kOutput, calls=%fused_computation.8 | convolution fusion | flops 8388608000 | bytes 49807364 | tf_op jit(solution)/shard_map/dot_general | solution.py:23
  1692.7 27.2 %multiply_convert_fusion.2 = (bf16[8192,200]{0,1:T(8,128)(2,1)}, bf16[8192,200]{0,1:T(8,128)(2,1)}, f32[8192,200]{0,1:T(8,128)}) fusion(f32[8192,200]{0,1:T(8,128)} %fusion.3, f32[8192,200]{0,1:T(8,128)} %fusion.6, bf16[2560,12800]{1,0:T(8,128)(2,1)} %all-gather.10.cloned.1.call-done, s32[]{:T(128)S(6)} %select_n.27, ...), kind=kOutput, calls=%fused_computation.22 | convolution fusion | flops 8409907200 | bytes 69468160 | tf_op jit(solution)/shard_map/dot_general | solution.py:23
  1719.9 27.4 %fusion.4 = f32[2560,400]{0,1:T(8,128)S(1)} fusion(bf16[2,8192,2560]{2,1,0:T(8,128)(2,1)} %all-gather.16.cloned.1.call-done, bf16[8192,200]{0,1:T(8,128)(2,1)} %get-tuple-element.85, bf16[8192,200]{0,1:T(8,128)(2,1)} %get-tuple-element.84), kind=kOutput, calls=%fused_computation.6 | convolution fusion | flops 16790323200 | bytes 52592640 | tf_op jit(solution)/shard_map/dot_general | solution.py:27
  1749.9 11.7 copy.140
  1771.5 24.6 %fusion.27 = bf16[256,2560]{1,0:T(8,128)(2,1)} fusion(f32[256,2560]{1,0:T(8,128)} %get-tuple-element.112, bf16[6400,2560]{1,0:T(8,128)(2,1)} %all-gather.12.cloned.1.call-done, f32[256,12800]{1,0:T(8,128)} %fusion.76, f32[256]{0:T(256)S(1)} %copy-done.53), kind=kOutput, calls=%fused_computation.52 | convolution fusion | flops 8401059840 | bytes 49808384 | tf_op jit(solution)/shard_map/dot_general | solution.py:23
  1799.7 11.2 slice.231
  1820.6 22.6 %fusion.2 = f32[200,2560]{1,0:T(8,128)} fusion(bf16[2,8192,2560]{2,1,0:T(8,128)(2,1)} %all-gather.16.cloned.1.call-done, f32[8192,200]{0,1:T(8,128)} %fusion.6, f32[8192,200]{0,1:T(8,128)} %get-tuple-element.118), kind=kOutput, calls=%fused_computation.4 | convolution fusion | flops 8398438400 | bytes 57098240 | tf_op jit(solution)/shard_map/dot_general | solution.py:27
  1843.1 43.1 %all-to-all-done.3 = f32[2560,1,480]{2,1,0:T(1,128)} async-done(((f32[2560,1,480]{2,1,0:T(1,128)}), f32[2560,1,480]{2,1,0:T(1,128)}, u32[]{:S(2)}, u32[]{:S(2)}) %all-to-all-start.3) | async-done | bytes 4915232 | tf_op jit(solution)/shard_map/all_to_all | solution.py:101
  (304 shorter events, 248.7 us)
Async XLA Ops:
  7.2 181.3 %all-gather.18.cloned.1.call-start = ((), (), s32[]{:S(2)}) async-start(), calls=%async_computation.8 | async-start | bytes 27912192 | tf_op jit(solution)/shard_map/all_gather | solution.py:77
  22.6 515.7 %all-gather.10.cloned.1.call-start = ((), (), s32[]{:S(2)}) async-start(), calls=%async_computation.4 | async-start | bytes 67584000 | tf_op jit(solution)/shard_map/all_gather | solution.py:156
  25.7 704.0 %all-gather.12.cloned.1.call-start = ((), (), s32[]{:S(2)}) async-start(), calls=%async_computation.5 | async-start | bytes 33792000 | tf_op jit(solution)/shard_map/all_gather | solution.py:159
  26.4 1168.2 %all-gather.14.cloned.1.call-start = ((), (), s32[]{:S(2)}) async-start(), calls=%async_computation.6 | async-start | bytes 60555264 | tf_op jit(solution)/shard_map/all_gather | solution.py:89
  27.6 272.1 %copy-start.36 = (f32[128,16]{0,1:T(8,128)}, f32[128,16]{0,1:T(8,128)S(1)}, u32[]{:S(2)}) copy-start(f32[128,16]{0,1:T(8,128)S(1)} %get-tuple-element.105) | copy-start | bytes 24580
  27.6 272.1 %copy-start.38 = (f32[128,16]{0,1:T(8,128)}, f32[128,16]{0,1:T(8,128)S(1)}, u32[]{:S(2)}) copy-start(f32[128,16]{0,1:T(8,128)S(1)} %get-tuple-element.106) | copy-start | bytes 24580
  228.5 7.1 slice-start
  239.6 5.3 slice-start.1
  242.1 5.5 copy-start.22
  254.6 48.5 %copy-start.13 = (bf16[2,128,40,128]{1,3,2,0:T(8,128)(2,1)}, bf16[2,128,40,128]{1,3,2,0:T(8,128)(2,1)S(1)}, u32[]{:S(2)}) copy-start(bf16[2,128,40,128]{1,3,2,0:T(8,128)(2,1)S(1)} %convolution_convert_fusion.1) | copy-start | bytes 7864324
  262.7 19.3 %copy-start.47 = (f32[768]{0:T(1024)}, f32[768]{0:T(1024)S(1)}, u32[]{:S(2)}) copy-start(f32[768]{0:T(1024)S(1)} %reshape.469) | copy-start | bytes 9220
  308.8 1340.1 %all-gather.16.cloned.1.call-start = ((), (), s32[]{:S(2)}) async-start(), calls=%async_computation.7 | async-start | bytes 86507520 | tf_op jit(solution)/shard_map/all_gather | solution.py:219
  311.3 483.1 %copy-start.52 = (f32[256]{0:T(256)}, f32[256]{0:T(256)S(1)}, u32[]{:S(2)}) copy-start(f32[256]{0:T(256)S(1)} %fusion.63) | copy-start | bytes 3076
  326.4 12.3 copy-start.46
  787.9 6.5 copy-start.4
  787.9 6.5 copy-start.11
  815.8 10.0 slice-start.2
  820.9 5.0 slice-start.3
  860.0 75.3 %all-to-all-start = ((bf16[256,2,32,80]{0,1,3,2:T(2,128)(2,1)}), bf16[256,2,32,80]{0,1,3,2:T(2,128)(2,1)}, u32[]{:S(2)}, u32[]{:S(2)}) async-start(bf16[256,2,32,80]{0,1,3,2:T(2,128)(2,1)} %pad_maximum_fusion), calls=%async_computation | async-start | bytes 5242880 | tf_op jit(solution)/shard_map/all_to_all | solution.py:95
  864.2 932.0 %all-gather.20.cloned.1.call-start = ((), (), s32[]{:S(2)}) async-start(), calls=%async_computation.9 | async-start | bytes 20680704 | tf_op jit(solution)/shard_map/all_gather | solution.py:324
  864.2 5.7 copy-start.8
  882.9 5.7 copy-start.14
  935.3 127.4 %all-to-all-start.1 = ((bf16[256,1,32,280]{0,3,1,2:T(8,128)(2,1)}), bf16[256,1,32,280]{0,3,1,2:T(8,128)(2,1)}, u32[]{:S(2)}, u32[]{:S(2)}) async-start(bf16[256,1,32,280]{0,3,1,2:T(8,128)(2,1)} %maximum_bitcast_fusion.1), calls=%async_computation.1 | async-start | bytes 9175040 | tf_op jit(solution)/shard_map/all_to_all | solution.py:95
  1206.1 11.2 copy-start.28
  1207.7 553.9 %all-to-all-start.2 = ((f32[32,1,4160]{2,1,0:T(1,128)}), f32[32,1,4160]{2,1,0:T(1,128)S(1)}, u32[]{:S(2)}, u32[]{:S(2)}) async-start(f32[32,1,4160]{2,1,0:T(1,128)} %copy.137), calls=%async_computation.2 | async-start | bytes 1081344 | tf_op jit(solution)/shard_map/all_to_all | solution.py:101
  1719.9 27.4 %copy-start.35 = (f32[2560,80]{0,1:T(8,128)S(1)}, f32[2560,80]{0,1:T(8,128)}, u32[]{:S(2)}) copy-start(f32[2560,80]{0,1:T(8,128)} %fusion) | copy-start | bytes 2457604
  1761.6 5.1 copy-start.60
  1761.6 5.1 copy-start.3
  1761.6 5.1 copy-start.42
  1761.6 5.1 copy-start.51
  1761.6 124.7 %all-to-all-start.3 = ((f32[2560,1,480]{2,1,0:T(1,128)}), f32[2560,1,480]{2,1,0:T(1,128)}, u32[]{:S(2)}, u32[]{:S(2)}) async-start(f32[2560,1,480]{2,1,0:T(1,128)} %copy.140), calls=%async_computation.3 | async-start | bytes 10485760 | tf_op jit(solution)/shard_map/all_to_all | solution.py:101
  1799.7 11.8 copy-start.29
  (46 other events, 115.7 us)
Sparse Core Ops, SparseCore 0:
  22.7 165.7 all-gather.17
  191.9 346.2 all-gather.9
  541.1 188.5 all-gather.11
  731.6 462.9 all-gather.13
  1197.4 451.4 all-gather.15
  1651.6 135.0 all-gather.19

commit v5 on v4

--- a/solution.py
+++ b/solution.py
@@ -200,10 +200,7 @@
     attended = attended.reshape(rows, HEADS * VDIM).astype(jnp.bfloat16)
     q_rank = query_low.shape[1]
     kv_rank = latent_low.shape[1]
-    latents_all = gather_tokens(jnp.concatenate([query_low, latent_low, attended], axis=1))
-    query_low_all = latents_all[:, :q_rank]
-    latent_low_all = latents_all[:, q_rank : q_rank + kv_rank]
-    attended_all = latents_all[:, q_rank + kv_rank :]
+    latent_src = jnp.concatenate([query_low, latent_low, attended], axis=1)
     middle = inputs + depth_scale * matmul(attended, weight_out)
     normed_two, inverse_two = normalize(middle)
     h_two = (normed_two * gain_two.astype(jnp.float32)).astype(jnp.bfloat16)
@@ -217,6 +214,11 @@
     grad_out = cotangent.reshape(rows, width).astype(jnp.float32) * valid_rows
     grad_feed = (depth_scale * grad_out).astype(jnp.bfloat16)
     feed_all = lax.all_gather(jnp.stack([h_two, grad_feed]), AXES, axis=1, tiled=True)
+    latent_src, feed_all = lax.optimization_barrier((latent_src, feed_all))
+    latents_all = gather_tokens(latent_src)
+    query_low_all = latents_all[:, :q_rank]
+    latent_low_all = latents_all[:, q_rank : q_rank + kv_rank]
+    attended_all = latents_all[:, q_rank + kv_rank :]
     h_two_all = feed_all[0]
     grad_feed_all = feed_all[1]
     grad_hidden = back_product(grad_feed, weight_down)

time: 1930 us -> 2000 us (1.036)
  waiting for transfers between devices: 1250 us -> 1330 us
    all_gather x1, waiting for transfers between devices: 0.01 us -> 138 us  [local(): lax.all_gather(jnp.concatenate([down_grads, gain_block], axis=0), AXES, a...]
    all_gather x1, waiting for transfers between devices: 127 us -> 83.3 us  [gather_tokens(): return lax.all_gather(values, AXES, axis=0, tiled=True)]
    all_to_all x2, waiting for transfers between devices: 43.1 us -> 0.01 us  [rows_from_columns(): moved = lax.all_to_all(grad, AXES, 0, 2, tiled=True)]
  transfers between devices with their start and end apart: 10 -> 10, of which waited for: 8 -> 8; matrix products, arithmetic and copies ran while one was open for 30% -> 26% of each run, Pallas kernels for 0% -> 0%
where the time goes in v5:
time: 2000 us; the launch traced here: 1990 us
  waiting for transfers between devices  1330 us (66%)
  matrix products  318 us (16%)
  local copies, waits for them, and re-layouts  246 us (12%)
  other arithmetic  60 us (3%)
  starting transfers between devices  24.6 us (1%)
    all_gather x1, waiting for transfers between devices, local(): lax.all_gather(jnp.stack([h_two, grad_feed]), AXES, axis=1, tiled=True)  429 us
    all_gather x1, waiting for transfers between devices, local(): lax.all_gather(jnp.concatenate([gate_weight, up_weight], axis=1), AXES, a...  208 us
    all_gather x1, waiting for transfers between devices, local(): weight_down = lax.all_gather(down_weight, AXES, axis=0, tiled=True)  160 us
    all_gather x1, waiting for transfers between devices, gather_packed(): gathered = lax.all_gather(jnp.concatenate(flat), AXES, axis=0, tiled=False)  155 us
    all_to_all x2, waiting for transfers between devices, column_shares(): moved = lax.all_to_all(blocks, AXES, 2, 0, tiled=True)  155 us
    all_gather x1, waiting for transfers between devices, local(): lax.all_gather(jnp.concatenate([down_grads, gain_block], axis=0), AXES, a...  138 us
    dot_general x9, matrix products, matmul(): return jnp.dot(left, right, preferred_element_type=jnp.float32)  123 us
    dot_general x8, matrix products, back_product(): lax.dot_general(left, right, (((1,), (1,)), ((), ())), preferred_element_...  95.1 us
  transfers between devices with their start and end apart: 10, of which 8 were waited for; matrix products, arithmetic and copies ran while one was open for 26% of the time, Pallas kernels for 0%

profile of v5, /device:TPU:0, one launch (start us, length us, event | category | flops | bytes accessed | tf_op | source)
XLA Modules:
  0.0 1993.2 jit_solution(12332562335416763243)
XLA Ops:
  33.0 155.5 %all-gather.18.cloned.1.call-done = bf16[13533184]{0:T(1024)(128)(2,1)} async-done(((bf16[422912]{0:T(1024)(128)(2,1)}), bf16[13533184]{0:T(1024)(128)(2,1)}) %all-gather.18.cloned.1.call-update) | async-done | bytes 27066384 | tf_op jit(solution)/shard_map/all_gather | solution.py:77
  188.5 35.8 %reshape.476 = bf16[32,422912]{1,0:T(8,128)(2,1)} reshape(bf16[13533184]{0:T(1024)(128)(2,1)} %all-gather.18.cloned.1.call-done) | data formatting | bytes 54132736 | tf_op jit(solution)/shard_map/all_gather | solution.py:77
  224.3 11.4 slice.216
  249.5 12.7 reshape.447
  288.6 7.0 reshape.445
  295.6 8.6 copy.110
  320.3 9.6 multiply_reduce_fusion.5
  329.9 208.4 %all-gather.10.cloned.1.call-done = bf16[2560,12800]{1,0:T(8,128)(2,1)} async-done(((bf16[80,12800]{1,0:T(8,128)(2,1)}), bf16[2560,12800]{1,0:T(8,128)(2,1)}) %all-gather.10.cloned.1.call-update) | async-done | bytes 65536016 | tf_op jit(solution)/shard_map/all_gather | solution.py:156
  538.3 31.4 %fusion.86 = f32[256,12800]{1,0:T(8,128)} fusion(bf16[2560,12800]{1,0:T(8,128)(2,1)} %all-gather.10.cloned.1.call-done, f32[256,2560]{1,0:T(8,128)S(1)} %get-tuple-element.116, f32[2560]{0:T(1024)} %reshape.471, f32[256]{0:T(256)S(1)} %add_rsqrt_fusion), kind=kOutput, calls=%fused_computation.185 | convolution fusion | flops 16779182080 | bytes 81275904 | tf_op jit(solution)/shard_map/dot_general | solution.py:23
  569.6 160.1 %all-gather.12.cloned.1.call-done = bf16[6400,2560]{1,0:T(8,128)(2,1)} async-done(((bf16[200,2560]{1,0:T(8,128)(2,1)}), bf16[6400,2560]{1,0:T(8,128)(2,1)}) %all-gather.12.cloned.1.call-update) | async-done | bytes 32768016 | tf_op jit(solution)/shard_map/all_gather | solution.py:159
  729.7 21.4 %multiply_convert_fusion.4 = (bf16[256,6400]{1,0:T(8,128)(2,1)}, bf16[256,6400]{1,0:T(8,128)(2,1)}) fusion(f32[256,12800]{1,0:T(8,128)} %fusion.86, bf16[256,2560]{1,0:T(8,128)(2,1)} %multiply_convert_fusion.12, bf16[6400,2560]{1,0:T(8,128)(2,1)} %all-gather.12.cloned.1.call-done), kind=kOutput, calls=%fused_computation.33 | convolution fusion | flops 8409907200 | bytes 53739520 | tf_op jit(solution)/shard_map/dot_general | solution.py:33
  751.1 27.9 %fusion.21 = f32[256,2560]{1,0:T(8,128)} fusion(bf16[2560,12800]{1,0:T(8,128)(2,1)} %all-gather.10.cloned.1.call-done, bf16[256,6400]{1,0:T(8,128)(2,1)} %get-tuple-element.87, bf16[256,6400]{1,0:T(8,128)(2,1)} %get-tuple-element.86), kind=kOutput, calls=%fused_computation.21 | convolution fusion | flops 16790323200 | bytes 74711040 | tf_op jit(solution)/shard_map/dot_general | solution.py:33
  789.5 428.9 %all-gather.14.cloned.1.call-done = bf16[2,8192,2560]{2,1,0:T(8,128)(2,1)} async-done(((bf16[2,256,2560]{2,1,0:T(8,128)(2,1)}), bf16[2,8192,2560]{2,1,0:T(8,128)(2,1)}) %all-gather.14.cloned.1.call-update) | async-done | bytes 83886096 | tf_op jit(solution)/shard_map/all_gather | solution.py:216
  1221.9 6.4 multiply_convert_fusion.10
  1235.5 10.2 convolution_convert_fusion
  1287.0 6.9 pad_maximum_fusion
  1329.8 38.9 %all-to-all-done = bf16[256,2,32,80]{0,1,3,2:T(2,128)(2,1)} async-done(((bf16[256,2,32,80]{0,1,3,2:T(2,128)(2,1)}), bf16[256,2,32,80]{0,1,3,2:T(2,128)(2,1)}, u32[]{:S(2)}, u32[]{:S(2)}) %all-to-all-start) | async-done | bytes 2621472 | tf_op jit(solution)/shard_map/all_to_all | solution.py:95
  1381.1 116.3 %all-to-all-done.1 = bf16[256,1,32,280]{0,3,1,2:T(8,128)(2,1)} async-done(((bf16[256,1,32,280]{0,3,1,2:T(8,128)(2,1)}), bf16[256,1,32,280]{0,3,1,2:T(8,128)(2,1)}, u32[]{:S(2)}, u32[]{:S(2)}) %all-to-all-start.1) | async-done | bytes 4587552 | tf_op jit(solution)/shard_map/all_to_all | solution.py:95
  1502.4 22.1 %fusion.4 = f32[8192,200]{0,1:T(8,128)} fusion(bf16[200,2560]{1,0:T(8,128)(2,1)S(1)} %copy-done.37, bf16[2,8192,2560]{2,1,0:T(8,128)(2,1)} %all-gather.14.cloned.1.call-done), kind=kOutput, calls=%fused_computation.4 | convolution fusion | flops 8388608000 | bytes 49520640 | tf_op jit(solution)/shard_map/dot_general | solution.py:33
  1524.5 22.4 %fusion.10 = f32[8192,200]{0,1:T(8,128)} fusion(bf16[2,8192,2560]{2,1,0:T(8,128)(2,1)} %all-gather.14.cloned.1.call-done, bf16[2560,12800]{1,0:T(8,128)(2,1)} %all-gather.10.cloned.1.call-done, s32[]{:T(128)S(6)} %select_n.26), kind=kOutput, calls=%fused_computation.10 | convolution fusion | flops 8388608000 | bytes 49807364 | tf_op jit(solution)/shard_map/dot_general | solution.py:23
  1546.9 26.5 %multiply_convert_fusion.2 = (bf16[8192,200]{0,1:T(8,128)(2,1)S(1)}, bf16[8192,200]{0,1:T(8,128)(2,1)}, f32[8192,200]{0,1:T(8,128)}) fusion(f32[8192,200]{0,1:T(8,128)} %fusion.4, f32[8192,200]{0,1:T(8,128)} %fusion.10, bf16[2560,12800]{1,0:T(8,128)(2,1)} %all-gather.10.cloned.1.call-done, s32[]{:T(128)S(6)} %select_n.27, ...), kind=kOutput, calls=%fused_computation.30 | convolution fusion | flops 8409907200 | bytes 69468160 | tf_op jit(solution)/shard_map/dot_general | solution.py:23
  1573.4 27.6 %fusion.6 = f32[2560,400]{0,1:T(8,128)} fusion(bf16[2,8192,2560]{2,1,0:T(8,128)(2,1)} %all-gather.14.cloned.1.call-done, bf16[8192,200]{0,1:T(8,128)(2,1)} %get-tuple-element.89, bf16[8192,200]{0,1:T(8,128)(2,1)S(1)} %get-tuple-element.88), kind=kOutput, calls=%fused_computation.6 | convolution fusion | flops 16790323200 | bytes 52592640 | tf_op jit(solution)/shard_map/dot_general | solution.py:27
  1600.9 83.3 %all-gather.16.cloned.1.call-done = bf16[8192,3584]{0,1:T(8,128)(2,1)} async-done(((bf16[256,3584]{0,1:T(8,128)(2,1)}), bf16[8192,3584]{0,1:T(8,128)(2,1)}) %all-gather.16.cloned.1.call-update) | async-done | bytes 58720272 | tf_op jit(solution)/shard_map/all_gather | solution.py:89
  1688.7 7.0 fusion.17
  1697.3 8.6 all-to-all-start.2
  1705.9 19.1 fusion
  1728.7 11.7 copy.140
  1740.4 6.1 all-to-all-start.3
  1751.4 24.3 %fusion.37 = bf16[256,2560]{1,0:T(8,128)(2,1)} fusion(f32[256,2560]{1,0:T(8,128)} %copy-done.6, bf16[6400,2560]{1,0:T(8,128)(2,1)} %all-gather.12.cloned.1.call-done, f32[256,12800]{1,0:T(8,128)} %fusion.86, f32[256]{0:T(256)S(1)} %copy-done.53), kind=kOutput, calls=%fused_computation.60 | convolution fusion | flops 8401059840 | bytes 49808384 | tf_op jit(solution)/shard_map/dot_general | solution.py:23
  1775.7 137.6 %all-gather.20.cloned.1.call-done = bf16[32,268,1056]{2,1,0:T(8,128)(2,1)} async-done(((bf16[1,268,1056]{2,1,0:T(8,128)(2,1)}), bf16[32,268,1056]{2,1,0:T(8,128)(2,1)}) %all-gather.20.cloned.1.call-update) | async-done | bytes 18112528 | tf_op jit(solution)/shard_map/all_gather | solution.py:326
  1916.8 11.2 slice.231
  1935.1 22.7 %fusion.2 = f32[200,2560]{1,0:T(8,128)} fusion(bf16[2,8192,2560]{2,1,0:T(8,128)(2,1)} %all-gather.14.cloned.1.call-done, f32[8192,200]{0,1:T(8,128)} %fusion.10, f32[8192,200]{0,1:T(8,128)} %get-tuple-element.122), kind=kOutput, calls=%fused_computation.2 | convolution fusion | flops 8398438400 | bytes 57098240 | tf_op jit(solution)/shard_map/dot_general | solution.py:27
  (302 shorter events, 250.4 us)
Async XLA Ops:
  7.2 181.3 %all-gather.18.cloned.1.call-start = ((), (), s32[]{:S(2)}) async-start(), calls=%async_computation.8 | async-start | bytes 27912192 | tf_op jit(solution)/shard_map/all_gather | solution.py:77
  22.6 515.7 %all-gather.10.cloned.1.call-start = ((), (), s32[]{:S(2)}) async-start(), calls=%async_computation.4 | async-start | bytes 67584000 | tf_op jit(solution)/shard_map/all_gather | solution.py:156
  25.7 704.0 %all-gather.12.cloned.1.call-start = ((), (), s32[]{:S(2)}) async-start(), calls=%async_computation.5 | async-start | bytes 33792000 | tf_op jit(solution)/shard_map/all_gather | solution.py:159
  26.5 1192.0 %all-gather.14.cloned.1.call-start = ((), (), s32[]{:S(2)}) async-start(), calls=%async_computation.6 | async-start | bytes 86507520 | tf_op jit(solution)/shard_map/all_gather | solution.py:216
  224.3 17.5 copy-start
  249.5 14.1 slice-start
  281.1 34.1 %copy-start.16 = (bf16[2,128,40,128]{1,3,2,0:T(8,128)(2,1)}, bf16[2,128,40,128]{1,3,2,0:T(8,128)(2,1)S(1)}, u32[]{:S(2)}) copy-start(bf16[2,128,40,128]{1,3,2,0:T(8,128)(2,1)S(1)} %convolution_convert_fusion.1) | copy-start | bytes 7864324
  288.6 19.6 copy-start.46
  329.9 449.1 %copy-start.6 = (f32[256,2560]{1,0:T(8,128)}, f32[256,2560]{1,0:T(8,128)S(1)}, u32[]{:S(2)}) copy-start(f32[256,2560]{1,0:T(8,128)S(1)} %get-tuple-element.116) | copy-start | bytes 7864324
  784.1 900.2 %all-gather.16.cloned.1.call-start = ((), (), s32[]{:S(2)}) async-start(), calls=%async_computation.7 | async-start | bytes 60555264 | tf_op jit(solution)/shard_map/all_gather | solution.py:89
  786.7 431.7 %copy-start.3 = (bf16[2,1,128,2560]{3,2,1,0:T(8,128)(2,1)S(1)}, bf16[2,1,128,2560]{3,2,1,0:T(8,128)(2,1)}, u32[]{:S(2)}) copy-start(bf16[2,1,128,2560]{3,2,1,0:T(8,128)(2,1)} %param.15) | copy-start | bytes 3932164
  789.5 432.3 %copy-start.42 = (f32[2,40,128]{2,1,0:T(8,128)S(1)}, f32[2,40,128]{2,1,0:T(8,128)}, u32[]{:S(2)}) copy-start(f32[2,40,128]{2,1,0:T(8,128)} %copy-done.41) | copy-start | bytes 122884
  789.5 432.3 %copy-start.49 = (f32[256]{0:T(256)S(1)}, f32[256]{0:T(256)}, u32[]{:S(2)}) copy-start(f32[256]{0:T(256)} %get-tuple-element.107) | copy-start | bytes 3076
  1221.9 6.5 copy-start.7
  1221.9 6.5 copy-start.14
  1221.9 6.5 copy-start.43
  1221.9 6.4 copy-start.52
  1250.1 10.2 slice-start.2
  1293.9 74.8 %all-to-all-start = ((bf16[256,2,32,80]{0,1,3,2:T(2,128)(2,1)}), bf16[256,2,32,80]{0,1,3,2:T(2,128)(2,1)}, u32[]{:S(2)}, u32[]{:S(2)}) async-start(bf16[256,2,32,80]{0,1,3,2:T(2,128)(2,1)} %pad_maximum_fusion), calls=%async_computation | async-start | bytes 5242880 | tf_op jit(solution)/shard_map/all_to_all | solution.py:95
  1297.6 615.7 %all-gather.20.cloned.1.call-start = ((), (), s32[]{:S(2)}) async-start(), calls=%async_computation.9 | async-start | bytes 20680704 | tf_op jit(solution)/shard_map/all_gather | solution.py:326
  1297.6 5.6 copy-start.11
  1315.8 5.7 copy-start.17
  1368.7 128.7 %all-to-all-start.1 = ((bf16[256,1,32,280]{0,3,1,2:T(8,128)(2,1)}), bf16[256,1,32,280]{0,3,1,2:T(8,128)(2,1)}, u32[]{:S(2)}, u32[]{:S(2)}) async-start(bf16[256,1,32,280]{0,3,1,2:T(8,128)(2,1)} %maximum_bitcast_fusion.1), calls=%async_computation.1 | async-start | bytes 9175040 | tf_op jit(solution)/shard_map/all_to_all | solution.py:95
  1695.7 10.2 copy-start.32
  1697.3 43.1 %all-to-all-start.2 = ((f32[32,1,4160]{2,1,0:T(1,128)}), f32[32,1,4160]{2,1,0:T(1,128)S(1)}, u32[]{:S(2)}, u32[]{:S(2)}) async-start(f32[32,1,4160]{2,1,0:T(1,128)} %copy.137), calls=%async_computation.2 | async-start | bytes 1081344 | tf_op jit(solution)/shard_map/all_to_all | solution.py:101
  1705.9 19.1 copy-start.27
  1740.4 6.2 copy-start.60
  1740.4 6.2 copy-start.4
  1740.4 6.2 copy-start.40
  1740.4 6.2 copy-start.50
  1740.4 220.0 %all-to-all-start.3 = ((f32[2560,1,480]{2,1,0:T(1,128)}), f32[2560,1,480]{2,1,0:T(1,128)}, u32[]{:S(2)}, u32[]{:S(2)}) async-start(f32[2560,1,480]{2,1,0:T(1,128)} %copy.140), calls=%async_computation.3 | async-start | bytes 10485760 | tf_op jit(solution)/shard_map/all_to_all | solution.py:101
  1916.8 11.8 copy-start.33
  (45 other events, 134.8 us)
Sparse Core Ops, SparseCore 0:
  22.7 165.7 all-gather.17
  191.9 346.2 all-gather.9
  541.1 188.5 all-gather.11
  784.2 434.2 all-gather.13
  1220.3 463.8 all-gather.15
  1686.9 226.3 all-gather.19

commit v6 on v5

--- a/solution.py
+++ b/solution.py
@@ -153,10 +153,9 @@
         gain_latent,
         gain_two,
     ) = gather_packed(attn_shards)
-    weight_gate_up = lax.all_gather(
-        jnp.concatenate([gate_weight, up_weight], axis=1), AXES, axis=0, tiled=True
-    )
-    weight_down = lax.all_gather(down_weight, AXES, axis=0, tiled=True)
+    weight_gate_up, weight_down = gather_packed(
+        (jnp.concatenate([gate_weight, up_weight], axis=1), down_weight)
+    )
     half = ROPE // 2
     freqs = 10000.0 ** (-(2.0 * jnp.arange(half, dtype=jnp.float32)) / ROPE)
     angles = jnp.arange(slot, dtype=jnp.float32)[:, None] * freqs[None, :]
@@ -200,7 +199,6 @@
     attended = attended.reshape(rows, HEADS * VDIM).astype(jnp.bfloat16)
     q_rank = query_low.shape[1]
     kv_rank = latent_low.shape[1]
-    latent_src = jnp.concatenate([query_low, latent_low, attended], axis=1)
     middle = inputs + depth_scale * matmul(attended, weight_out)
     normed_two, inverse_two = normalize(middle)
     h_two = (normed_two * gain_two.astype(jnp.float32)).astype(jnp.bfloat16)
@@ -213,14 +211,15 @@
     output = result.astype(jnp.bfloat16).reshape(tokens.shape)
     grad_out = cotangent.reshape(rows, width).astype(jnp.float32) * valid_rows
     grad_feed = (depth_scale * grad_out).astype(jnp.bfloat16)
-    feed_all = lax.all_gather(jnp.stack([h_two, grad_feed]), AXES, axis=1, tiled=True)
-    latent_src, feed_all = lax.optimization_barrier((latent_src, feed_all))
-    latents_all = gather_tokens(latent_src)
+    latents_all = gather_tokens(
+        jnp.concatenate([query_low, latent_low, attended, h_two], axis=1)
+    )
     query_low_all = latents_all[:, :q_rank]
     latent_low_all = latents_all[:, q_rank : q_rank + kv_rank]
-    attended_all = latents_all[:, q_rank + kv_rank :]
-    h_two_all = feed_all[0]
-    grad_feed_all = feed_all[1]
+    attended_all = latents_all[:, q_rank + kv_rank : q_rank + kv_rank + width]
+    h_two_all = latents_all[:, q_rank + kv_rank + width :]
+    grad_feed_late, latents_all = lax.optimization_barrier((grad_feed, latents_all))
+    grad_feed_all = gather_tokens(grad_feed_late)
     grad_hidden = back_product(grad_feed, weight_down)
     grad_gate = (grad_hidden * upward * sigma * (1.0 + gate * (1.0 - sigma))).astype(jnp.bfloat16)
     grad_up = (grad_hidden * gate * sigma).astype(jnp.bfloat16)

time: 2000 us -> 1910 us (0.955)
  waiting for transfers between devices: 1330 us -> 917 us
  local copies, waits for them, and re-layouts: 246 us -> 548 us
    all_gather x3 -> x0, waiting for transfers between devices: 797 us -> none  [the longest x1 429 us: local(): lax.all_gather(jnp.stack([h_two, grad_feed]), AXES, axis=1, tiled=True)]
    all_gather x1 -> x2, waiting for transfers between devices: 155 us -> 504 us  [gather_packed(): gathered = lax.all_gather(jnp.concatenate(flat), AXES, axis=0, tiled=False)]
    all_gather x1, waiting for transfers between devices: 138 us -> 0.01 us  [local(): lax.all_gather(jnp.concatenate([down_grads, gain_block], axis=0), AXES, a...]
    reshape x5 -> x7, local copies, waits for them, and re-layouts: 31.4 us -> 154 us  [gather_packed(): results.append(piece.reshape((devices * shard.shape[0],) + shard.shape[1:]))]
    all_gather x1 -> x2, local copies, waits for them, and re-layouts: 35.8 us -> 142 us  [gather_packed(): gathered = lax.all_gather(jnp.concatenate(flat), AXES, axis=0, tiled=False)]
    all_to_all x2, waiting for transfers between devices: 155 us -> 241 us  [column_shares(): moved = lax.all_to_all(blocks, AXES, 2, 0, tiled=True)]
    slice x7 -> x9, local copies, waits for them, and re-layouts: 19.1 us -> 85.6 us  [gather_packed(): piece = gathered[:, offset:offset + shard.size]]
    all_gather x1 -> x2, waiting for transfers between devices: 83.3 us -> 134 us  [gather_tokens(): return lax.all_gather(values, AXES, axis=0, tiled=True)]
  transfers between devices with their start and end apart: 10 -> 9, of which waited for: 8 -> 6; matrix products, arithmetic and copies ran while one was open for 26% -> 46% of each run, Pallas kernels for 0% -> 0%
where the time goes in v6:
time: 1910 us; the launch traced here: 1890 us
  waiting for transfers between devices  917 us (48%)
  local copies, waits for them, and re-layouts  548 us (29%)
  matrix products  321 us (17%)
  other arithmetic  62.2 us (3%)
  starting transfers between devices  30.5 us (2%)
    all_gather x2, waiting for transfers between devices, gather_packed(): gathered = lax.all_gather(jnp.concatenate(flat), AXES, axis=0, tiled=False)  504 us
    all_to_all x2, waiting for transfers between devices, column_shares(): moved = lax.all_to_all(blocks, AXES, 2, 0, tiled=True)  241 us
    reshape x7, local copies, waits for them, and re-layouts, gather_packed(): results.append(piece.reshape((devices * shard.shape[0],) + shard.shape[1:]))  154 us
    all_gather x2, local copies, waits for them, and re-layouts, gather_packed(): gathered = lax.all_gather(jnp.concatenate(flat), AXES, axis=0, tiled=False)  142 us
    all_gather x2, waiting for transfers between devices, gather_tokens(): return lax.all_gather(values, AXES, axis=0, tiled=True)  134 us
    dot_general x9, matrix products, matmul(): return jnp.dot(left, right, preferred_element_type=jnp.float32)  127 us
    dot_general x8, matrix products, back_product(): lax.dot_general(left, right, (((1,), (1,)), ((), ())), preferred_element_...  98.1 us
    slice x9, local copies, waits for them, and re-layouts, gather_packed(): piece = gathered[:, offset:offset + shard.size]  85.6 us
  transfers between devices with their start and end apart: 9, of which 6 were waited for; matrix products, arithmetic and copies ran while one was open for 46% of the time, Pallas kernels for 0%

profile of v6, /device:TPU:0, one launch (start us, length us, event | category | flops | bytes accessed | tf_op | source)
XLA Modules:
  0.0 1894.1 jit_solution(8877059877875618955)
XLA Ops:
  43.0 147.4 %all-gather.14.cloned.1.call-done = bf16[13533184]{0:T(1024)(128)(2,1)} async-done(((bf16[422912]{0:T(1024)(128)(2,1)}), bf16[13533184]{0:T(1024)(128)(2,1)}) %all-gather.14.cloned.1.call-update) | async-done | bytes 27066384 | tf_op jit(solution)/shard_map/all_gather | solution.py:77
  190.4 35.6 %reshape.459 = bf16[32,422912]{1,0:T(8,128)(2,1)} reshape(bf16[13533184]{0:T(1024)(128)(2,1)} %all-gather.14.cloned.1.call-done) | data formatting | bytes 54132736 | tf_op jit(solution)/shard_map/all_gather | solution.py:77
  226.0 11.4 slice.220
  251.2 12.5 reshape.427
  299.5 8.6 copy.112
  323.4 9.5 multiply_reduce_fusion.5
  340.2 356.3 %all-gather.16.cloned.1.call-done = bf16[49152000]{0:T(1024)(128)(2,1)} async-done(((bf16[1536000]{0:T(1024)(128)(2,1)}), bf16[49152000]{0:T(1024)(128)(2,1)}) %all-gather.16.cloned.1.call-update) | async-done | bytes 98304016 | tf_op jit(solution)/shard_map/all_gather | solution.py:77
  696.5 106.2 %reshape.460 = bf16[32,1536000]{1,0:T(8,128)(2,1)} reshape(bf16[49152000]{0:T(1024)(128)(2,1)} %all-gather.16.cloned.1.call-done) | data formatting | bytes 196608000 | tf_op jit(solution)/shard_map/all_gather | solution.py:77
  802.7 22.8 %slice.225 = bf16[32,512000]{1,0:T(8,128)(2,1)} slice(bf16[32,1536000]{1,0:T(8,128)(2,1)} %reshape.460), slice={[0:32], [1024000:1536000]} | slice | bytes 65536000 | tf_op jit(solution)/shard_map/slice | solution.py:82
  825.6 43.6 %slice.222 = bf16[32,1024000]{1,0:T(8,128)(2,1)} slice(bf16[32,1536000]{1,0:T(8,128)(2,1)} %reshape.460), slice={[0:32], [0:1024000]} | slice | bytes 131072000 | tf_op jit(solution)/shard_map/slice | solution.py:82
  869.2 41.9 %reshape.431 = bf16[6400,2560]{1,0:T(8,128)(2,1)} reshape(bf16[32,512000]{1,0:T(8,128)(2,1)} %slice.225) | data formatting | bytes 65536000 | tf_op jit(solution)/shard_map/reshape | solution.py:83
  911.1 80.4 %reshape.430 = bf16[2560,12800]{1,0:T(8,128)(2,1)} reshape(bf16[32,1024000]{1,0:T(8,128)(2,1)} %slice.222) | data formatting | bytes 131072000 | tf_op jit(solution)/shard_map/reshape | solution.py:83
  991.4 30.7 %fusion.83 = f32[256,12800]{1,0:T(8,128)} fusion(bf16[256,2560]{1,0:T(8,128)(2,1)S(1)} %copy-done.18, bf16[2560,12800]{1,0:T(8,128)(2,1)} %reshape.430), kind=kOutput, calls=%fused_computation.182 | convolution fusion | flops 16777216000 | bytes 79953920 | tf_op jit(solution)/shard_map/dot_general | solution.py:23
  1022.1 22.7 %multiply_convert_fusion.4 = (bf16[256,6400]{1,0:T(8,128)(2,1)}, bf16[256,6400]{1,0:T(8,128)(2,1)}) fusion(f32[256,12800]{1,0:T(8,128)} %fusion.83, bf16[256,2560]{1,0:T(8,128)(2,1)} %bitcast.201, bf16[6400,2560]{1,0:T(8,128)(2,1)} %reshape.431), kind=kOutput, calls=%fused_computation.24 | convolution fusion | flops 8409907200 | bytes 53739520 | tf_op jit(solution)/shard_map/dot_general | solution.py:33
  1044.9 28.7 %multiply_reduce_fusion.1 = (f32[2560]{0:T(1024)S(1)}, f32[256]{0:T(256)S(1)}, f32[256,2560]{1,0:T(8,128)}) fusion(f32[256,2560]{1,0:T(8,128)S(1)} %copy-done.6, f32[256]{0:T(256)S(1)} %copy-done.68, f32[2560]{0:T(1024)S(1)} %copy-done.58, bf16[2560,12800]{1,0:T(8,128)(2,1)} %reshape.430, bf16[256,6400]{1,0:T(8,128)(2,1)} %get-tuple-element.85, ...), kind=kOutput, calls=%fused_computation.69 | convolution fusion | flops 16794253312 | bytes 77355008 | tf_op jit(solution)/shard_map/dot_general | solution.py:33
  1080.1 134.0 %all-gather.10.cloned.1.call-done = bf16[8192,6144]{1,0:T(8,128)(2,1)} async-done(((bf16[256,6144]{1,0:T(8,128)(2,1)}), bf16[8192,6144]{1,0:T(8,128)(2,1)}) %all-gather.10.cloned.1.call-update) | async-done | bytes 100663312 | tf_op jit(solution)/shard_map/all_gather | solution.py:89
  1225.9 10.0 convolution_convert_fusion
  1273.8 7.3 pad_maximum_fusion.2
  1323.8 58.7 %all-to-all-done = bf16[256,2,32,80]{0,1,3,2:T(2,128)(2,1)} async-done(((bf16[256,2,32,80]{0,1,3,2:T(2,128)(2,1)}), bf16[256,2,32,80]{0,1,3,2:T(2,128)(2,1)}, u32[]{:S(2)}, u32[]{:S(2)}) %all-to-all-start) | async-done | bytes 2621472 | tf_op jit(solution)/shard_map/all_to_all | solution.py:95
  1382.5 11.1 all-to-all-start.1
  1400.1 181.9 %all-to-all-done.1 = bf16[256,1,32,280]{0,3,1,2:T(8,128)(2,1)} async-done(((bf16[256,1,32,280]{0,3,1,2:T(8,128)(2,1)}), bf16[256,1,32,280]{0,3,1,2:T(8,128)(2,1)}, u32[]{:S(2)}, u32[]{:S(2)}) %all-to-all-start.1) | async-done | bytes 4587552 | tf_op jit(solution)/shard_map/all_to_all | solution.py:95
  1599.5 9.0 all-to-all-start.2
  1608.5 16.2 fusion
  1624.7 22.4 %fusion.6 = f32[8192,200]{0,1:T(8,128)} fusion(bf16[8192,6144]{1,0:T(8,128)(2,1)} %all-gather.10.cloned.1.call-done, bf16[2560,12800]{1,0:T(8,128)(2,1)} %reshape.430, s32[]{:T(128)S(6)} %select_n.26), kind=kOutput, calls=%fused_computation.6 | convolution fusion | flops 8388608000 | bytes 49807364 | tf_op jit(solution)/shard_map/dot_general | solution.py:23
  1647.1 22.7 %fusion.85 = f32[8192,200]{0,1:T(8,128)} fusion(bf16[8192,2560]{1,0:T(8,128)(2,1)} %all-gather.12.cloned.1.call-done, bf16[200,2560]{1,0:T(8,128)(2,1)S(1)} %copy-done.41), kind=kOutput, calls=%fused_computation.184 | convolution fusion | flops 8388608000 | bytes 49520640 | tf_op jit(solution)/shard_map/dot_general | solution.py:33
  1669.9 29.6 %multiply_convert_fusion.2 = (bf16[8192,200]{0,1:T(8,128)(2,1)}, bf16[8192,200]{0,1:T(8,128)(2,1)}, f32[8192,200]{0,1:T(8,128)}) fusion(f32[8192,200]{0,1:T(8,128)} %fusion.85, f32[8192,200]{0,1:T(8,128)} %fusion.6, bf16[2560,12800]{1,0:T(8,128)(2,1)} %reshape.430, s32[]{:T(128)S(6)} %select_n.27, bf16[8192,6144]{1,0:T(8,128)(2,1)} %all-gather.10.cloned.1.call-done), kind=kOutput, calls=%fused_computation.21 | convolution fusion | flops 8409907200 | bytes 69468160 | tf_op jit(solution)/shard_map/dot_general | solution.py:23
  1699.4 27.4 %fusion.2 = f32[2560,400]{0,1:T(8,128)S(1)} fusion(bf16[8192,6144]{1,0:T(8,128)(2,1)} %all-gather.10.cloned.1.call-done, bf16[8192,200]{0,1:T(8,128)(2,1)} %get-tuple-element.87, bf16[8192,200]{0,1:T(8,128)(2,1)} %get-tuple-element.86), kind=kOutput, calls=%fused_computation.2 | convolution fusion | flops 16790323200 | bytes 52592640 | tf_op jit(solution)/shard_map/dot_general | solution.py:27
  1729.4 11.7 copy.143
  1752.0 24.1 %fusion.28 = bf16[256,2560]{1,0:T(8,128)(2,1)} fusion(f32[256,2560]{1,0:T(8,128)} %copy-done.5, bf16[6400,2560]{1,0:T(8,128)(2,1)} %reshape.431, f32[256,12800]{1,0:T(8,128)} %fusion.83, f32[256]{0:T(256)S(1)} %copy-done.72), kind=kOutput, calls=%fused_computation.51 | convolution fusion | flops 8401059840 | bytes 49808384 | tf_op jit(solution)/shard_map/dot_general | solution.py:23
  1779.6 10.9 slice.237
  1800.2 22.7 %fusion.29 = f32[200,2560]{1,0:T(8,128)} fusion(bf16[8192,2560]{1,0:T(8,128)(2,1)} %all-gather.12.cloned.1.call-done, f32[8192,200]{0,1:T(8,128)} %fusion.6, f32[8192,200]{0,1:T(8,128)} %get-tuple-element.123), kind=kOutput, calls=%fused_computation.53 | convolution fusion | flops 8398438400 | bytes 57098240 | tf_op jit(solution)/shard_map/dot_general | solution.py:27
  1822.9 38.6 %all-to-all-done.3 = f32[2560,1,480]{2,1,0:T(1,128)} async-done(((f32[2560,1,480]{2,1,0:T(1,128)}), f32[2560,1,480]{2,1,0:T(1,128)}, u32[]{:S(2)}, u32[]{:S(2)}) %all-to-all-start.3) | async-done | bytes 4915232 | tf_op jit(solution)/shard_map/all_to_all | solution.py:101
  (331 shorter events, 282.1 us)
Async XLA Ops:
  7.2 17.3 copy-start.40
  7.2 19.4 %copy-start.42 = (bf16[80,6400]{1,0:T(8,128)(2,1)S(1)}, bf16[80,6400]{1,0:T(8,128)(2,1)}, u32[]{:S(2)}) copy-start(bf16[80,6400]{1,0:T(8,128)(2,1)} %param.27) | copy-start | bytes 3072004
  7.2 183.2 %all-gather.14.cloned.1.call-start = ((), (), s32[]{:S(2)}) async-start(), calls=%async_computation.6 | async-start | bytes 27912192 | tf_op jit(solution)/shard_map/all_gather | solution.py:77
  24.4 672.1 %all-gather.16.cloned.1.call-start = ((), (), s32[]{:S(2)}) async-start(), calls=%async_computation.7 | async-start | bytes 101376000 | tf_op jit(solution)/shard_map/all_gather | solution.py:77
  39.5 1174.6 %all-gather.10.cloned.1.call-start = ((), (), s32[]{:S(2)}) async-start(), calls=%async_computation.4 | async-start | bytes 103809024 | tf_op jit(solution)/shard_map/all_gather | solution.py:89
  42.9 272.1 %copy-start.44 = (f32[128,16]{0,1:T(8,128)}, f32[128,16]{0,1:T(8,128)S(1)}, u32[]{:S(2)}) copy-start(f32[128,16]{0,1:T(8,128)S(1)} %get-tuple-element.109) | copy-start | bytes 24580
  42.9 272.1 %copy-start.46 = (f32[128,16]{0,1:T(8,128)}, f32[128,16]{0,1:T(8,128)S(1)}, u32[]{:S(2)}) copy-start(f32[128,16]{0,1:T(8,128)S(1)} %get-tuple-element.110) | copy-start | bytes 24580
  226.0 17.5 copy-start
  251.2 13.3 slice-start
  284.9 34.2 %copy-start.13 = (bf16[2,128,40,128]{1,3,2,0:T(8,128)(2,1)}, bf16[2,128,40,128]{1,3,2,0:T(8,128)(2,1)S(1)}, u32[]{:S(2)}) copy-start(bf16[2,128,40,128]{1,3,2,0:T(8,128)(2,1)S(1)} %convolution_convert_fusion.1) | copy-start | bytes 7864324
  292.5 19.6 %copy-start.59 = (f32[768]{0:T(1024)}, f32[768]{0:T(1024)S(1)}, u32[]{:S(2)}) copy-start(f32[768]{0:T(1024)S(1)} %reshape.453) | copy-start | bytes 9220
  321.6 11.3 copy-start.57
  337.5 1309.6 %all-gather.12.cloned.1.call-start = ((), (), s32[]{:S(2)}) async-start(), calls=%async_computation.5 | async-start | bytes 43253760 | tf_op jit(solution)/shard_map/all_gather | solution.py:89
  911.1 80.4 %copy-start.18 = (bf16[256,2560]{1,0:T(8,128)(2,1)S(1)}, bf16[256,2560]{1,0:T(8,128)(2,1)}, u32[]{:S(2)}) copy-start(bf16[256,2560]{1,0:T(8,128)(2,1)} %copy-done.17) | copy-start | bytes 3932164
  1022.1 22.7 %copy-start.6 = (f32[256,2560]{1,0:T(8,128)S(1)}, f32[256,2560]{1,0:T(8,128)}, u32[]{:S(2)}) copy-start(f32[256,2560]{1,0:T(8,128)} %copy-done.5) | copy-start | bytes 7864324
  1022.1 22.7 %copy-start.58 = (f32[2560]{0:T(1024)S(1)}, f32[2560]{0:T(1024)}, u32[]{:S(2)}) copy-start(f32[2560]{0:T(1024)} %copy-done.57) | copy-start | bytes 30724
  1022.1 22.7 %copy-start.68 = (f32[256]{0:T(256)S(1)}, f32[256]{0:T(256)}, u32[]{:S(2)}) copy-start(f32[256]{0:T(256)} %copy-done.67) | copy-start | bytes 3076
  1044.9 28.7 %copy-start.71 = (f32[256]{0:T(256)S(1)}, f32[256]{0:T(256)}, u32[]{:S(2)}) copy-start(f32[256]{0:T(256)} %get-tuple-element.108) | copy-start | bytes 3076
  1073.6 140.5 %copy-start.3 = (bf16[2,1,128,2560]{3,2,1,0:T(8,128)(2,1)S(1)}, bf16[2,1,128,2560]{3,2,1,0:T(8,128)(2,1)}, u32[]{:S(2)}) copy-start(bf16[2,1,128,2560]{3,2,1,0:T(8,128)(2,1)} %param.15) | copy-start | bytes 3932164
  1080.1 136.9 %copy-start.52 = (f32[2,40,128]{2,1,0:T(8,128)S(1)}, f32[2,40,128]{2,1,0:T(8,128)}, u32[]{:S(2)}) copy-start(f32[2,40,128]{2,1,0:T(8,128)} %copy-done.51) | copy-start | bytes 122884
  1080.1 136.9 %copy-start.54 = (f32[2,40,128]{2,1,0:T(8,128)S(1)}, f32[2,40,128]{2,1,0:T(8,128)}, u32[]{:S(2)}) copy-start(f32[2,40,128]{2,1,0:T(8,128)} %copy-done.53) | copy-start | bytes 122884
  1080.1 136.9 %copy-start.56 = (f32[32,80]{1,0:T(8,128)S(1)}, f32[32,80]{1,0:T(8,128)}, u32[]{:S(2)}) copy-start(f32[32,80]{1,0:T(8,128)} %copy-done.55) | copy-start | bytes 30724
  1080.1 136.9 %copy-start.61 = (f32[256]{0:T(256)S(1)}, f32[256]{0:T(256)}, u32[]{:S(2)}) copy-start(f32[256]{0:T(256)} %get-tuple-element.105) | copy-start | bytes 3076
  1281.0 101.4 %all-to-all-start = ((bf16[256,2,32,80]{0,1,3,2:T(2,128)(2,1)}), bf16[256,2,32,80]{0,1,3,2:T(2,128)(2,1)}, u32[]{:S(2)}, u32[]{:S(2)}) async-start(bf16[256,2,32,80]{0,1,3,2:T(2,128)(2,1)} %pad_maximum_fusion.2), calls=%async_computation | async-start | bytes 5242880 | tf_op jit(solution)/shard_map/all_to_all | solution.py:95
  1284.8 491.2 %all-gather.18.cloned.1.call-start = ((), (), s32[]{:S(2)}) async-start(), calls=%async_computation.8 | async-start | bytes 20680704 | tf_op jit(solution)/shard_map/all_gather | solution.py:325
  1382.5 199.5 %all-to-all-start.1 = ((bf16[256,1,32,280]{0,3,1,2:T(8,128)(2,1)}), bf16[256,1,32,280]{0,3,1,2:T(8,128)(2,1)}, u32[]{:S(2)}, u32[]{:S(2)}) async-start(bf16[256,1,32,280]{0,3,1,2:T(8,128)(2,1)} %maximum_bitcast_fusion.1), calls=%async_computation.1 | async-start | bytes 9175040 | tf_op jit(solution)/shard_map/all_to_all | solution.py:95
  1597.8 10.7 copy-start.32
  1599.5 141.7 %all-to-all-start.2 = ((f32[32,1,4160]{2,1,0:T(1,128)}), f32[32,1,4160]{2,1,0:T(1,128)S(1)}, u32[]{:S(2)}, u32[]{:S(2)}) async-start(f32[32,1,4160]{2,1,0:T(1,128)} %copy.140), calls=%async_computation.2 | async-start | bytes 1081344 | tf_op jit(solution)/shard_map/all_to_all | solution.py:101
  1624.7 22.4 %copy-start.41 = (bf16[200,2560]{1,0:T(8,128)(2,1)S(1)}, bf16[200,2560]{1,0:T(8,128)(2,1)}, u32[]{:S(2)}) copy-start(bf16[200,2560]{1,0:T(8,128)(2,1)} %param.28) | copy-start | bytes 3072004
  1699.4 27.4 %copy-start.43 = (f32[2560,80]{0,1:T(8,128)S(1)}, f32[2560,80]{0,1:T(8,128)}, u32[]{:S(2)}) copy-start(f32[2560,80]{0,1:T(8,128)} %fusion) | copy-start | bytes 2457604
  1741.2 120.4 %all-to-all-start.3 = ((f32[2560,1,480]{2,1,0:T(1,128)}), f32[2560,1,480]{2,1,0:T(1,128)}, u32[]{:S(2)}, u32[]{:S(2)}) async-start(f32[2560,1,480]{2,1,0:T(1,128)} %copy.143), calls=%async_computation.3 | async-start | bytes 10485760 | tf_op jit(solution)/shard_map/all_to_all | solution.py:101
  1779.5 11.5 copy-start.33
  (57 other events, 219.0 us)
Sparse Core Ops, SparseCore 0:
  24.5 165.7 all-gather.13
  193.2 503.2 all-gather.15
  699.4 514.6 all-gather.9
  1217.3 375.2 all-gather.11
  1595.3 138.4 all-gather.17

commit v7 on v6

--- a/solution.py
+++ b/solution.py
@@ -153,9 +153,10 @@
         gain_latent,
         gain_two,
     ) = gather_packed(attn_shards)
-    weight_gate_up, weight_down = gather_packed(
-        (jnp.concatenate([gate_weight, up_weight], axis=1), down_weight)
-    )
+    weight_gate_up = lax.all_gather(
+        jnp.concatenate([gate_weight, up_weight], axis=1), AXES, axis=0, tiled=True
+    )
+    weight_down = lax.all_gather(down_weight, AXES, axis=0, tiled=True)
     half = ROPE // 2
     freqs = 10000.0 ** (-(2.0 * jnp.arange(half, dtype=jnp.float32)) / ROPE)
     angles = jnp.arange(slot, dtype=jnp.float32)[:, None] * freqs[None, :]
@@ -212,14 +213,13 @@
     grad_out = cotangent.reshape(rows, width).astype(jnp.float32) * valid_rows
     grad_feed = (depth_scale * grad_out).astype(jnp.bfloat16)
     latents_all = gather_tokens(
-        jnp.concatenate([query_low, latent_low, attended, h_two], axis=1)
+        jnp.concatenate([query_low, latent_low, attended, h_two, grad_feed], axis=1)
     )
     query_low_all = latents_all[:, :q_rank]
     latent_low_all = latents_all[:, q_rank : q_rank + kv_rank]
     attended_all = latents_all[:, q_rank + kv_rank : q_rank + kv_rank + width]
-    h_two_all = latents_all[:, q_rank + kv_rank + width :]
-    grad_feed_late, latents_all = lax.optimization_barrier((grad_feed, latents_all))
-    grad_feed_all = gather_tokens(grad_feed_late)
+    h_two_all = latents_all[:, q_rank + kv_rank + width : q_rank + kv_rank + 2 * width]
+    grad_feed_all = latents_all[:, q_rank + kv_rank + 2 * width :]
     grad_hidden = back_product(grad_feed, weight_down)
     grad_gate = (grad_hidden * upward * sigma * (1.0 + gate * (1.0 - sigma))).astype(jnp.bfloat16)
     grad_up = (grad_hidden * gate * sigma).astype(jnp.bfloat16)

time: 1910 us -> 1910 us (level)
  waiting for transfers between devices: 917 us -> 1240 us
  local copies, waits for them, and re-layouts: 548 us -> 248 us
    all_gather x0 -> x2, waiting for transfers between devices: none -> 352 us  [the longest x1 191 us: local(): lax.all_gather(jnp.concatenate([gate_weight, up_weight], axis=1), AXES, a...]
    all_gather x2 -> x1, waiting for transfers between devices: 504 us -> 158 us  [gather_packed(): gathered = lax.all_gather(jnp.concatenate(flat), AXES, axis=0, tiled=False)]
    all_gather x2 -> x1, waiting for transfers between devices: 134 us -> 416 us  [gather_tokens(): return lax.all_gather(values, AXES, axis=0, tiled=True)]
    reshape x7 -> x5, local copies, waits for them, and re-layouts: 154 us -> 31.4 us  [gather_packed(): results.append(piece.reshape((devices * shard.shape[0],) + shard.shape[1:]))]
    all_gather x2 -> x1, local copies, waits for them, and re-layouts: 142 us -> 35.3 us  [gather_packed(): gathered = lax.all_gather(jnp.concatenate(flat), AXES, axis=0, tiled=False)]
    slice x9 -> x7, local copies, waits for them, and re-layouts: 85.6 us -> 19.2 us  [gather_packed(): piece = gathered[:, offset:offset + shard.size]]
    all_to_all x2, waiting for transfers between devices: 241 us -> 273 us  [column_shares(): moved = lax.all_to_all(blocks, AXES, 2, 0, tiled=True)]
  transfers between devices with their start and end apart: 9 -> 9, of which waited for: 6 -> 7; matrix products, arithmetic and copies ran while one was open for 46% -> 30% of each run, Pallas kernels for 0% -> 0%
where the time goes in v7:
time: 1910 us; the launch traced here: 1900 us
  waiting for transfers between devices  1240 us (65%)
  matrix products  322 us (17%)
  local copies, waits for them, and re-layouts  248 us (13%)
  other arithmetic  52.1 us (3%)
  starting transfers between devices  27.6 us (1%)
    all_gather x1, waiting for transfers between devices, gather_tokens(): return lax.all_gather(values, AXES, axis=0, tiled=True)  416 us
    all_to_all x2, waiting for transfers between devices, column_shares(): moved = lax.all_to_all(blocks, AXES, 2, 0, tiled=True)  273 us
    all_gather x1, waiting for transfers between devices, local(): lax.all_gather(jnp.concatenate([gate_weight, up_weight], axis=1), AXES, a...  191 us
    all_gather x1, waiting for transfers between devices, local(): weight_down = lax.all_gather(down_weight, AXES, axis=0, tiled=True)  161 us
    all_gather x1, waiting for transfers between devices, gather_packed(): gathered = lax.all_gather(jnp.concatenate(flat), AXES, axis=0, tiled=False)  158 us
    dot_general x9, matrix products, matmul(): return jnp.dot(left, right, preferred_element_type=jnp.float32)  126 us
    dot_general x8, matrix products, back_product(): lax.dot_general(left, right, (((1,), (1,)), ((), ())), preferred_element_...  99.5 us
    dot_general x7, matrix products, rows_product(): lax.dot_general(left, right, (((0,), (0,)), ((), ())), preferred_element_...  84.2 us
  transfers between devices with their start and end apart: 9, of which 7 were waited for; matrix products, arithmetic and copies ran while one was open for 30% of the time, Pallas kernels for 0%

profile of v7, /device:TPU:0, one launch (start us, length us, event | category | flops | bytes accessed | tf_op | source)
XLA Modules:
  0.0 1901.3 jit_solution(18048364131921257597)
XLA Ops:
  30.3 158.3 %all-gather.15.cloned.1.call-done = bf16[13533184]{0:T(1024)(128)(2,1)} async-done(((bf16[422912]{0:T(1024)(128)(2,1)}), bf16[13533184]{0:T(1024)(128)(2,1)}) %all-gather.15.cloned.1.call-update) | async-done | bytes 27066384 | tf_op jit(solution)/shard_map/all_gather | solution.py:77
  188.6 35.3 %reshape.435 = bf16[32,422912]{1,0:T(8,128)(2,1)} reshape(bf16[13533184]{0:T(1024)(128)(2,1)} %all-gather.15.cloned.1.call-done) | data formatting | bytes 54132736 | tf_op jit(solution)/shard_map/all_gather | solution.py:77
  223.9 11.4 slice.216
  235.3 6.2 copy-done
  249.3 12.7 reshape.407
  290.2 6.9 reshape.405
  297.1 8.6 copy.112
  322.9 9.5 multiply_reduce_fusion.5
  341.5 6.2 multiply_convert_fusion.9
  347.7 190.6 %all-gather.9.cloned.1.call-done = bf16[2560,12800]{1,0:T(8,128)(2,1)} async-done(((bf16[80,12800]{1,0:T(8,128)(2,1)}), bf16[2560,12800]{1,0:T(8,128)(2,1)}) %all-gather.9.cloned.1.call-update) | async-done | bytes 65536016 | tf_op jit(solution)/shard_map/all_gather | solution.py:156
  538.4 30.4 %fusion.83 = f32[256,12800]{1,0:T(8,128)} fusion(bf16[2560,12800]{1,0:T(8,128)(2,1)} %all-gather.9.cloned.1.call-done, f32[256,2560]{1,0:T(8,128)} %copy-done.5, f32[2560]{0:T(1024)S(1)} %reshape.431, f32[256]{0:T(256)S(1)} %add_rsqrt_fusion), kind=kOutput, calls=%fused_computation.182 | convolution fusion | flops 16779182080 | bytes 81275904 | tf_op jit(solution)/shard_map/dot_general | solution.py:23
  568.8 161.0 %all-gather.11.cloned.1.call-done = bf16[6400,2560]{1,0:T(8,128)(2,1)} async-done(((bf16[200,2560]{1,0:T(8,128)(2,1)}), bf16[6400,2560]{1,0:T(8,128)(2,1)}) %all-gather.11.cloned.1.call-update) | async-done | bytes 32768016 | tf_op jit(solution)/shard_map/all_gather | solution.py:159
  729.8 24.4 %multiply_convert_fusion.4 = (bf16[256,6400]{1,0:T(8,128)(2,1)}, bf16[256,6400]{1,0:T(8,128)(2,1)}) fusion(f32[256,12800]{1,0:T(8,128)} %fusion.83, bf16[256,2560]{1,0:T(8,128)(2,1)} %get-tuple-element.121, bf16[6400,2560]{1,0:T(8,128)(2,1)} %all-gather.11.cloned.1.call-done), kind=kOutput, calls=%fused_computation.28 | convolution fusion | flops 8409907200 | bytes 53739520 | tf_op jit(solution)/shard_map/dot_general | solution.py:33
  754.2 30.0 %multiply_reduce_fusion.1 = (f32[2560]{0:T(1024)S(1)}, f32[256]{0:T(256)S(1)}, f32[256,2560]{1,0:T(8,128)}) fusion(f32[256,2560]{1,0:T(8,128)} %copy-done.5, f32[256]{0:T(256)S(1)} %add_rsqrt_fusion, f32[2560]{0:T(1024)S(1)} %reshape.431, bf16[2560,12800]{1,0:T(8,128)(2,1)} %all-gather.9.cloned.1.call-done, bf16[256,6400]{1,0:T(8,128)(2,1)} %get-tuple-element.85, ...), kind=kOutput, calls=%fused_computation.72 | convolution fusion | flops 16794253312 | bytes 77355008 | tf_op jit(solution)/shard_map/dot_general | solution.py:33
  792.7 9.8 convolution_convert_fusion
  843.1 6.9 pad_maximum_fusion
  853.8 6.0 multiply_reduce_fusion.7
  886.8 87.5 %all-to-all-done = bf16[256,2,32,80]{0,1,3,2:T(2,128)(2,1)} async-done(((bf16[256,2,32,80]{0,1,3,2:T(2,128)(2,1)}), bf16[256,2,32,80]{0,1,3,2:T(2,128)(2,1)}, u32[]{:S(2)}, u32[]{:S(2)}) %all-to-all-start) | async-done | bytes 2621472 | tf_op jit(solution)/shard_map/all_to_all | solution.py:95
  974.3 14.3 all-to-all-start.1
  995.0 185.6 %all-to-all-done.1 = bf16[256,1,32,280]{0,3,1,2:T(8,128)(2,1)} async-done(((bf16[256,1,32,280]{0,3,1,2:T(8,128)(2,1)}), bf16[256,1,32,280]{0,3,1,2:T(8,128)(2,1)}, u32[]{:S(2)}, u32[]{:S(2)}) %all-to-all-start.1) | async-done | bytes 4587552 | tf_op jit(solution)/shard_map/all_to_all | solution.py:95
  1185.7 416.0 %all-gather.13.cloned.1.call-done = bf16[8192,8704]{1,0:T(8,128)(2,1)} async-done(((bf16[256,8704]{1,0:T(8,128)(2,1)}), bf16[8192,8704]{1,0:T(8,128)(2,1)}) %all-gather.13.cloned.1.call-update) | async-done | bytes 142606352 | tf_op jit(solution)/shard_map/all_gather | solution.py:89
  1606.1 7.3 fusion.12
  1618.6 21.1 %fusion.4 = f32[8192,200]{0,1:T(8,128)} fusion(bf16[200,2560]{1,0:T(8,128)(2,1)S(1)} %copy-done.33, bf16[8192,8704]{1,0:T(8,128)(2,1)} %all-gather.13.cloned.1.call-done), kind=kOutput, calls=%fused_computation.4 | convolution fusion | flops 8388608000 | bytes 49520640 | tf_op jit(solution)/shard_map/dot_general | solution.py:33
  1639.7 21.7 %fusion.10 = f32[8192,200]{0,1:T(8,128)} fusion(bf16[8192,8704]{1,0:T(8,128)(2,1)} %all-gather.13.cloned.1.call-done, bf16[2560,12800]{1,0:T(8,128)(2,1)} %all-gather.9.cloned.1.call-done, s32[]{:T(128)S(6)} %select_n.26), kind=kOutput, calls=%fused_computation.10 | convolution fusion | flops 8388608000 | bytes 49807364 | tf_op jit(solution)/shard_map/dot_general | solution.py:23
  1661.4 29.8 %multiply_convert_fusion.2 = (bf16[8192,200]{0,1:T(8,128)(2,1)}, bf16[8192,200]{0,1:T(8,128)(2,1)}, f32[8192,200]{0,1:T(8,128)}) fusion(f32[8192,200]{0,1:T(8,128)} %fusion.4, f32[8192,200]{0,1:T(8,128)} %fusion.10, bf16[2560,12800]{1,0:T(8,128)(2,1)} %all-gather.9.cloned.1.call-done, s32[]{:T(128)S(6)} %select_n.27, ...), kind=kOutput, calls=%fused_computation.25 | convolution fusion | flops 8409907200 | bytes 69468160 | tf_op jit(solution)/shard_map/dot_general | solution.py:23
  1691.2 27.3 %fusion.6 = f32[2560,400]{0,1:T(8,128)S(1)} fusion(bf16[8192,8704]{1,0:T(8,128)(2,1)} %all-gather.13.cloned.1.call-done, bf16[8192,200]{0,1:T(8,128)(2,1)} %get-tuple-element.87, bf16[8192,200]{0,1:T(8,128)(2,1)} %get-tuple-element.86), kind=kOutput, calls=%fused_computation.6 | convolution fusion | flops 16790323200 | bytes 52592640 | tf_op jit(solution)/shard_map/dot_general | solution.py:27
  1718.5 16.0 fusion
  1737.1 11.8 copy.143
  1759.2 24.0 %fusion.32 = bf16[256,2560]{1,0:T(8,128)(2,1)} fusion(f32[256,2560]{1,0:T(8,128)} %copy-done.5, bf16[6400,2560]{1,0:T(8,128)(2,1)} %all-gather.11.cloned.1.call-done, f32[256,12800]{1,0:T(8,128)} %fusion.83, f32[256]{0:T(256)S(1)} %copy-done.50), kind=kOutput, calls=%fused_computation.55 | convolution fusion | flops 8401059840 | bytes 49808384 | tf_op jit(solution)/shard_map/dot_general | solution.py:23
  1786.9 11.2 slice.231
  1805.2 22.6 %fusion.2 = f32[200,2560]{1,0:T(8,128)} fusion(bf16[8192,8704]{1,0:T(8,128)(2,1)} %all-gather.13.cloned.1.call-done, f32[8192,200]{0,1:T(8,128)} %fusion.10, f32[8192,200]{0,1:T(8,128)} %get-tuple-element.122), kind=kOutput, calls=%fused_computation.2 | convolution fusion | flops 8398438400 | bytes 57098240 | tf_op jit(solution)/shard_map/dot_general | solution.py:27
  1831.5 37.2 %all-to-all-done.3 = f32[2560,1,480]{2,1,0:T(1,128)} async-done(((f32[2560,1,480]{2,1,0:T(1,128)}), f32[2560,1,480]{2,1,0:T(1,128)}, u32[]{:S(2)}, u32[]{:S(2)}) %all-to-all-start.3) | async-done | bytes 4915232 | tf_op jit(solution)/shard_map/all_to_all | solution.py:101
  (279 shorter events, 238.0 us)
Async XLA Ops:
  7.2 15.5 copy-start.34
  7.2 181.4 %all-gather.15.cloned.1.call-start = ((), (), s32[]{:S(2)}) async-start(), calls=%async_computation.7 | async-start | bytes 27912192 | tf_op jit(solution)/shard_map/all_gather | solution.py:77
  22.7 515.7 %all-gather.9.cloned.1.call-start = ((), (), s32[]{:S(2)}) async-start(), calls=%async_computation.4 | async-start | bytes 67584000 | tf_op jit(solution)/shard_map/all_gather | solution.py:156
  25.5 704.3 %all-gather.11.cloned.1.call-start = ((), (), s32[]{:S(2)}) async-start(), calls=%async_computation.5 | async-start | bytes 33792000 | tf_op jit(solution)/shard_map/all_gather | solution.py:159
  26.2 1575.5 %all-gather.13.cloned.1.call-start = ((), (), s32[]{:S(2)}) async-start(), calls=%async_computation.6 | async-start | bytes 147062784 | tf_op jit(solution)/shard_map/all_gather | solution.py:89
  29.5 831.8 %copy-start.41 = (f32[256]{0:T(256)}, f32[256]{0:T(256)S(1)}, u32[]{:S(2)}) copy-start(f32[256]{0:T(256)S(1)} %get-tuple-element.104) | copy-start | bytes 3076
  223.9 17.6 copy-start
  249.3 13.5 slice-start
  262.8 5.5 copy-start.35
  266.5 6.4 slice-start.1
  271.7 8.2 copy-start.22
  272.6 7.4 copy-start.43
  272.7 7.3 copy-start.45
  282.6 34.3 %copy-start.11 = (bf16[2,128,40,128]{1,3,2,0:T(8,128)(2,1)}, bf16[2,128,40,128]{1,3,2,0:T(8,128)(2,1)S(1)}, u32[]{:S(2)}) copy-start(bf16[2,128,40,128]{1,3,2,0:T(8,128)(2,1)S(1)} %convolution_convert_fusion.1) | copy-start | bytes 7864324
  284.7 25.0 %copy-start.38 = (f32[768]{0:T(1024)}, f32[768]{0:T(1024)S(1)}, u32[]{:S(2)}) copy-start(f32[768]{0:T(1024)S(1)} %reshape.429) | copy-start | bytes 9220
  305.7 5.0 copy-start.6
  322.9 9.5 copy-start.14
  806.8 9.8 slice-start.2
  850.0 124.3 %all-to-all-start = ((bf16[256,2,32,80]{0,1,3,2:T(2,128)(2,1)}), bf16[256,2,32,80]{0,1,3,2:T(2,128)(2,1)}, u32[]{:S(2)}, u32[]{:S(2)}) async-start(bf16[256,2,32,80]{0,1,3,2:T(2,128)(2,1)} %pad_maximum_fusion), calls=%async_computation | async-start | bytes 5242880 | tf_op jit(solution)/shard_map/all_to_all | solution.py:95
  853.7 929.5 %all-gather.17.cloned.1.call-start = ((), (), s32[]{:S(2)}) async-start(), calls=%async_computation.8 | async-start | bytes 20680704 | tf_op jit(solution)/shard_map/all_gather | solution.py:325
  853.8 6.2 copy-start.9
  872.9 5.7 copy-start.12
  974.3 206.4 %all-to-all-start.1 = ((bf16[256,1,32,280]{0,3,1,2:T(8,128)(2,1)}), bf16[256,1,32,280]{0,3,1,2:T(8,128)(2,1)}, u32[]{:S(2)}, u32[]{:S(2)}) async-start(bf16[256,1,32,280]{0,3,1,2:T(8,128)(2,1)} %maximum_bitcast_fusion.1), calls=%async_computation.1 | async-start | bytes 9175040 | tf_op jit(solution)/shard_map/all_to_all | solution.py:95
  1613.5 5.1 copy-start.33
  1615.1 133.8 %all-to-all-start.2 = ((f32[32,1,4160]{2,1,0:T(1,128)}), f32[32,1,4160]{2,1,0:T(1,128)}, u32[]{:S(2)}, u32[]{:S(2)}) async-start(f32[32,1,4160]{2,1,0:T(1,128)} %copy.140), calls=%async_computation.2 | async-start | bytes 1081344 | tf_op jit(solution)/shard_map/all_to_all | solution.py:101
  1691.2 27.3 %copy-start.26 = (bf16[8192,2,80]{0,2,1:T(8,128)(2,1)S(1)}, bf16[8192,2,80]{0,2,1:T(8,128)(2,1)}, u32[]{:S(2)}) copy-start(bf16[8192,2,80]{0,2,1:T(8,128)(2,1)} %reshape.414) | copy-start | bytes 7864324
  1748.9 5.5 copy-start.51
  1748.9 5.5 copy-start.4
  1748.9 5.5 copy-start.37
  1748.9 5.5 copy-start.42
  1749.0 119.8 %all-to-all-start.3 = ((f32[2560,1,480]{2,1,0:T(1,128)}), f32[2560,1,480]{2,1,0:T(1,128)}, u32[]{:S(2)}, u32[]{:S(2)}) async-start(f32[2560,1,480]{2,1,0:T(1,128)} %copy.143), calls=%async_computation.3 | async-start | bytes 10485760 | tf_op jit(solution)/shard_map/all_to_all | solution.py:101
  1786.9 11.8 copy-start.27
  (34 other events, 98.7 us)
Sparse Core Ops, SparseCore 0:
  22.8 165.7 all-gather.14
  192.0 346.2 all-gather.8
  541.2 188.5 all-gather.10
  732.6 869.0 all-gather.12
  1604.9 137.1 all-gather.16

commit v8 on v7

--- a/solution.py
+++ b/solution.py
@@ -102,6 +102,14 @@
     return moved.reshape(rows // devices, count, devices, share).reshape(
         rows // devices, count, devices * share
     )
+
+
+def interleave(first, second, devices):
+    rows, width = first.shape
+    share = width // devices
+    return jnp.stack(
+        [first.reshape(rows, devices, share), second.reshape(rows, devices, share)], axis=2
+    ).reshape(rows, 2 * width)
 
 
 def split_exact(values):
@@ -153,8 +161,9 @@
         gain_latent,
         gain_two,
     ) = gather_packed(attn_shards)
+    ff_share = ffn // devices
     weight_gate_up = lax.all_gather(
-        jnp.concatenate([gate_weight, up_weight], axis=1), AXES, axis=0, tiled=True
+        interleave(gate_weight, up_weight, devices), AXES, axis=0, tiled=True
     )
     weight_down = lax.all_gather(down_weight, AXES, axis=0, tiled=True)
     half = ROPE // 2
@@ -203,9 +212,9 @@
     middle = inputs + depth_scale * matmul(attended, weight_out)
     normed_two, inverse_two = normalize(middle)
     h_two = (normed_two * gain_two.astype(jnp.float32)).astype(jnp.bfloat16)
-    gate_up = matmul(h_two, weight_gate_up)
-    gate = gate_up[:, :ffn]
-    upward = gate_up[:, ffn:]
+    gate_up = matmul(h_two, weight_gate_up).reshape(rows, devices, 2, ff_share)
+    gate = gate_up[:, :, 0].reshape(rows, ffn)
+    upward = gate_up[:, :, 1].reshape(rows, ffn)
     sigma = jax.nn.sigmoid(gate)
     hidden = (gate * sigma * upward).astype(jnp.bfloat16)
     result = (middle + depth_scale * matmul(hidden, weight_down)) * valid_rows
@@ -223,16 +232,16 @@
     grad_hidden = back_product(grad_feed, weight_down)
     grad_gate = (grad_hidden * upward * sigma * (1.0 + gate * (1.0 - sigma))).astype(jnp.bfloat16)
     grad_up = (grad_hidden * gate * sigma).astype(jnp.bfloat16)
-    grad_h_two = back_product(jnp.concatenate([grad_gate, grad_up], axis=1), weight_gate_up)
+    grad_h_two = back_product(interleave(grad_gate, grad_up, devices), weight_gate_up)
     gain_two_term, grad_middle_norm = norm_back(grad_h_two, normed_two, inverse_two, gain_two)
     grad_middle = grad_out + grad_middle_norm
     grad_attn = (depth_scale * grad_middle).astype(jnp.bfloat16)
-    ff_share = ffn // devices
     attn_share = width // devices
-    gate_c = matmul(h_two_all, lax.dynamic_slice_in_dim(weight_gate_up, me * ff_share, ff_share, 1))
-    up_c = matmul(
-        h_two_all, lax.dynamic_slice_in_dim(weight_gate_up, ffn + me * ff_share, ff_share, 1)
-    )
+    gate_up_c = matmul(
+        h_two_all, lax.dynamic_slice_in_dim(weight_gate_up, me * 2 * ff_share, 2 * ff_share, 1)
+    )
+    gate_c = gate_up_c[:, :ff_share]
+    up_c = gate_up_c[:, ff_share:]
     sigma_c = jax.nn.sigmoid(gate_c)
     hidden_c = (gate_c * sigma_c * up_c).astype(jnp.bfloat16)
     grad_hidden_c = back_product(grad_feed_all, down_weight)

time: 1910 us -> 1890 us (0.990)
  waiting for transfers between devices: 1240 us -> 1160 us
  local copies, waits for them, and re-layouts: 248 us -> 310 us
  matrix products: 322 us -> 301 us
    another operation x1 -> x6, local copies, waits for them, and re-layouts: 0.1 us -> 35.1 us  [the longest x3 18.6 us: interleave(): jnp.stack([first.reshape(rows, devices, share), second.reshape(rows, devi...]
    all_gather x1, waiting for transfers between devices: 161 us -> 129 us  [local(): weight_down = lax.all_gather(down_weight, AXES, axis=0, tiled=True)]
    all_gather x1, waiting for transfers between devices: 158 us -> 132 us  [gather_packed(): gathered = lax.all_gather(jnp.concatenate(flat), AXES, axis=0, tiled=False)]
    dot_general x9 -> x8, matrix products: 126 us -> 103 us  [matmul(): return jnp.dot(left, right, preferred_element_type=jnp.float32)]
  transfers between devices with their start and end apart: 9 -> 9, of which waited for: 7 -> 7; matrix products, arithmetic and copies ran while one was open for 30% -> 33% of each run, Pallas kernels for 0% -> 0%
where the time goes in v8:
time: 1890 us; the launch traced here: 1880 us
  waiting for transfers between devices  1160 us (61%)
  local copies, waits for them, and re-layouts  310 us (16%)
  matrix products  301 us (16%)
  other arithmetic  59.6 us (3%)
  starting transfers between devices  28.1 us (1%)
    all_gather x1, waiting for transfers between devices, gather_tokens(): return lax.all_gather(values, AXES, axis=0, tiled=True)  397 us
    all_to_all x2, waiting for transfers between devices, column_shares(): moved = lax.all_to_all(blocks, AXES, 2, 0, tiled=True)  274 us
    all_gather x1, waiting for transfers between devices, local(): lax.all_gather(interleave(gate_weight, up_weight, devices), AXES, axis=0,...  189 us
    all_gather x1, waiting for transfers between devices, gather_packed(): gathered = lax.all_gather(jnp.concatenate(flat), AXES, axis=0, tiled=False)  132 us
    all_gather x1, waiting for transfers between devices, local(): weight_down = lax.all_gather(down_weight, AXES, axis=0, tiled=True)  129 us
    dot_general x8, matrix products, matmul(): return jnp.dot(left, right, preferred_element_type=jnp.float32)  103 us
    dot_general x8, matrix products, back_product(): lax.dot_general(left, right, (((1,), (1,)), ((), ())), preferred_element_...  102 us
    dot_general x7, matrix products, rows_product(): lax.dot_general(left, right, (((0,), (0,)), ((), ())), preferred_element_...  84 us
  transfers between devices with their start and end apart: 9, of which 7 were waited for; matrix products, arithmetic and copies ran while one was open for 33% of the time, Pallas kernels for 0%

profile of v8, /device:TPU:0, one launch (start us, length us, event | category | flops | bytes accessed | tf_op | source)
XLA Modules:
  0.0 1878.4 jit_solution(4798807762931820318)
XLA Ops:
  29.6 8.3 stack_reshape.16
  37.9 8.3 pad_maximum_fusion.1
  57.0 131.5 %all-gather.15.cloned.1.call-done = bf16[13533184]{0:T(1024)(128)(2,1)} async-done(((bf16[422912]{0:T(1024)(128)(2,1)}), bf16[13533184]{0:T(1024)(128)(2,1)}) %all-gather.15.cloned.1.call-update) | async-done | bytes 27066384 | tf_op jit(solution)/shard_map/all_gather | solution.py:77
  188.5 35.4 %reshape.447 = bf16[32,422912]{1,0:T(8,128)(2,1)} reshape(bf16[13533184]{0:T(1024)(128)(2,1)} %all-gather.15.cloned.1.call-done) | data formatting | bytes 54132736 | tf_op jit(solution)/shard_map/all_gather | solution.py:77
  223.9 11.4 slice.224
  249.2 12.7 reshape.416
  298.1 8.7 copy.136
  324.0 9.5 multiply_reduce_fusion.5
  349.0 189.3 %all-gather.9.cloned.1.call-done = bf16[2560,12800]{1,0:T(8,128)(2,1)} async-done(((bf16[80,12800]{1,0:T(8,128)(2,1)}), bf16[2560,12800]{1,0:T(8,128)(2,1)}) %all-gather.9.cloned.1.call-update) | async-done | bytes 65536016 | tf_op jit(solution)/shard_map/all_gather | solution.py:165
  538.3 35.8 %fusion.74 = f32[256,12800]{0,1:T(8,128)} fusion(bf16[2560,12800]{1,0:T(8,128)(2,1)} %all-gather.9.cloned.1.call-done, f32[256,2560]{1,0:T(8,128)S(1)} %copy-done.7, f32[2560]{0:T(1024)S(1)} %reshape.443, f32[256]{0:T(256)S(1)} %add_rsqrt_fusion), kind=kOutput, calls=%fused_computation.174 | convolution fusion | flops 16779182080 | bytes 81275904 | tf_op jit(solution)/shard_map/dot_general | solution.py:23
  574.1 10.5 fusion.76
  584.6 8.2 copy.146
  592.8 8.2 copy.145
  601.0 128.8 %all-gather.11.cloned.1.call-done = bf16[6400,2560]{1,0:T(8,128)(2,1)} async-done(((bf16[200,2560]{1,0:T(8,128)(2,1)}), bf16[6400,2560]{1,0:T(8,128)(2,1)}) %all-gather.11.cloned.1.call-update) | async-done | bytes 32768016 | tf_op jit(solution)/shard_map/all_gather | solution.py:168
  729.7 24.5 %multiply_convert_fusion.4 = (bf16[256,6400]{1,0:T(8,128)(2,1)}, bf16[256,6400]{1,0:T(8,128)(2,1)}) fusion(f32[256,6400]{1,0:T(8,128)} %copy.145, f32[256,6400]{1,0:T(8,128)} %copy.146, bf16[256,2560]{1,0:T(8,128)(2,1)} %get-tuple-element.123, bf16[6400,2560]{1,0:T(8,128)(2,1)} %all-gather.11.cloned.1.call-done), kind=kOutput, calls=%fused_computation.23 | convolution fusion | flops 8409907200 | bytes 53739520 | tf_op jit(solution)/shard_map/dot_general | solution.py:33
  772.3 28.8 %multiply_reduce_fusion.1 = (f32[2560]{0:T(1024)S(1)}, f32[256]{0:T(256)S(1)}, f32[256,2560]{1,0:T(8,128)}) fusion(f32[256,2560]{1,0:T(8,128)S(1)} %copy-done.7, f32[256]{0:T(256)S(1)} %add_rsqrt_fusion, f32[2560]{0:T(1024)S(1)} %reshape.443, bf16[256,12800]{0,1:T(8,128)(2,1)} %bitcast.195, bf16[2560,12800]{1,0:T(8,128)(2,1)} %all-gather.9.cloned.1.call-done), kind=kOutput, calls=%fused_computation.69 | convolution fusion | flops 16781146112 | bytes 77355008 | tf_op jit(solution)/shard_map/dot_general | solution.py:33
  808.6 8.8 convolution_convert_fusion
  869.8 8.5 pad_maximum_fusion.2
  900.1 105.9 %all-to-all-done = bf16[256,2,32,80]{0,1,3,2:T(2,128)(2,1)} async-done(((bf16[256,2,32,80]{0,1,3,2:T(2,128)(2,1)}), bf16[256,2,32,80]{0,1,3,2:T(2,128)(2,1)}, u32[]{:S(2)}, u32[]{:S(2)}) %all-to-all-start) | async-done | bytes 2621472 | tf_op jit(solution)/shard_map/all_to_all | solution.py:95
  1006.0 14.3 all-to-all-start.1
  1026.8 168.3 %all-to-all-done.1 = bf16[256,1,32,280]{0,3,1,2:T(8,128)(2,1)} async-done(((bf16[256,1,32,280]{0,3,1,2:T(8,128)(2,1)}), bf16[256,1,32,280]{0,3,1,2:T(8,128)(2,1)}, u32[]{:S(2)}, u32[]{:S(2)}) %all-to-all-start.1) | async-done | bytes 4587552 | tf_op jit(solution)/shard_map/all_to_all | solution.py:95
  1200.5 397.5 %all-gather.13.cloned.1.call-done = bf16[8192,8704]{1,0:T(8,128)(2,1)} async-done(((bf16[256,8704]{1,0:T(8,128)(2,1)}), bf16[8192,8704]{1,0:T(8,128)(2,1)}) %all-gather.13.cloned.1.call-update) | async-done | bytes 142606352 | tf_op jit(solution)/shard_map/all_gather | solution.py:89
  1602.5 7.3 fusion.10
  1615.0 25.9 %fusion.4 = f32[8192,400]{0,1:T(8,128)} fusion(bf16[8192,8704]{1,0:T(8,128)(2,1)} %all-gather.13.cloned.1.call-done, bf16[2560,12800]{1,0:T(8,128)(2,1)} %all-gather.9.cloned.1.call-done, s32[]{:T(128)S(6)} %select_n.23), kind=kOutput, calls=%fused_computation.4 | convolution fusion | flops 16777216000 | bytes 57671684 | tf_op jit(solution)/shard_map/dot_general | solution.py:23
  1640.9 24.8 %multiply_convert_fusion.2 = (bf16[8192,200]{0,1:T(8,128)(2,1)}, bf16[8192,200]{0,1:T(8,128)(2,1)}) fusion(f32[8192,400]{0,1:T(8,128)} %fusion.4, bf16[200,2560]{1,0:T(8,128)(2,1)S(1)} %copy-done.34, bf16[8192,8704]{1,0:T(8,128)(2,1)} %all-gather.13.cloned.1.call-done), kind=kOutput, calls=%fused_computation.20 | convolution fusion | flops 8409907200 | bytes 62627840 | tf_op jit(solution)/shard_map/dot_general | solution.py:33
  1665.7 27.0 %fusion.2 = f32[2560,400]{0,1:T(8,128)S(1)} fusion(bf16[8192,8704]{1,0:T(8,128)(2,1)} %all-gather.13.cloned.1.call-done, bf16[8192,200]{0,1:T(8,128)(2,1)} %get-tuple-element.85, bf16[8192,200]{0,1:T(8,128)(2,1)} %get-tuple-element.84), kind=kOutput, calls=%fused_computation.2 | convolution fusion | flops 16790323200 | bytes 52592640 | tf_op jit(solution)/shard_map/dot_general | solution.py:27
  1692.7 15.9 fusion
  1711.1 11.7 copy.179
  1733.8 21.6 %fusion.26 = bf16[256,2560]{1,0:T(8,128)(2,1)} fusion(f32[256,2560]{1,0:T(8,128)} %copy-done.6, bf16[6400,2560]{1,0:T(8,128)(2,1)} %all-gather.11.cloned.1.call-done, f32[256,6400]{1,0:T(8,128)} %copy.146, f32[256,6400]{1,0:T(8,128)} %copy.145, f32[256]{0:T(256)S(1)} %copy-done.54), kind=kOutput, calls=%fused_computation.50 | convolution fusion | flops 8401059840 | bytes 49808384 | tf_op jit(solution)/shard_map/dot_general | solution.py:23
  1759.0 10.9 slice.239
  1777.1 23.0 %fusion.6 = f32[200,2560]{1,0:T(8,128)} fusion(bf16[8192,8704]{1,0:T(8,128)(2,1)} %all-gather.13.cloned.1.call-done, f32[8192,400]{0,1:T(8,128)} %fusion.4), kind=kOutput, calls=%fused_computation.6 | convolution fusion | flops 8398438400 | bytes 57098240 | tf_op jit(solution)/shard_map/dot_general | solution.py:27
  1803.7 42.1 %all-to-all-done.3 = f32[2560,1,480]{2,1,0:T(1,128)} async-done(((f32[2560,1,480]{2,1,0:T(1,128)}), f32[2560,1,480]{2,1,0:T(1,128)}, u32[]{:S(2)}, u32[]{:S(2)}) %all-to-all-start.3) | async-done | bytes 4915232 | tf_op jit(solution)/shard_map/all_to_all | solution.py:101
  (296 shorter events, 290.0 us)
Async XLA Ops:
  7.2 181.3 %all-gather.15.cloned.1.call-start = ((), (), s32[]{:S(2)}) async-start(), calls=%async_computation.7 | async-start | bytes 27912192 | tf_op jit(solution)/shard_map/all_gather | solution.py:77
  22.6 515.7 %all-gather.9.cloned.1.call-start = ((), (), s32[]{:S(2)}) async-start(), calls=%async_computation.4 | async-start | bytes 67584000 | tf_op jit(solution)/shard_map/all_gather | solution.py:165
  46.3 8.3 copy-start.2
  53.6 676.2 %all-gather.11.cloned.1.call-start = ((), (), s32[]{:S(2)}) async-start(), calls=%async_computation.5 | async-start | bytes 33792000 | tf_op jit(solution)/shard_map/all_gather | solution.py:168
  54.3 1543.7 %all-gather.13.cloned.1.call-start = ((), (), s32[]{:S(2)}) async-start(), calls=%async_computation.6 | async-start | bytes 147062784 | tf_op jit(solution)/shard_map/all_gather | solution.py:89
  56.8 744.3 %copy-start.53 = (f32[256]{0:T(256)}, f32[256]{0:T(256)S(1)}, u32[]{:S(2)}) copy-start(f32[256]{0:T(256)S(1)} %fusion.64) | copy-start | bytes 3076
  56.8 285.8 %copy-start.44 = (f32[256]{0:T(256)}, f32[256]{0:T(256)S(1)}, u32[]{:S(2)}) copy-start(f32[256]{0:T(256)S(1)} %get-tuple-element.106) | copy-start | bytes 3076
  56.9 256.9 %copy-start.35 = (f32[128,16]{0,1:T(8,128)}, f32[128,16]{0,1:T(8,128)S(1)}, u32[]{:S(2)}) copy-start(f32[128,16]{0,1:T(8,128)S(1)} %get-tuple-element.108) | copy-start | bytes 24580
  56.9 256.9 %copy-start.37 = (f32[128,16]{0,1:T(8,128)}, f32[128,16]{0,1:T(8,128)S(1)}, u32[]{:S(2)}) copy-start(f32[128,16]{0,1:T(8,128)S(1)} %get-tuple-element.109) | copy-start | bytes 24580
  223.9 17.6 copy-start
  249.2 13.5 slice-start
  266.3 7.5 slice-start.1
  271.6 9.3 copy-start.21
  283.5 34.5 %copy-start.11 = (bf16[2,128,40,128]{1,3,2,0:T(8,128)(2,1)}, bf16[2,128,40,128]{1,3,2,0:T(8,128)(2,1)S(1)}, u32[]{:S(2)}) copy-start(bf16[2,128,40,128]{1,3,2,0:T(8,128)(2,1)S(1)} %convolution_convert_fusion.1) | copy-start | bytes 7864324
  285.6 25.1 %copy-start.42 = (f32[768]{0:T(1024)}, f32[768]{0:T(1024)S(1)}, u32[]{:S(2)}) copy-start(f32[768]{0:T(1024)S(1)} %reshape.441) | copy-start | bytes 9220
  324.0 9.5 copy-start.13
  339.2 1416.2 %all-gather.17.cloned.1.call-start = ((), (), s32[]{:S(2)}) async-start(), calls=%async_computation.8 | async-start | bytes 20680704 | tf_op jit(solution)/shard_map/all_gather | solution.py:334
  342.6 195.7 %copy-start.7 = (f32[256,2560]{1,0:T(8,128)S(1)}, f32[256,2560]{1,0:T(8,128)}, u32[]{:S(2)}) copy-start(f32[256,2560]{1,0:T(8,128)} %copy-done.6) | copy-start | bytes 7864324
  820.0 8.9 slice-start.2
  847.4 6.9 copy-start.24
  847.4 7.5 copy-start.10
  878.3 127.8 %all-to-all-start = ((bf16[256,2,32,80]{0,1,3,2:T(2,128)(2,1)}), bf16[256,2,32,80]{0,1,3,2:T(2,128)(2,1)}, u32[]{:S(2)}, u32[]{:S(2)}) async-start(bf16[256,2,32,80]{0,1,3,2:T(2,128)(2,1)} %pad_maximum_fusion.2), calls=%async_computation | async-start | bytes 5242880 | tf_op jit(solution)/shard_map/all_to_all | solution.py:95
  1006.0 189.0 %all-to-all-start.1 = ((bf16[256,1,32,280]{0,3,1,2:T(8,128)(2,1)}), bf16[256,1,32,280]{0,3,1,2:T(8,128)(2,1)}, u32[]{:S(2)}, u32[]{:S(2)}) async-start(bf16[256,1,32,280]{0,3,1,2:T(8,128)(2,1)} %maximum_bitcast_fusion.1), calls=%async_computation.1 | async-start | bytes 9175040 | tf_op jit(solution)/shard_map/all_to_all | solution.py:95
  1611.4 111.4 %all-to-all-start.2 = ((f32[32,1,4160]{2,1,0:T(1,128)}), f32[32,1,4160]{2,1,0:T(1,128)}, u32[]{:S(2)}, u32[]{:S(2)}) async-start(f32[32,1,4160]{2,1,0:T(1,128)} %copy.176), calls=%async_computation.2 | async-start | bytes 1081344 | tf_op jit(solution)/shard_map/all_to_all | solution.py:101
  1615.0 25.9 %copy-start.34 = (bf16[200,2560]{1,0:T(8,128)(2,1)S(1)}, bf16[200,2560]{1,0:T(8,128)(2,1)}, u32[]{:S(2)}) copy-start(bf16[200,2560]{1,0:T(8,128)(2,1)} %param.28) | copy-start | bytes 3072004
  1665.7 27.0 %copy-start.27 = (bf16[8192,2,80]{0,2,1:T(8,128)(2,1)S(1)}, bf16[8192,2,80]{0,2,1:T(8,128)(2,1)}, u32[]{:S(2)}) copy-start(bf16[8192,2,80]{0,2,1:T(8,128)(2,1)} %reshape.426) | copy-start | bytes 7864324
  1722.8 6.2 copy-start.55
  1722.8 6.2 copy-start.5
  1722.8 6.2 copy-start.41
  1722.8 6.2 copy-start.46
  1722.8 123.0 %all-to-all-start.3 = ((f32[2560,1,480]{2,1,0:T(1,128)}), f32[2560,1,480]{2,1,0:T(1,128)}, u32[]{:S(2)}, u32[]{:S(2)}) async-start(f32[2560,1,480]{2,1,0:T(1,128)} %copy.179), calls=%async_computation.3 | async-start | bytes 10485760 | tf_op jit(solution)/shard_map/all_to_all | solution.py:101
  1759.0 11.5 copy-start.28
  (38 other events, 102.3 us)
Sparse Core Ops, SparseCore 0:
  22.7 165.7 all-gather.14
  191.9 346.2 all-gather.8
  541.1 188.5 all-gather.10
  732.5 865.5 all-gather.12
  1601.2 142.7 all-gather.16

commit v9 on v8

--- a/solution.py
+++ b/solution.py
@@ -251,15 +251,11 @@
     grad_up_c = (grad_hidden_c * gate_c * sigma_c).astype(jnp.bfloat16)
     down_grad = rows_product(hidden_c, grad_feed_all)
     gate_up_cols = rows_product(h_two_all, jnp.concatenate([grad_gate_c, grad_up_c], axis=1))
-    inner_cols = column_shares(jnp.stack([h_one, grad_attn], axis=1), devices)
-    h_one_cols = inner_cols[:, 0]
-    out_cols = rows_product(attended_all, inner_cols[:, 1])
-    wide_rows = rows_from_columns(
-        jnp.concatenate([gate_up_cols, out_cols], axis=1)[:, None, :], devices
-    ).reshape(width // devices, devices, 2 * ff_share + attn_share)
+    wide_rows = rows_from_columns(gate_up_cols[:, None, :], devices).reshape(
+        width // devices, devices, 2 * ff_share
+    )
     gate_grad = wide_rows[:, :, :ff_share].reshape(width // devices, ffn)
-    up_grad = wide_rows[:, :, ff_share : 2 * ff_share].reshape(width // devices, ffn)
-    output_weight_grad = wide_rows[:, :, 2 * ff_share :].reshape(width // devices, width)
+    up_grad = wide_rows[:, :, ff_share:].reshape(width // devices, ffn)
     grad_heads = (
         back_product(grad_attn, weight_out).astype(jnp.bfloat16).reshape(micro, slot, HEADS, VDIM)
     )
@@ -310,14 +306,19 @@
             [
                 grad_query_raw.reshape(rows, devices, query_width // devices),
                 grad_kv.reshape(rows, devices, kv_width // devices),
+                h_one.reshape(rows, devices, attn_share),
+                grad_attn.reshape(rows, devices, attn_share),
             ],
             axis=2,
-        ).reshape(rows, 1, query_width + kv_width),
+        ).reshape(rows, 1, query_width + kv_width + 2 * width),
         devices,
     )[:, 0]
+    inner_at = (query_width + kv_width) // devices
+    h_one_cols = up_cols[:, inner_at : inner_at + attn_share]
+    out_cols = rows_product(attended_all, up_cols[:, inner_at + attn_share :])
     query_cols = query_width // devices
     query_up_cols = rows_product(query_low_all, up_cols[:, :query_cols])
-    latent_up_cols = rows_product(latent_low_all, up_cols[:, query_cols:])
+    latent_up_cols = rows_product(latent_low_all, up_cols[:, query_cols:inner_at])
     grad_h_one = back_product(grad_latent_all, down_latent) + back_product(
         grad_latent_query, down_query
     )
@@ -349,6 +350,7 @@
             [
                 query_up_cols.reshape(devices, -1),
                 latent_up_cols.reshape(devices, -1),
+                out_cols.reshape(devices, -1),
             ],
             axis=1,
         ).reshape(devices, 1, -1),
@@ -364,11 +366,18 @@
         .transpose(1, 0, 2)
         .reshape(q_rows, query_width)
     )
+    kv_end = q_rows * query_cols + kv_rows * kv_cols
     latent_up_grad = (
-        up_rows[:, q_rows * query_cols :]
+        up_rows[:, q_rows * query_cols : kv_end]
         .reshape(devices, kv_rows, kv_cols)
         .transpose(1, 0, 2)
         .reshape(kv_rows, kv_width)
+    )
+    output_weight_grad = (
+        up_rows[:, kv_end:]
+        .reshape(devices, width // devices, attn_share)
+        .transpose(1, 0, 2)
+        .reshape(width // devices, width)
     )
 
     def own(vector, offset, size):

time: 1890 us -> 1890 us (level)
  waiting for transfers between devices: 1160 us -> 1200 us
    all_to_all x2 -> x1, waiting for transfers between devices: 274 us -> 292 us  [column_shares(): moved = lax.all_to_all(blocks, AXES, 2, 0, tiled=True)]
  transfers between devices with their start and end apart: 9 -> 8, of which waited for: 7 -> 7; matrix products, arithmetic and copies ran while one was open for 33% -> 32% of each run, Pallas kernels for 0% -> 0%
where the time goes in v9:
time: 1890 us; the launch traced here: 1880 us
  waiting for transfers between devices  1200 us (63%)
  matrix products  306 us (16%)
  local copies, waits for them, and re-layouts  302 us (16%)
  other arithmetic  47.1 us (2%)
    all_gather x1, waiting for transfers between devices, gather_tokens(): return lax.all_gather(values, AXES, axis=0, tiled=True)  394 us
    all_to_all x1, waiting for transfers between devices, column_shares(): moved = lax.all_to_all(blocks, AXES, 2, 0, tiled=True)  292 us
    all_gather x1, waiting for transfers between devices, local(): lax.all_gather(interleave(gate_weight, up_weight, devices), AXES, axis=0,...  201 us
    all_gather x1, waiting for transfers between devices, gather_packed(): gathered = lax.all_gather(jnp.concatenate(flat), AXES, axis=0, tiled=False)  131 us
    all_gather x1, waiting for transfers between devices, local(): weight_down = lax.all_gather(down_weight, AXES, axis=0, tiled=True)  129 us
    dot_general x8, matrix products, matmul(): return jnp.dot(left, right, preferred_element_type=jnp.float32)  103 us
    dot_general x8, matrix products, back_product(): lax.dot_general(left, right, (((1,), (1,)), ((), ())), preferred_element_...  99.8 us
    dot_general x7, matrix products, rows_product(): lax.dot_general(left, right, (((0,), (0,)), ((), ())), preferred_element_...  91.5 us
  transfers between devices with their start and end apart: 8, of which 7 were waited for; matrix products, arithmetic and copies ran while one was open for 32% of the time, Pallas kernels for 0%

profile of v9, /device:TPU:0, one launch (start us, length us, event | category | flops | bytes accessed | tf_op | source)
XLA Modules:
  0.0 1882.3 jit_solution(8365558392948461206)
XLA Ops:
  29.6 8.3 stack_reshape.16
  37.9 8.3 pad_maximum_fusion.1
  46.3 7.3 reshape.395
  57.6 130.9 %all-gather.15.cloned.1.call-done = bf16[13533184]{0:T(1024)(128)(2,1)} async-done(((bf16[422912]{0:T(1024)(128)(2,1)}), bf16[13533184]{0:T(1024)(128)(2,1)}) %all-gather.15.cloned.1.call-update) | async-done | bytes 27066384 | tf_op jit(solution)/shard_map/all_gather | solution.py:77
  188.5 35.4 %reshape.427 = bf16[32,422912]{1,0:T(8,128)(2,1)} reshape(bf16[13533184]{0:T(1024)(128)(2,1)} %all-gather.15.cloned.1.call-done) | data formatting | bytes 54132736 | tf_op jit(solution)/shard_map/all_gather | solution.py:77
  224.0 11.4 slice.224
  249.2 12.7 reshape.394
  298.1 8.6 copy.133
  322.9 9.7 multiply_reduce_fusion.5
  337.7 200.5 %all-gather.9.cloned.1.call-done = bf16[2560,12800]{1,0:T(8,128)(2,1)} async-done(((bf16[80,12800]{1,0:T(8,128)(2,1)}), bf16[2560,12800]{1,0:T(8,128)(2,1)}) %all-gather.9.cloned.1.call-update) | async-done | bytes 65536016 | tf_op jit(solution)/shard_map/all_gather | solution.py:165
  538.3 35.9 %fusion.82 = f32[256,12800]{0,1:T(8,128)} fusion(bf16[2560,12800]{1,0:T(8,128)(2,1)} %all-gather.9.cloned.1.call-done, f32[256,2560]{1,0:T(8,128)S(1)} %get-tuple-element.115, f32[2560]{0:T(1024)S(1)} %reshape.423, f32[256]{0:T(256)S(1)} %add_rsqrt_fusion), kind=kOutput, calls=%fused_computation.173 | convolution fusion | flops 16779182080 | bytes 81275904 | tf_op jit(solution)/shard_map/dot_general | solution.py:23
  574.1 10.6 fusion.84
  584.8 8.2 copy.143
  593.0 8.2 copy.142
  601.2 128.5 %all-gather.11.cloned.1.call-done = bf16[6400,2560]{1,0:T(8,128)(2,1)} async-done(((bf16[200,2560]{1,0:T(8,128)(2,1)}), bf16[6400,2560]{1,0:T(8,128)(2,1)}) %all-gather.11.cloned.1.call-update) | async-done | bytes 32768016 | tf_op jit(solution)/shard_map/all_gather | solution.py:168
  729.7 24.5 %multiply_convert_fusion.4 = (bf16[256,6400]{1,0:T(8,128)(2,1)}, bf16[256,6400]{1,0:T(8,128)(2,1)}) fusion(f32[256,6400]{1,0:T(8,128)} %copy.142, f32[256,6400]{1,0:T(8,128)} %copy.143, bf16[256,2560]{1,0:T(8,128)(2,1)} %get-tuple-element.123, bf16[6400,2560]{1,0:T(8,128)(2,1)} %all-gather.11.cloned.1.call-done), kind=kOutput, calls=%fused_computation.24 | convolution fusion | flops 8409907200 | bytes 53739520 | tf_op jit(solution)/shard_map/dot_general | solution.py:33
  772.3 28.8 %multiply_reduce_fusion.1 = (f32[2560]{0:T(1024)S(1)}, f32[256]{0:T(256)S(1)}, f32[256,2560]{1,0:T(8,128)}) fusion(f32[256,2560]{1,0:T(8,128)S(1)} %get-tuple-element.115, f32[256]{0:T(256)S(1)} %add_rsqrt_fusion, f32[2560]{0:T(1024)S(1)} %reshape.423, bf16[256,12800]{0,1:T(8,128)(2,1)} %bitcast.185, bf16[2560,12800]{1,0:T(8,128)(2,1)} %all-gather.9.cloned.1.call-done), kind=kOutput, calls=%fused_computation.68 | convolution fusion | flops 16781146112 | bytes 77355008 | tf_op jit(solution)/shard_map/dot_general | solution.py:33
  806.8 8.4 convolution_convert_fusion
  901.3 291.9 %all-to-all-done = bf16[256,1,32,440]{0,3,1,2:T(8,128)(2,1)} async-done(((bf16[256,1,32,440]{0,3,1,2:T(8,128)(2,1)}), bf16[256,1,32,440]{0,3,1,2:T(8,128)(2,1)}, u32[]{:S(2)}, u32[]{:S(2)}) %all-to-all-start) | async-done | bytes 7208992 | tf_op jit(solution)/shard_map/all_to_all | solution.py:95
  1193.2 8.8 copy.203
  1202.0 394.2 %all-gather.13.cloned.1.call-done = bf16[8192,8704]{1,0:T(8,128)(2,1)} async-done(((bf16[256,8704]{1,0:T(8,128)(2,1)}), bf16[8192,8704]{1,0:T(8,128)(2,1)}) %all-gather.13.cloned.1.call-update) | async-done | bytes 142606352 | tf_op jit(solution)/shard_map/all_gather | solution.py:89
  1596.1 7.3 fusion.10
  1608.5 17.7 fusion
  1633.8 25.9 %fusion.4 = f32[8192,400]{0,1:T(8,128)} fusion(bf16[8192,8704]{1,0:T(8,128)(2,1)} %all-gather.13.cloned.1.call-done, bf16[2560,12800]{1,0:T(8,128)(2,1)} %all-gather.9.cloned.1.call-done, s32[]{:T(128)S(6)} %select_n.24), kind=kOutput, calls=%fused_computation.4 | convolution fusion | flops 16777216000 | bytes 57671684 | tf_op jit(solution)/shard_map/dot_general | solution.py:23
  1659.7 25.1 %multiply_convert_fusion.2 = (bf16[8192,200]{0,1:T(8,128)(2,1)}, bf16[8192,200]{0,1:T(8,128)(2,1)}) fusion(f32[8192,400]{0,1:T(8,128)} %fusion.4, bf16[200,2560]{1,0:T(8,128)(2,1)S(1)} %copy-done.32, bf16[8192,8704]{1,0:T(8,128)(2,1)} %all-gather.13.cloned.1.call-done), kind=kOutput, calls=%fused_computation.21 | convolution fusion | flops 8409907200 | bytes 62627840 | tf_op jit(solution)/shard_map/dot_general | solution.py:33
  1684.7 29.8 %fusion.20 = f32[2560,1,400]{0,2,1:T(8,128)} fusion(bf16[8192,8704]{1,0:T(8,128)(2,1)} %all-gather.13.cloned.1.call-done, bf16[8192,200]{0,1:T(8,128)(2,1)} %get-tuple-element.85, bf16[8192,200]{0,1:T(8,128)(2,1)} %get-tuple-element.84), kind=kOutput, calls=%fused_computation.37 | convolution fusion | flops 16790323200 | bytes 52592640 | tf_op jit(solution)/shard_map/dot_general | solution.py:27
  1714.5 11.4 copy.176
  1732.1 21.2 %fusion.31 = bf16[256,2560]{1,0:T(8,128)(2,1)} fusion(f32[256,2560]{1,0:T(8,128)S(1)} %copy-done.5, bf16[6400,2560]{1,0:T(8,128)(2,1)} %all-gather.11.cloned.1.call-done, f32[256,6400]{1,0:T(8,128)} %copy.143, f32[256,6400]{1,0:T(8,128)} %copy.142, f32[256]{0:T(256)S(1)} %copy-done.51), kind=kOutput, calls=%fused_computation.50 | convolution fusion | flops 8401059840 | bytes 49808384 | tf_op jit(solution)/shard_map/dot_general | solution.py:23
  1753.3 11.0 all-gather.17.cloned.1.call-done
  1767.9 10.6 slice.239
  1788.3 22.9 %fusion.6 = f32[200,2560]{1,0:T(8,128)} fusion(bf16[8192,8704]{1,0:T(8,128)(2,1)} %all-gather.13.cloned.1.call-done, f32[8192,400]{0,1:T(8,128)} %fusion.4), kind=kOutput, calls=%fused_computation.6 | convolution fusion | flops 8398438400 | bytes 57098240 | tf_op jit(solution)/shard_map/dot_general | solution.py:27
  1818.6 39.0 %all-to-all-done.2 = f32[2560,1,400]{2,1,0:T(1,128)} async-done(((f32[2560,1,400]{2,1,0:T(1,128)}), f32[2560,1,400]{2,1,0:T(1,128)}, u32[]{:S(2)}, u32[]{:S(2)}) %all-to-all-start.2) | async-done | bytes 4096032 | tf_op jit(solution)/shard_map/all_to_all | solution.py:101
  (284 shorter events, 264.0 us)
Async XLA Ops:
  7.2 181.3 %all-gather.15.cloned.1.call-start = ((), (), s32[]{:S(2)}) async-start(), calls=%async_computation.6 | async-start | bytes 27912192 | tf_op jit(solution)/shard_map/all_gather | solution.py:77
  22.6 515.7 %all-gather.9.cloned.1.call-start = ((), (), s32[]{:S(2)}) async-start(), calls=%async_computation.3 | async-start | bytes 67584000 | tf_op jit(solution)/shard_map/all_gather | solution.py:165
  46.3 8.3 copy-start.2
  53.6 676.1 %all-gather.11.cloned.1.call-start = ((), (), s32[]{:S(2)}) async-start(), calls=%async_computation.4 | async-start | bytes 33792000 | tf_op jit(solution)/shard_map/all_gather | solution.py:168
  54.3 1541.8 %all-gather.13.cloned.1.call-start = ((), (), s32[]{:S(2)}) async-start(), calls=%async_computation.5 | async-start | bytes 147062784 | tf_op jit(solution)/shard_map/all_gather | solution.py:89
  56.8 744.4 %copy-start.50 = (f32[256]{0:T(256)}, f32[256]{0:T(256)S(1)}, u32[]{:S(2)}) copy-start(f32[256]{0:T(256)S(1)} %fusion.72) | copy-start | bytes 3076
  57.5 256.3 %copy-start.33 = (f32[128,16]{0,1:T(8,128)}, f32[128,16]{0,1:T(8,128)S(1)}, u32[]{:S(2)}) copy-start(f32[128,16]{0,1:T(8,128)S(1)} %get-tuple-element.108) | copy-start | bytes 24580
  57.5 256.3 %copy-start.35 = (f32[128,16]{0,1:T(8,128)}, f32[128,16]{0,1:T(8,128)S(1)}, u32[]{:S(2)}) copy-start(f32[128,16]{0,1:T(8,128)S(1)} %get-tuple-element.109) | copy-start | bytes 24580
  223.9 17.6 copy-start
  249.2 13.5 slice-start
  262.6 5.6 copy-start.39
  262.7 5.5 copy-start.37
  266.4 7.5 slice-start.1
  271.7 9.3 copy-start.21
  283.6 34.4 %copy-start.11 = (bf16[2,128,40,128]{1,3,2,0:T(8,128)(2,1)}, bf16[2,128,40,128]{1,3,2,0:T(8,128)(2,1)S(1)}, u32[]{:S(2)}) copy-start(bf16[2,128,40,128]{1,3,2,0:T(8,128)(2,1)S(1)} %convolution_convert_fusion.1) | copy-start | bytes 7864324
  285.7 25.0 %copy-start.41 = (f32[768]{0:T(1024)}, f32[768]{0:T(1024)S(1)}, u32[]{:S(2)}) copy-start(f32[768]{0:T(1024)S(1)} %reshape.421) | copy-start | bytes 9220
  306.7 5.0 copy-start.6
  322.9 9.7 copy-start.16
  332.6 468.5 %copy-start.4 = (f32[256,2560]{1,0:T(8,128)}, f32[256,2560]{1,0:T(8,128)S(1)}, u32[]{:S(2)}) copy-start(f32[256,2560]{1,0:T(8,128)S(1)} %get-tuple-element.115) | copy-start | bytes 7864324
  337.3 1427.0 %all-gather.17.cloned.1.call-start = ((), (), s32[]{:S(2)}) async-start(), calls=%async_computation.7 | async-start | bytes 20680704 | tf_op jit(solution)/shard_map/all_gather | solution.py:335
  818.0 8.9 slice-start.2
  822.3 4.6 slice-start.3
  837.8 7.4 copy-start.7
  845.6 5.5 copy-start.24
  845.6 5.7 copy-start.9
  861.5 4.8 copy-start.40
  892.9 300.3 %all-to-all-start = ((bf16[256,1,32,440]{0,3,1,2:T(8,128)(2,1)}), bf16[256,1,32,440]{0,3,1,2:T(8,128)(2,1)}, u32[]{:S(2)}, u32[]{:S(2)}) async-start(bf16[256,1,32,440]{0,3,1,2:T(8,128)(2,1)} %maximum_bitcast_fusion), calls=%async_computation | async-start | bytes 14417920 | tf_op jit(solution)/shard_map/all_to_all | solution.py:95
  1630.0 96.0 %all-to-all-start.1 = ((f32[32,1,10560]{2,1,0:T(1,128)}), f32[32,1,10560]{2,1,0:T(1,128)}, u32[]{:S(2)}, u32[]{:S(2)}) async-start(f32[32,1,10560]{2,1,0:T(1,128)} %copy.172), calls=%async_computation.1 | async-start | bytes 2719744 | tf_op jit(solution)/shard_map/all_to_all | solution.py:101
  1633.8 25.9 %copy-start.32 = (bf16[200,2560]{1,0:T(8,128)(2,1)S(1)}, bf16[200,2560]{1,0:T(8,128)(2,1)}, u32[]{:S(2)}) copy-start(bf16[200,2560]{1,0:T(8,128)(2,1)} %param.28) | copy-start | bytes 3072004
  1726.0 6.1 copy-start.5
  1726.0 6.2 copy-start.51
  1726.0 131.6 %all-to-all-start.2 = ((f32[2560,1,400]{2,1,0:T(1,128)}), f32[2560,1,400]{2,1,0:T(1,128)}, u32[]{:S(2)}, u32[]{:S(2)}) async-start(f32[2560,1,400]{2,1,0:T(1,128)} %copy.176), calls=%async_computation.2 | async-start | bytes 10485760 | tf_op jit(solution)/shard_map/all_to_all | solution.py:101
  (33 other events, 79.5 us)
Sparse Core Ops, SparseCore 0:
  22.7 165.7 all-gather.14
  191.9 346.2 all-gather.8
  541.1 188.5 all-gather.10
  732.5 863.6 all-gather.12
  1599.3 164.9 all-gather.16

commit v10 on v8

--- a/solution.py
+++ b/solution.py
@@ -250,16 +250,17 @@
     )
     grad_up_c = (grad_hidden_c * gate_c * sigma_c).astype(jnp.bfloat16)
     down_grad = rows_product(hidden_c, grad_feed_all)
-    gate_up_cols = rows_product(h_two_all, jnp.concatenate([grad_gate_c, grad_up_c], axis=1))
+    gate_cols_grad = rows_product(h_two_all, grad_gate_c)
     inner_cols = column_shares(jnp.stack([h_one, grad_attn], axis=1), devices)
     h_one_cols = inner_cols[:, 0]
     out_cols = rows_product(attended_all, inner_cols[:, 1])
     wide_rows = rows_from_columns(
-        jnp.concatenate([gate_up_cols, out_cols], axis=1)[:, None, :], devices
-    ).reshape(width // devices, devices, 2 * ff_share + attn_share)
+        jnp.concatenate([gate_cols_grad, out_cols], axis=1)[:, None, :], devices
+    ).reshape(width // devices, devices, ff_share + attn_share)
     gate_grad = wide_rows[:, :, :ff_share].reshape(width // devices, ffn)
-    up_grad = wide_rows[:, :, ff_share : 2 * ff_share].reshape(width // devices, ffn)
-    output_weight_grad = wide_rows[:, :, 2 * ff_share :].reshape(width // devices, width)
+    output_weight_grad = wide_rows[:, :, ff_share:].reshape(width // devices, width)
+    up_cols_grad = rows_product(h_two_all, grad_up_c)
+    up_grad = rows_from_columns(up_cols_grad[:, None, :], devices).reshape(width // devices, ffn)
     grad_heads = (
         back_product(grad_attn, weight_out).astype(jnp.bfloat16).reshape(micro, slot, HEADS, VDIM)
     )

time: 1890 us -> 1930 us (1.021)
  waiting for transfers between devices: 1160 us -> 1180 us
    all_to_all x2 -> x3, waiting for transfers between devices: 42.1 us -> 76.3 us  [rows_from_columns(): moved = lax.all_to_all(grad, AXES, 0, 2, tiled=True)]
    all_to_all x2, waiting for transfers between devices: 274 us -> 248 us  [column_shares(): moved = lax.all_to_all(blocks, AXES, 2, 0, tiled=True)]
    dot_general x7 -> x8, matrix products: 84 us -> 103 us  [rows_product(): lax.dot_general(left, right, (((0,), (0,)), ((), ())), preferred_element_...]
  transfers between devices with their start and end apart: 9 -> 10, of which waited for: 7 -> 8; matrix products, arithmetic and copies ran while one was open for 33% -> 33% of each run, Pallas kernels for 0% -> 0%
where the time goes in v10:
time: 1930 us; the launch traced here: 1920 us
  waiting for transfers between devices  1180 us (61%)
  local copies, waits for them, and re-layouts  319 us (17%)
  matrix products  314 us (16%)
  other arithmetic  54.8 us (3%)
  starting transfers between devices  33.3 us (2%)
    all_gather x1, waiting for transfers between devices, gather_tokens(): return lax.all_gather(values, AXES, axis=0, tiled=True)  408 us
    all_to_all x2, waiting for transfers between devices, column_shares(): moved = lax.all_to_all(blocks, AXES, 2, 0, tiled=True)  248 us
    all_gather x1, waiting for transfers between devices, local(): lax.all_gather(interleave(gate_weight, up_weight, devices), AXES, axis=0,...  191 us
    all_gather x1, waiting for transfers between devices, gather_packed(): gathered = lax.all_gather(jnp.concatenate(flat), AXES, axis=0, tiled=False)  131 us
    all_gather x1, waiting for transfers between devices, local(): weight_down = lax.all_gather(down_weight, AXES, axis=0, tiled=True)  129 us
    dot_general x8, matrix products, rows_product(): lax.dot_general(left, right, (((0,), (0,)), ((), ())), preferred_element_...  103 us
    dot_general x8, matrix products, matmul(): return jnp.dot(left, right, preferred_element_type=jnp.float32)  101 us
    dot_general x8, matrix products, back_product(): lax.dot_general(left, right, (((1,), (1,)), ((), ())), preferred_element_...  97.6 us
  transfers between devices with their start and end apart: 10, of which 8 were waited for; matrix products, arithmetic and copies ran while one was open for 33% of the time, Pallas kernels for 0%

profile of v10, /device:TPU:0, one launch (start us, length us, event | category | flops | bytes accessed | tf_op | source)
XLA Modules:
  0.0 1920.2 jit_solution(5875582495010600543)
XLA Ops:
  29.6 8.3 stack_reshape.16
  37.9 8.3 pad_maximum_fusion.1
  57.3 131.2 %all-gather.15.cloned.1.call-done = bf16[13533184]{0:T(1024)(128)(2,1)} async-done(((bf16[422912]{0:T(1024)(128)(2,1)}), bf16[13533184]{0:T(1024)(128)(2,1)}) %all-gather.15.cloned.1.call-update) | async-done | bytes 27066384 | tf_op jit(solution)/shard_map/all_gather | solution.py:77
  188.5 35.4 %reshape.444 = bf16[32,422912]{1,0:T(8,128)(2,1)} reshape(bf16[13533184]{0:T(1024)(128)(2,1)} %all-gather.15.cloned.1.call-done) | data formatting | bytes 54132736 | tf_op jit(solution)/shard_map/all_gather | solution.py:77
  223.9 11.4 slice.220
  249.2 12.7 reshape.414
  295.6 8.6 copy.136
  321.5 9.5 multiply_reduce_fusion.5
  347.6 190.6 %all-gather.9.cloned.1.call-done = bf16[2560,12800]{1,0:T(8,128)(2,1)} async-done(((bf16[80,12800]{1,0:T(8,128)(2,1)}), bf16[2560,12800]{1,0:T(8,128)(2,1)}) %all-gather.9.cloned.1.call-update) | async-done | bytes 65536016 | tf_op jit(solution)/shard_map/all_gather | solution.py:165
  538.3 35.8 %fusion.79 = f32[256,12800]{0,1:T(8,128)} fusion(bf16[2560,12800]{1,0:T(8,128)(2,1)} %all-gather.9.cloned.1.call-done, f32[256,2560]{1,0:T(8,128)S(1)} %copy-done.7, f32[2560]{0:T(1024)S(1)} %reshape.440, f32[256]{0:T(256)S(1)} %add_rsqrt_fusion), kind=kOutput, calls=%fused_computation.177 | convolution fusion | flops 16779182080 | bytes 81275904 | tf_op jit(solution)/shard_map/dot_general | solution.py:23
  574.1 10.5 fusion.81
  584.6 8.1 copy.146
  592.7 8.2 copy.145
  600.9 128.8 %all-gather.11.cloned.1.call-done = bf16[6400,2560]{1,0:T(8,128)(2,1)} async-done(((bf16[200,2560]{1,0:T(8,128)(2,1)}), bf16[6400,2560]{1,0:T(8,128)(2,1)}) %all-gather.11.cloned.1.call-update) | async-done | bytes 32768016 | tf_op jit(solution)/shard_map/all_gather | solution.py:168
  729.7 24.4 %multiply_convert_fusion.4 = (bf16[256,6400]{1,0:T(8,128)(2,1)}, bf16[256,6400]{1,0:T(8,128)(2,1)}) fusion(f32[256,6400]{1,0:T(8,128)} %copy.145, f32[256,6400]{1,0:T(8,128)} %copy.146, bf16[256,2560]{1,0:T(8,128)(2,1)} %get-tuple-element.119, bf16[6400,2560]{1,0:T(8,128)(2,1)} %all-gather.11.cloned.1.call-done), kind=kOutput, calls=%fused_computation.22 | convolution fusion | flops 8409907200 | bytes 53739520 | tf_op jit(solution)/shard_map/dot_general | solution.py:33
  772.2 29.7 %multiply_reduce_fusion.1 = (f32[2560]{0:T(1024)}, f32[256]{0:T(256)S(1)}, f32[256,2560]{1,0:T(8,128)}) fusion(f32[256,2560]{1,0:T(8,128)S(1)} %copy-done.7, f32[256]{0:T(256)S(1)} %add_rsqrt_fusion, f32[2560]{0:T(1024)S(1)} %reshape.440, bf16[256,12800]{0,1:T(8,128)(2,1)} %bitcast.205, bf16[2560,12800]{1,0:T(8,128)(2,1)} %all-gather.9.cloned.1.call-done), kind=kOutput, calls=%fused_computation.71 | convolution fusion | flops 16781146112 | bytes 77355008 | tf_op jit(solution)/shard_map/dot_general | solution.py:33
  809.4 8.8 convolution_convert_fusion
  897.3 92.2 %all-to-all-done = bf16[256,2,32,80]{0,1,3,2:T(2,128)(2,1)} async-done(((bf16[256,2,32,80]{0,1,3,2:T(2,128)(2,1)}), bf16[256,2,32,80]{0,1,3,2:T(2,128)(2,1)}, u32[]{:S(2)}, u32[]{:S(2)}) %all-to-all-start) | async-done | bytes 2621472 | tf_op jit(solution)/shard_map/all_to_all | solution.py:95
  989.5 14.8 all-to-all-start.1
  1004.9 21.2 %fusion.28 = bf16[256,2560]{1,0:T(8,128)(2,1)} fusion(f32[256,2560]{1,0:T(8,128)S(1)} %copy-done.8, bf16[6400,2560]{1,0:T(8,128)(2,1)} %all-gather.11.cloned.1.call-done, f32[256,6400]{1,0:T(8,128)} %copy.146, f32[256,6400]{1,0:T(8,128)} %copy.145, f32[256]{0:T(256)S(1)} %copy-done.62), kind=kOutput, calls=%fused_computation.49 | convolution fusion | flops 8401059840 | bytes 49808384 | tf_op jit(solution)/shard_map/dot_general | solution.py:23
  1032.6 156.0 %all-to-all-done.1 = bf16[256,1,32,280]{0,3,1,2:T(8,128)(2,1)} async-done(((bf16[256,1,32,280]{0,3,1,2:T(8,128)(2,1)}), bf16[256,1,32,280]{0,3,1,2:T(8,128)(2,1)}, u32[]{:S(2)}, u32[]{:S(2)}) %all-to-all-start.1) | async-done | bytes 4587552 | tf_op jit(solution)/shard_map/all_to_all | solution.py:95
  1193.6 408.0 %all-gather.13.cloned.1.call-done = bf16[8192,8704]{1,0:T(8,128)(2,1)} async-done(((bf16[256,8704]{1,0:T(8,128)(2,1)}), bf16[8192,8704]{1,0:T(8,128)(2,1)}) %all-gather.13.cloned.1.call-update) | async-done | bytes 142606352 | tf_op jit(solution)/shard_map/all_gather | solution.py:89
  1618.1 21.2 %fusion.4 = f32[8192,200]{0,1:T(8,128)} fusion(bf16[200,2560]{1,0:T(8,128)(2,1)S(1)} %copy-done.39, bf16[8192,8704]{1,0:T(8,128)(2,1)} %all-gather.13.cloned.1.call-done), kind=kOutput, calls=%fused_computation.4 | convolution fusion | flops 8388608000 | bytes 49520640 | tf_op jit(solution)/shard_map/dot_general | solution.py:33
  1639.2 25.8 %fusion.10 = f32[8192,400]{0,1:T(8,128)} fusion(bf16[8192,8704]{1,0:T(8,128)(2,1)} %all-gather.13.cloned.1.call-done, bf16[2560,12800]{1,0:T(8,128)(2,1)} %all-gather.9.cloned.1.call-done, s32[]{:T(128)S(6)} %select_n.23), kind=kOutput, calls=%fused_computation.10 | convolution fusion | flops 16777216000 | bytes 57671684 | tf_op jit(solution)/shard_map/dot_general | solution.py:23
  1665.0 23.5 %fusion.25 = f32[2560,1,200]{0,2,1:T(8,128)S(1)} fusion(bf16[8192,8704]{1,0:T(8,128)(2,1)} %all-gather.13.cloned.1.call-done, f32[8192,200]{0,1:T(8,128)} %fusion.4, f32[8192,400]{0,1:T(8,128)} %fusion.10), kind=kOutput, calls=%fused_computation.48 | convolution fusion | flops 8398438400 | bytes 57098240 | tf_op jit(solution)/shard_map/dot_general | solution.py:27
  1698.7 23.5 %fusion.8 = f32[2560,200]{0,1:T(8,128)} fusion(bf16[8192,8704]{1,0:T(8,128)(2,1)} %all-gather.13.cloned.1.call-done, f32[8192,200]{0,1:T(8,128)} %fusion.4, f32[8192,400]{0,1:T(8,128)} %fusion.10), kind=kOutput, calls=%fused_computation.8 | convolution fusion | flops 8404992000 | bytes 63651840 | tf_op jit(solution)/shard_map/dot_general | solution.py:27
  1722.2 15.4 fusion
  1744.0 47.6 %all-to-all-done.4 = f32[2560,1,200]{2,1,0:T(1,128)} async-done(((f32[2560,1,200]{2,1,0:T(1,128)}), f32[2560,1,200]{2,1,0:T(1,128)}, u32[]{:S(2)}, u32[]{:S(2)}) %all-to-all-start.4) | async-done | bytes 2048032 | tf_op jit(solution)/shard_map/all_to_all | solution.py:101
  1804.9 10.8 slice.235
  1822.8 22.8 %fusion.2 = f32[200,2560]{1,0:T(8,128)} fusion(bf16[8192,8704]{1,0:T(8,128)(2,1)} %all-gather.13.cloned.1.call-done, f32[8192,400]{0,1:T(8,128)} %fusion.10), kind=kOutput, calls=%fused_computation.2 | convolution fusion | flops 8398438400 | bytes 57098240 | tf_op jit(solution)/shard_map/dot_general | solution.py:27
  1854.1 28.7 %all-to-all-done.3 = f32[2560,1,280]{2,1,0:T(1,128)} async-done(((f32[2560,1,280]{2,1,0:T(1,128)}), f32[2560,1,280]{2,1,0:T(1,128)}, u32[]{:S(2)}, u32[]{:S(2)}) %all-to-all-start.3) | async-done | bytes 2867232 | tf_op jit(solution)/shard_map/all_to_all | solution.py:101
  1882.8 7.5 copy.180
  (321 shorter events, 315.6 us)
Async XLA Ops:
  7.2 181.3 %all-gather.15.cloned.1.call-start = ((), (), s32[]{:S(2)}) async-start(), calls=%async_computation.8 | async-start | bytes 27912192 | tf_op jit(solution)/shard_map/all_gather | solution.py:77
  22.6 515.7 %all-gather.9.cloned.1.call-start = ((), (), s32[]{:S(2)}) async-start(), calls=%async_computation.5 | async-start | bytes 67584000 | tf_op jit(solution)/shard_map/all_gather | solution.py:165
  46.3 8.5 copy-start.2
  53.5 676.2 %all-gather.11.cloned.1.call-start = ((), (), s32[]{:S(2)}) async-start(), calls=%async_computation.6 | async-start | bytes 33792000 | tf_op jit(solution)/shard_map/all_gather | solution.py:168
  54.3 1547.3 %all-gather.13.cloned.1.call-start = ((), (), s32[]{:S(2)}) async-start(), calls=%async_computation.7 | async-start | bytes 147062784 | tf_op jit(solution)/shard_map/all_gather | solution.py:89
  57.1 744.9 %copy-start.61 = (f32[256]{0:T(256)}, f32[256]{0:T(256)S(1)}, u32[]{:S(2)}) copy-start(f32[256]{0:T(256)S(1)} %fusion.68) | copy-start | bytes 3076
  57.1 284.2 %copy-start.51 = (f32[256]{0:T(256)}, f32[256]{0:T(256)S(1)}, u32[]{:S(2)}) copy-start(f32[256]{0:T(256)S(1)} %get-tuple-element.102) | copy-start | bytes 3076
  57.2 254.2 %copy-start.42 = (f32[128,16]{0,1:T(8,128)}, f32[128,16]{0,1:T(8,128)S(1)}, u32[]{:S(2)}) copy-start(f32[128,16]{0,1:T(8,128)S(1)} %get-tuple-element.104) | copy-start | bytes 24580
  57.2 254.2 %copy-start.44 = (f32[128,16]{0,1:T(8,128)}, f32[128,16]{0,1:T(8,128)S(1)}, u32[]{:S(2)}) copy-start(f32[128,16]{0,1:T(8,128)S(1)} %get-tuple-element.105) | copy-start | bytes 24580
  223.9 17.6 copy-start
  249.2 13.5 slice-start
  281.1 34.4 %copy-start.13 = (bf16[2,128,40,128]{1,3,2,0:T(8,128)(2,1)}, bf16[2,128,40,128]{1,3,2,0:T(8,128)(2,1)S(1)}, u32[]{:S(2)}) copy-start(bf16[2,128,40,128]{1,3,2,0:T(8,128)(2,1)S(1)} %convolution_convert_fusion.1) | copy-start | bytes 7864324
  283.2 25.0 %copy-start.49 = (f32[768]{0:T(1024)}, f32[768]{0:T(1024)S(1)}, u32[]{:S(2)}) copy-start(f32[768]{0:T(1024)S(1)} %reshape.438) | copy-start | bytes 9220
  321.5 9.5 copy-start.16
  341.2 197.1 %copy-start.7 = (f32[256,2560]{1,0:T(8,128)S(1)}, f32[256,2560]{1,0:T(8,128)}, u32[]{:S(2)}) copy-start(f32[256,2560]{1,0:T(8,128)} %copy-done.6) | copy-start | bytes 7864324
  820.8 8.8 slice-start.2
  861.5 128.0 %all-to-all-start = ((bf16[256,2,32,80]{0,1,3,2:T(2,128)(2,1)}), bf16[256,2,32,80]{0,1,3,2:T(2,128)(2,1)}, u32[]{:S(2)}, u32[]{:S(2)}) async-start(bf16[256,2,32,80]{0,1,3,2:T(2,128)(2,1)} %pad_maximum_fusion.2), calls=%async_computation | async-start | bytes 5242880 | tf_op jit(solution)/shard_map/all_to_all | solution.py:95
  865.2 936.2 %all-gather.17.cloned.1.call-start = ((), (), s32[]{:S(2)}) async-start(), calls=%async_computation.9 | async-start | bytes 20680704 | tf_op jit(solution)/shard_map/all_gather | solution.py:335
  883.4 5.7 copy-start.14
  897.3 107.6 %copy-start.8 = (f32[256,2560]{1,0:T(8,128)S(1)}, f32[256,2560]{1,0:T(8,128)}, u32[]{:S(2)}) copy-start(f32[256,2560]{1,0:T(8,128)} %copy-done.6) | copy-start | bytes 7864324
  897.3 107.6 %copy-start.62 = (f32[256]{0:T(256)S(1)}, f32[256]{0:T(256)}, u32[]{:S(2)}) copy-start(f32[256]{0:T(256)} %copy-done.61) | copy-start | bytes 3076
  989.5 199.1 %all-to-all-start.1 = ((bf16[256,1,32,280]{0,3,1,2:T(8,128)(2,1)}), bf16[256,1,32,280]{0,3,1,2:T(8,128)(2,1)}, u32[]{:S(2)}, u32[]{:S(2)}) async-start(bf16[256,1,32,280]{0,3,1,2:T(8,128)(2,1)} %maximum_bitcast_fusion), calls=%async_computation.1 | async-start | bytes 9175040 | tf_op jit(solution)/shard_map/all_to_all | solution.py:95
  1615.1 77.5 %all-to-all-start.2 = ((f32[32,1,4160]{2,1,0:T(1,128)}), f32[32,1,4160]{2,1,0:T(1,128)S(1)}, u32[]{:S(2)}, u32[]{:S(2)}) async-start(f32[32,1,4160]{2,1,0:T(1,128)} %copy.176), calls=%async_computation.2 | async-start | bytes 1081344 | tf_op jit(solution)/shard_map/all_to_all | solution.py:101
  1692.5 99.0 %all-to-all-start.4 = ((f32[2560,1,200]{2,1,0:T(1,128)}), f32[2560,1,200]{2,1,0:T(1,128)}, u32[]{:S(2)}, u32[]{:S(2)}) async-start(f32[2560,1,200]{2,1,0:T(1,128)} %copy.183), calls=%async_computation.4 | async-start | bytes 5242880 | tf_op jit(solution)/shard_map/all_to_all | solution.py:101
  1698.7 23.5 %copy-start.31 = (bf16[8192,2,80]{0,2,1:T(8,128)(2,1)S(1)}, bf16[8192,2,80]{0,2,1:T(8,128)(2,1)}, u32[]{:S(2)}) copy-start(bf16[8192,2,80]{0,2,1:T(8,128)(2,1)} %reshape.424) | copy-start | bytes 7864324
  1722.2 15.4 copy-start.33
  1743.9 52.7 %copy-start.5 = (bf16[2,1,128,2560]{3,2,1,0:T(8,128)(2,1)S(1)}, bf16[2,1,128,2560]{3,2,1,0:T(8,128)(2,1)}, u32[]{:S(2)}) copy-start(bf16[2,1,128,2560]{3,2,1,0:T(8,128)(2,1)} %param.15) | copy-start | bytes 3932164
  1743.9 52.7 %copy-start.48 = (f32[2560]{0:T(1024)S(1)}, f32[2560]{0:T(1024)}, u32[]{:S(2)}) copy-start(f32[2560]{0:T(1024)} %copy-done.46) | copy-start | bytes 30724
  1743.9 52.7 %copy-start.53 = (f32[256]{0:T(256)S(1)}, f32[256]{0:T(256)}, u32[]{:S(2)}) copy-start(f32[256]{0:T(256)} %copy-done.51) | copy-start | bytes 3076
  1744.0 52.7 %copy-start.63 = (f32[256]{0:T(256)S(1)}, f32[256]{0:T(256)}, u32[]{:S(2)}) copy-start(f32[256]{0:T(256)} %broadcast_multiply_fusion) | copy-start | bytes 3076
  1791.6 91.3 %all-to-all-start.3 = ((f32[2560,1,280]{2,1,0:T(1,128)}), f32[2560,1,280]{2,1,0:T(1,128)}, u32[]{:S(2)}, u32[]{:S(2)}) async-start(f32[2560,1,280]{2,1,0:T(1,128)} %copy.179), calls=%async_computation.3 | async-start | bytes 7864320 | tf_op jit(solution)/shard_map/all_to_all | solution.py:101
  1804.9 11.4 copy-start.32
  (49 other events, 139.3 us)
Sparse Core Ops, SparseCore 0:
  22.7 165.7 all-gather.14
  191.9 346.2 all-gather.8
  541.1 188.5 all-gather.10
  732.5 869.1 all-gather.12
  1604.9 180.3 all-gather.16

commit v11 on v8

--- a/solution.py
+++ b/solution.py
@@ -254,12 +254,7 @@
     inner_cols = column_shares(jnp.stack([h_one, grad_attn], axis=1), devices)
     h_one_cols = inner_cols[:, 0]
     out_cols = rows_product(attended_all, inner_cols[:, 1])
-    wide_rows = rows_from_columns(
-        jnp.concatenate([gate_up_cols, out_cols], axis=1)[:, None, :], devices
-    ).reshape(width // devices, devices, 2 * ff_share + attn_share)
-    gate_grad = wide_rows[:, :, :ff_share].reshape(width // devices, ffn)
-    up_grad = wide_rows[:, :, ff_share : 2 * ff_share].reshape(width // devices, ffn)
-    output_weight_grad = wide_rows[:, :, 2 * ff_share :].reshape(width // devices, width)
+    wide_cols = jnp.concatenate([gate_up_cols, out_cols], axis=1).reshape(devices, -1)
     grad_heads = (
         back_product(grad_attn, weight_out).astype(jnp.bfloat16).reshape(micro, slot, HEADS, VDIM)
     )
@@ -344,16 +339,27 @@
     latent_width = grad_latent_all.shape[1]
     latent_down_grad = rows_product(h_one_cols, down_grads_all[:, :latent_width])
     query_down_grad = rows_product(h_one_cols, down_grads_all[:, latent_width:])
-    up_rows = rows_from_columns(
+    wide_size = wide_cols.shape[1]
+    all_rows = rows_from_columns(
         jnp.concatenate(
             [
+                wide_cols,
                 query_up_cols.reshape(devices, -1),
                 latent_up_cols.reshape(devices, -1),
             ],
             axis=1,
         ).reshape(devices, 1, -1),
         devices,
-    )
+    ).reshape(devices, -1)
+    wide_rows = (
+        all_rows[:, :wide_size]
+        .reshape(devices, width // devices, 2 * ff_share + attn_share)
+        .transpose(1, 0, 2)
+    )
+    gate_grad = wide_rows[:, :, :ff_share].reshape(width // devices, ffn)
+    up_grad = wide_rows[:, :, ff_share : 2 * ff_share].reshape(width // devices, ffn)
+    output_weight_grad = wide_rows[:, :, 2 * ff_share :].reshape(width // devices, width)
+    up_rows = all_rows[:, wide_size:]
     q_rows = up_query.shape[0] // devices
     kv_rows = up_latent.shape[0] // devices
     kv_cols = kv_width // devices

time: 1890 us -> 1930 us (1.021)
  local copies, waits for them, and re-layouts: 310 us -> 343 us
    reshape x1 -> x3, local copies, waits for them, and re-layouts: 1.36 us -> 21.8 us  [the longest x1 7.76 us: local(): all_rows = rows_from_columns(jnp.concatenate([wide_cols, query_up_cols.re...]
    unnamed x134 -> x143, local copies, waits for them, and re-layouts: 34.3 us -> 41.9 us
    all_to_all x2 -> x1, waiting for transfers between devices: 42.1 us -> 48.1 us  [rows_from_columns(): moved = lax.all_to_all(grad, AXES, 0, 2, tiled=True)]
  transfers between devices with their start and end apart: 9 -> 8, of which waited for: 7 -> 7; matrix products, arithmetic and copies ran while one was open for 33% -> 33% of each run, Pallas kernels for 0% -> 0%
where the time goes in v11:
time: 1930 us; the launch traced here: 1920 us
  waiting for transfers between devices  1170 us (61%)
  local copies, waits for them, and re-layouts  343 us (18%)
  matrix products  306 us (16%)
  other arithmetic  59.4 us (3%)
  starting transfers between devices  22.6 us (1%)
    all_gather x1, waiting for transfers between devices, gather_tokens(): return lax.all_gather(values, AXES, axis=0, tiled=True)  416 us
    all_to_all x2, waiting for transfers between devices, column_shares(): moved = lax.all_to_all(blocks, AXES, 2, 0, tiled=True)  259 us
    all_gather x1, waiting for transfers between devices, local(): lax.all_gather(interleave(gate_weight, up_weight, devices), AXES, axis=0,...  189 us
    all_gather x1, waiting for transfers between devices, gather_packed(): gathered = lax.all_gather(jnp.concatenate(flat), AXES, axis=0, tiled=False)  132 us
    all_gather x1, waiting for transfers between devices, local(): weight_down = lax.all_gather(down_weight, AXES, axis=0, tiled=True)  129 us
    dot_general x8, matrix products, matmul(): return jnp.dot(left, right, preferred_element_type=jnp.float32)  104 us
    dot_general x8, matrix products, back_product(): lax.dot_general(left, right, (((1,), (1,)), ((), ())), preferred_element_...  100 us
    dot_general x7, matrix products, rows_product(): lax.dot_general(left, right, (((0,), (0,)), ((), ())), preferred_element_...  86.9 us
  transfers between devices with their start and end apart: 8, of which 7 were waited for; matrix products, arithmetic and copies ran while one was open for 33% of the time, Pallas kernels for 0%

profile of v11, /device:TPU:0, one launch (start us, length us, event | category | flops | bytes accessed | tf_op | source)
XLA Modules:
  0.0 1919.6 jit_solution(4060316756490745201)
XLA Ops:
  29.6 8.3 stack_reshape.16
  37.9 8.3 pad_maximum_fusion.2
  46.3 7.3 reshape.422
  57.0 131.5 %all-gather.15.cloned.1.call-done = bf16[13533184]{0:T(1024)(128)(2,1)} async-done(((bf16[422912]{0:T(1024)(128)(2,1)}), bf16[13533184]{0:T(1024)(128)(2,1)}) %all-gather.15.cloned.1.call-update) | async-done | bytes 27066384 | tf_op jit(solution)/shard_map/all_gather | solution.py:77
  188.5 35.3 %reshape.454 = bf16[32,422912]{1,0:T(8,128)(2,1)} reshape(bf16[13533184]{0:T(1024)(128)(2,1)} %all-gather.15.cloned.1.call-done) | data formatting | bytes 54132736 | tf_op jit(solution)/shard_map/all_gather | solution.py:77
  223.9 11.4 slice.231
  249.1 12.7 reshape.421
  298.1 8.6 copy.133
  323.9 9.5 multiply_reduce_fusion.5
  348.9 189.4 %all-gather.9.cloned.1.call-done = bf16[2560,12800]{1,0:T(8,128)(2,1)} async-done(((bf16[80,12800]{1,0:T(8,128)(2,1)}), bf16[2560,12800]{1,0:T(8,128)(2,1)}) %all-gather.9.cloned.1.call-update) | async-done | bytes 65536016 | tf_op jit(solution)/shard_map/all_gather | solution.py:165
  538.3 35.9 %fusion.74 = f32[256,12800]{0,1:T(8,128)} fusion(bf16[2560,12800]{1,0:T(8,128)(2,1)} %all-gather.9.cloned.1.call-done, f32[256,2560]{1,0:T(8,128)S(1)} %copy-done.7, f32[2560]{0:T(1024)S(1)} %reshape.450, f32[256]{0:T(256)S(1)} %add_rsqrt_fusion), kind=kOutput, calls=%fused_computation.174 | convolution fusion | flops 16779182080 | bytes 81275904 | tf_op jit(solution)/shard_map/dot_general | solution.py:23
  574.2 10.4 fusion.76
  584.7 8.1 copy.143
  592.8 8.2 copy.142
  601.0 128.7 %all-gather.11.cloned.1.call-done = bf16[6400,2560]{1,0:T(8,128)(2,1)} async-done(((bf16[200,2560]{1,0:T(8,128)(2,1)}), bf16[6400,2560]{1,0:T(8,128)(2,1)}) %all-gather.11.cloned.1.call-update) | async-done | bytes 32768016 | tf_op jit(solution)/shard_map/all_gather | solution.py:168
  729.7 24.4 %multiply_convert_fusion.4 = (bf16[256,6400]{1,0:T(8,128)(2,1)}, bf16[256,6400]{1,0:T(8,128)(2,1)}) fusion(f32[256,6400]{1,0:T(8,128)} %copy.142, f32[256,6400]{1,0:T(8,128)} %copy.143, bf16[256,2560]{1,0:T(8,128)(2,1)} %get-tuple-element.123, bf16[6400,2560]{1,0:T(8,128)(2,1)} %all-gather.11.cloned.1.call-done), kind=kOutput, calls=%fused_computation.23 | convolution fusion | flops 8409907200 | bytes 53739520 | tf_op jit(solution)/shard_map/dot_general | solution.py:33
  772.2 28.8 %multiply_reduce_fusion.1 = (f32[2560]{0:T(1024)S(1)}, f32[256]{0:T(256)S(1)}, f32[256,2560]{1,0:T(8,128)}) fusion(f32[256,2560]{1,0:T(8,128)S(1)} %copy-done.7, f32[256]{0:T(256)S(1)} %add_rsqrt_fusion, f32[2560]{0:T(1024)S(1)} %reshape.450, bf16[256,12800]{0,1:T(8,128)(2,1)} %bitcast.192, bf16[2560,12800]{1,0:T(8,128)(2,1)} %all-gather.9.cloned.1.call-done), kind=kOutput, calls=%fused_computation.70 | convolution fusion | flops 16781146112 | bytes 77355008 | tf_op jit(solution)/shard_map/dot_general | solution.py:33
  808.5 8.8 convolution_convert_fusion
  900.7 73.5 %all-to-all-done = bf16[256,2,32,80]{0,1,3,2:T(2,128)(2,1)} async-done(((bf16[256,2,32,80]{0,1,3,2:T(2,128)(2,1)}), bf16[256,2,32,80]{0,1,3,2:T(2,128)(2,1)}, u32[]{:S(2)}, u32[]{:S(2)}) %all-to-all-start) | async-done | bytes 2621472 | tf_op jit(solution)/shard_map/all_to_all | solution.py:95
  974.2 14.5 all-to-all-start.1
  995.2 185.4 %all-to-all-done.1 = bf16[256,1,32,280]{0,3,1,2:T(8,128)(2,1)} async-done(((bf16[256,1,32,280]{0,3,1,2:T(8,128)(2,1)}), bf16[256,1,32,280]{0,3,1,2:T(8,128)(2,1)}, u32[]{:S(2)}, u32[]{:S(2)}) %all-to-all-start.1) | async-done | bytes 4587552 | tf_op jit(solution)/shard_map/all_to_all | solution.py:95
  1185.7 415.9 %all-gather.13.cloned.1.call-done = bf16[8192,8704]{1,0:T(8,128)(2,1)} async-done(((bf16[256,8704]{1,0:T(8,128)(2,1)}), bf16[8192,8704]{1,0:T(8,128)(2,1)}) %all-gather.13.cloned.1.call-update) | async-done | bytes 142606352 | tf_op jit(solution)/shard_map/all_gather | solution.py:89
  1601.6 16.0 fusion
  1617.6 26.3 %fusion.4 = f32[8192,400]{0,1:T(8,128)} fusion(bf16[8192,8704]{1,0:T(8,128)(2,1)} %all-gather.13.cloned.1.call-done, bf16[2560,12800]{1,0:T(8,128)(2,1)} %all-gather.9.cloned.1.call-done, s32[]{:T(128)S(6)} %select_n.22), kind=kOutput, calls=%fused_computation.4 | convolution fusion | flops 16777216000 | bytes 57671684 | tf_op jit(solution)/shard_map/dot_general | solution.py:23
  1643.9 24.8 %multiply_convert_fusion.2 = (bf16[8192,200]{0,1:T(8,128)(2,1)}, bf16[8192,200]{0,1:T(8,128)(2,1)}) fusion(f32[8192,400]{0,1:T(8,128)} %fusion.4, bf16[200,2560]{1,0:T(8,128)(2,1)S(1)} %copy-done.38, bf16[8192,8704]{1,0:T(8,128)(2,1)} %all-gather.13.cloned.1.call-done), kind=kOutput, calls=%fused_computation.20 | convolution fusion | flops 8409907200 | bytes 62627840 | tf_op jit(solution)/shard_map/dot_general | solution.py:33
  1668.7 29.8 %fusion.2 = f32[2560,400]{0,1:T(8,128)S(1)} fusion(bf16[8192,8704]{1,0:T(8,128)(2,1)} %all-gather.13.cloned.1.call-done, bf16[8192,200]{0,1:T(8,128)(2,1)} %get-tuple-element.85, bf16[8192,200]{0,1:T(8,128)(2,1)} %get-tuple-element.84), kind=kOutput, calls=%fused_computation.2 | convolution fusion | flops 16790323200 | bytes 52592640 | tf_op jit(solution)/shard_map/dot_general | solution.py:27
  1735.7 7.8 copy.174
  1752.5 21.5 %fusion.26 = bf16[256,2560]{1,0:T(8,128)(2,1)} fusion(f32[256,2560]{1,0:T(8,128)} %copy-done.6, bf16[6400,2560]{1,0:T(8,128)(2,1)} %all-gather.11.cloned.1.call-done, f32[256,6400]{1,0:T(8,128)} %copy.143, f32[256,6400]{1,0:T(8,128)} %copy.142, f32[256]{0:T(256)S(1)} %copy-done.58), kind=kOutput, calls=%fused_computation.51 | convolution fusion | flops 8401059840 | bytes 49808384 | tf_op jit(solution)/shard_map/dot_general | solution.py:23
  1777.6 10.9 slice.246
  1795.6 22.8 %fusion.6 = f32[200,2560]{1,0:T(8,128)} fusion(bf16[8192,8704]{1,0:T(8,128)(2,1)} %all-gather.13.cloned.1.call-done, f32[8192,400]{0,1:T(8,128)} %fusion.4), kind=kOutput, calls=%fused_computation.6 | convolution fusion | flops 8398438400 | bytes 57098240 | tf_op jit(solution)/shard_map/dot_general | solution.py:27
  1818.4 48.1 %all-to-all-done.2 = f32[32,1,42560]{2,1,0:T(1,128)} async-done(((f32[32,1,42560]{2,1,0:T(1,128)}), f32[32,1,42560]{2,1,0:T(1,128)}, u32[]{:S(2)}, u32[]{:S(2)}) %all-to-all-start.2) | async-done | bytes 5447712 | tf_op jit(solution)/shard_map/all_to_all | solution.py:101
  1872.9 7.2 reshape.441
  (306 shorter events, 324.1 us)
Async XLA Ops:
  7.2 181.3 %all-gather.15.cloned.1.call-start = ((), (), s32[]{:S(2)}) async-start(), calls=%async_computation.6 | async-start | bytes 27912192 | tf_op jit(solution)/shard_map/all_gather | solution.py:77
  22.6 515.7 %all-gather.9.cloned.1.call-start = ((), (), s32[]{:S(2)}) async-start(), calls=%async_computation.3 | async-start | bytes 67584000 | tf_op jit(solution)/shard_map/all_gather | solution.py:165
  46.3 8.3 copy-start.2
  53.6 676.2 %all-gather.11.cloned.1.call-start = ((), (), s32[]{:S(2)}) async-start(), calls=%async_computation.4 | async-start | bytes 33792000 | tf_op jit(solution)/shard_map/all_gather | solution.py:168
  54.3 1547.3 %all-gather.13.cloned.1.call-start = ((), (), s32[]{:S(2)}) async-start(), calls=%async_computation.5 | async-start | bytes 147062784 | tf_op jit(solution)/shard_map/all_gather | solution.py:89
  56.8 744.3 %copy-start.57 = (f32[256]{0:T(256)}, f32[256]{0:T(256)S(1)}, u32[]{:S(2)}) copy-start(f32[256]{0:T(256)S(1)} %fusion.64) | copy-start | bytes 3076
  56.8 285.8 %copy-start.48 = (f32[256]{0:T(256)}, f32[256]{0:T(256)S(1)}, u32[]{:S(2)}) copy-start(f32[256]{0:T(256)S(1)} %get-tuple-element.106) | copy-start | bytes 3076
  56.9 256.9 %copy-start.39 = (f32[128,16]{0,1:T(8,128)}, f32[128,16]{0,1:T(8,128)S(1)}, u32[]{:S(2)}) copy-start(f32[128,16]{0,1:T(8,128)S(1)} %get-tuple-element.108) | copy-start | bytes 24580
  56.9 256.9 %copy-start.41 = (f32[128,16]{0,1:T(8,128)}, f32[128,16]{0,1:T(8,128)S(1)}, u32[]{:S(2)}) copy-start(f32[128,16]{0,1:T(8,128)S(1)} %get-tuple-element.109) | copy-start | bytes 24580
  223.8 17.6 copy-start
  249.1 13.5 slice-start
  262.6 5.5 copy-start.43
  266.3 7.6 slice-start.1
  271.5 9.3 copy-start.25
  283.5 34.5 %copy-start.12 = (bf16[2,128,40,128]{1,3,2,0:T(8,128)(2,1)}, bf16[2,128,40,128]{1,3,2,0:T(8,128)(2,1)S(1)}, u32[]{:S(2)}) copy-start(bf16[2,128,40,128]{1,3,2,0:T(8,128)(2,1)S(1)} %convolution_convert_fusion.1) | copy-start | bytes 7864324
  285.6 25.1 %copy-start.46 = (f32[768]{0:T(1024)}, f32[768]{0:T(1024)S(1)}, u32[]{:S(2)}) copy-start(f32[768]{0:T(1024)S(1)} %reshape.448) | copy-start | bytes 9220
  306.7 5.0 copy-start.8
  323.9 9.5 copy-start.15
  342.5 195.8 %copy-start.7 = (f32[256,2560]{1,0:T(8,128)S(1)}, f32[256,2560]{1,0:T(8,128)}, u32[]{:S(2)}) copy-start(f32[256,2560]{1,0:T(8,128)} %copy-done.6) | copy-start | bytes 7864324
  819.9 8.9 slice-start.2
  835.3 5.2 copy-start.20
  850.3 124.0 %all-to-all-start = ((bf16[256,2,32,80]{0,1,3,2:T(2,128)(2,1)}), bf16[256,2,32,80]{0,1,3,2:T(2,128)(2,1)}, u32[]{:S(2)}, u32[]{:S(2)}) async-start(bf16[256,2,32,80]{0,1,3,2:T(2,128)(2,1)} %pad_maximum_fusion.3), calls=%async_computation | async-start | bytes 5242880 | tf_op jit(solution)/shard_map/all_to_all | solution.py:95
  853.8 920.1 %all-gather.17.cloned.1.call-start = ((), (), s32[]{:S(2)}) async-start(), calls=%async_computation.7 | async-start | bytes 20680704 | tf_op jit(solution)/shard_map/all_gather | solution.py:329
  855.5 4.8 copy-start.18
  868.1 5.5 copy-start.28
  868.2 5.7 copy-start.10
  886.8 5.7 copy-start.13
  974.2 206.4 %all-to-all-start.1 = ((bf16[256,1,32,280]{0,3,1,2:T(8,128)(2,1)}), bf16[256,1,32,280]{0,3,1,2:T(8,128)(2,1)}, u32[]{:S(2)}, u32[]{:S(2)}) async-start(bf16[256,1,32,280]{0,3,1,2:T(8,128)(2,1)} %maximum_bitcast_fusion), calls=%async_computation.1 | async-start | bytes 9175040 | tf_op jit(solution)/shard_map/all_to_all | solution.py:95
  1180.6 421.0 %copy-start.31 = (bf16[8192,2,80]{0,2,1:T(8,128)(2,1)S(1)}, bf16[8192,2,80]{0,2,1:T(8,128)(2,1)}, u32[]{:S(2)}) copy-start(bf16[8192,2,80]{0,2,1:T(8,128)(2,1)} %reshape.431) | copy-start | bytes 7864324
  1617.6 26.3 %copy-start.38 = (bf16[200,2560]{1,0:T(8,128)(2,1)S(1)}, bf16[200,2560]{1,0:T(8,128)(2,1)}, u32[]{:S(2)}) copy-start(bf16[200,2560]{1,0:T(8,128)(2,1)} %param.28) | copy-start | bytes 3072004
  1743.5 123.0 %all-to-all-start.2 = ((f32[32,1,42560]{2,1,0:T(1,128)}), f32[32,1,42560]{2,1,0:T(1,128)}, u32[]{:S(2)}, u32[]{:S(2)}) async-start(f32[32,1,42560]{2,1,0:T(1,128)} %copy.174), calls=%async_computation.2 | async-start | bytes 10911744 | tf_op jit(solution)/shard_map/all_to_all | solution.py:101
  1777.6 11.5 copy-start.32
  (41 other events, 107.9 us)
Sparse Core Ops, SparseCore 0:
  22.7 165.7 all-gather.14
  191.9 346.2 all-gather.8
  541.1 188.5 all-gather.10
  732.5 869.0 all-gather.12
  1604.8 127.6 all-gather.16
